TPU v7x, 256 devices: a whole 4x4x8 slice. The times are simulated.
256 devices in a mesh: req: 32 (over z_hi, y, core), tp: 8 (over x, z_lo).
Axes of the slice: x: 4, y: 4, z: 8 (z_hi: 4, z_lo: 2; z = z_hi * 2 + z_lo), core: 2. Of those that a mesh axis runs over, the one named last changes fastest.
Arguments:
- hidden_in: bfloat16 [4096, 5120], P('req', 'tp'), may hold values from -6 to 6
- norm_gain: bfloat16 [5120], P('tp'), may hold values from 0.099609375 to 1.8984375
- q_weight: bfloat16 [5120, 3072], P(None, 'tp'), may hold values from -0.078125 to 0.078125
- q_bias: bfloat16 [3072], P('tp'), may hold values from -4 to 4
- k_weight: bfloat16 [5120, 1024], P(None, 'tp'), may hold values from -0.125 to 0.125
- k_bias: bfloat16 [1024], P('tp'), may hold values from -5 to 5
- v_weight: bfloat16 [5120, 1024], P(None, 'tp'), may hold values from -0.3125 to 0.3125
- v_bias: bfloat16 [1024], P('tp'), may hold values from -10 to 10
- o_weight: bfloat16 [3072, 5120], P('tp'), may hold values from -0.3125 to 0.3125
- prefix_kv: bfloat16 [32768, 2, 1024], P('req', None, 'tp'), as said below
- suffix_len: int32 [32], P('req'), may hold values from 18 to 128, as said below
- req_prefix: int32 [32], P('req'), may hold values from 0 to 3, as said below
- block_owner: int32 [32], replicated, may hold values from 0 to 31, each once
Outputs:
- attn_out: bfloat16 [4096, 5120], P('req', 'tp')
Inputs may be any that keep to these rules, and one draw needn't show every extreme that they name: `suffix_len`: suffix tokens of each request; some request has exactly 128 and some exactly 18. `req_prefix`: every prefix is continued by exactly 8 requests. Block j of prefix p is held by req index block_owner[p * 8 + j]; each req index holds one block. `prefix_kv`: cached keys already carry the rotary embedding of their prefix positions.
All inputs are finite; a program needn't handle non-finite values.
Results may differ from a plain program's by a relative error of at most 0.022.
Values may be sent and summed in bfloat16 or wider, within the bound.
No kernel may reach another device: no remote copies, remote signals or barrier semaphores. Data moves between devices by JAX's collectives and lax.ppermute only.
A program may use at most 128 MiB of HBM per device.

v0:
```python
import jax
import jax.numpy as jnp
from jax import lax
from jax.sharding import PartitionSpec as P

HD = 128
NPREF = 4


THETA = 1000000.0
EPSILON = 1e-06


def rotate(heads, positions):
    half = HD // 2
    freqs = THETA ** (-(jnp.arange(half, dtype=jnp.float32) * 2.0) / HD)
    angles = positions.astype(jnp.float32)[:, None] * freqs[None, :]
    cosine = jnp.cos(angles)[:, None, :]
    sine = jnp.sin(angles)[:, None, :]
    first = heads[..., :half]
    second = heads[..., half:]
    return jnp.concatenate(
        [first * cosine - second * sine, second * cosine + first * sine], axis=-1
    )


def block_stats(grouped, keys, values, allowed):
    scores = jnp.einsum(
        "sghd,kgd->sghk", grouped, keys, preferred_element_type=jnp.float32
    ) * HD ** (-0.5)
    if allowed is not None:
        scores = jnp.where(allowed[:, None, None, :], scores, -jnp.inf)
    peak = jnp.max(scores, axis=-1)
    weights = jnp.exp(scores - peak[..., None])
    total = jnp.sum(weights, axis=-1)
    mixed = jnp.einsum(
        "sghk,kgd->sghd", weights.astype(jnp.bfloat16), values, preferred_element_type=jnp.float32
    )
    return (peak, total, mixed)


def combine(first, second):
    peak = jnp.maximum(first[0], second[0])
    left = jnp.exp(first[0] - peak)
    right = jnp.exp(second[0] - peak)
    total = first[1] * left + second[1] * right
    mixed = first[2] * left[..., None] + second[2] * right[..., None]
    return (peak, total, mixed)


def shards(
    hidden_in,
    norm_gain,
    q_weight,
    q_bias,
    k_weight,
    k_bias,
    v_weight,
    v_bias,
    o_weight,
    prefix_kv,
    suffix_len,
    req_prefix,
    block_owner,
):
    length = hidden_in.shape[0]
    devices = lax.axis_size("req")
    owned = devices // NPREF
    block = prefix_kv.shape[0]
    prefix_len = block * owned
    kv_heads = k_weight.shape[1] // HD
    q_heads = q_weight.shape[1] // HD
    group = q_heads // kv_heads
    full, gain = (
        lax.all_gather(hidden_in, "tp", axis=1, tiled=True),
        lax.all_gather(norm_gain, "tp", axis=0, tiled=True),
    )
    tokens = full.astype(jnp.float32)
    meansq = jnp.mean(tokens * tokens, axis=-1, keepdims=True)
    normed = (tokens * lax.rsqrt(meansq + EPSILON) * gain.astype(jnp.float32)).astype(jnp.bfloat16)
    positions = prefix_len + jnp.arange(length, dtype=jnp.int32)
    queries = jnp.dot(normed, q_weight, preferred_element_type=jnp.float32) + q_bias.astype(
        jnp.float32
    )
    queries = rotate(queries.reshape(length, q_heads, HD), positions).astype(jnp.bfloat16)
    queries = queries.reshape(length, kv_heads, group, HD)
    keys = jnp.dot(normed, k_weight, preferred_element_type=jnp.float32) + k_bias.astype(
        jnp.float32
    )
    keys = rotate(keys.reshape(length, kv_heads, HD), positions).astype(jnp.bfloat16)
    values = jnp.dot(normed, v_weight, preferred_element_type=jnp.float32) + v_bias.astype(
        jnp.float32
    )
    values = values.astype(jnp.bfloat16).reshape(length, kv_heads, HD)
    slot_index = jnp.arange(length, dtype=jnp.int32)
    causal = slot_index[None, :] <= slot_index[:, None]
    state = block_stats(queries, keys, values, causal)
    which = req_prefix[0]

    def advance(current, cached):
        return (combine(current, block_stats(queries, cached[:, 0], cached[:, 1], None)), None)

    everything = lax.all_gather(prefix_kv, "req", axis=0, tiled=True)
    stacked = everything.reshape(devices, block, 2, kv_heads, HD)
    owners = lax.dynamic_slice_in_dim(block_owner, which * owned, owned)
    chosen = jnp.take(stacked, owners, axis=0)
    state, unused = lax.scan(advance, state, chosen)
    peak, total, mixed = state
    context = (mixed / total[..., None]).astype(jnp.bfloat16).reshape(length, q_heads * HD)
    partial_value = jnp.dot(context, o_weight, preferred_element_type=jnp.float32)
    summed = lax.psum_scatter(
        partial_value.astype(jnp.bfloat16), "tp", scatter_dimension=1, tiled=True
    ).astype(jnp.float32)
    valid = slot_index < suffix_len[0]
    return jnp.where(valid[:, None], summed, jnp.float32(0.0)).astype(jnp.bfloat16)


def solution(mesh):
    placed = (
        P("req", "tp"),
        P("tp"),
        P(None, "tp"),
        P("tp"),
        P(None, "tp"),
        P("tp"),
        P(None, "tp"),
        P("tp"),
        P("tp", None),
        P("req", None, "tp"),
        P("req"),
        P("req"),
        P(),
    )
    return jax.shard_map(
        shards, mesh=mesh, in_specs=placed, out_specs=P("req", "tp"), check_vma=False
    )
```

profile of v0, /device:TPU:1, one launch (start us, length us, event | category | flops | bytes accessed | tf_op | source)
XLA Modules:
  0.0 273.3 jit_solution(18251878204632939527)
XLA Ops:
  6.6 0.7 all-gather.4.cloned.1.call-update
  7.3 1.9 copy.47
  9.3 23.4 %all-gather = bf16[8,1,640]{2,1,0:T(2,128)(2,1)S(1)} all-gather(bf16[1,1,640]{2,1,0:T(2,128)(2,1)S(1)} %reshape.278), channel_id=1, replica_groups=mesh['req'=32,'tp'=8] {'tp'}, dimensions={0}, use_global_device_ids=true | all-gather | bytes 11520 | tf_op jit(solution)/shard_map/all_gather | solution.py:76
  33.6 0.3 multiply_cosine_fusion
  33.9 20.4 %all-gather.4.cloned.1.call-done = bf16[128,5120]{1,0:T(8,128)(2,1)} async-done(((bf16[128,640]{1,0:T(8,128)(2,1)}), bf16[128,5120]{1,0:T(8,128)(2,1)}) %all-gather.4.cloned.1.call-update) | async-done | bytes 1310736 | tf_op jit(solution)/shard_map/all_gather | solution.py:75
  54.4 1.6 fusion.15
  56.0 3.4 %convolution_add_fusion = f32[128,384]{1,0:T(8,128)S(1)} fusion(bf16[5120,384]{1,0:T(8,128)(2,1)} %param.17, f32[384]{0:T(512)S(1)} %convert_element_type.79, bf16[128,5120]{1,0:T(8,128)(2,1)} %all-gather.4.cloned.1.call-done, f32[5120]{0:T(1024)S(1)} %bitcast.155, f32[128]{0:T(128)S(1)} %add_rsqrt_fusion), kind=kOutput, calls=%fused_computation.36 | convolution fusion | flops 505987072 | bytes 5462016 | tf_op jit(solution)/shard_map/dot_general | solution.py:82
  60.1 0.7 copy-done.1
  60.8 2.1 fusion.20
  63.1 0.3 fusion.50
  63.4 0.8 convolution_bitcast_fusion.1
  64.2 108.0 %all-gather.6.cloned.1.call-done = bf16[32768,2,128]{2,0,1:T(8,128)(2,1)} async-done(((bf16[1024,2,128]{2,0,1:T(8,128)(2,1)}), bf16[32768,2,128]{2,0,1:T(8,128)(2,1)}) %all-gather.6.cloned.1.call-update) | async-done | bytes 16777232 | tf_op jit(solution)/shard_map/all_gather | solution.py:103
  172.2 13.8 %copy.48 = bf16[32,1024,2,128]{3,1,2,0:T(8,128)(2,1)} copy(bf16[32,1024,2,128]{3,1,0,2:T(8,128)(2,1)} %bitcast.145) | data formatting | bytes 33554432 | tf_op jit(solution)/shard_map/reshape | solution.py:104
  186.0 8.8 %gather_fusion = bf16[8,1024,2,128]{3,1,2,0:T(8,128)(2,1)} fusion(bf16[32,1024,2,128]{3,1,2,0:T(8,128)(2,1)} %copy.48, s32[1024]{0:T(1024)S(1)} %pad_clamp_fusion), kind=kCustom, calls=%fused_computation | custom fusion | bytes 8388640 | tf_op jit(solution)/shard_map/jit(_take)/gather | solution.py:106
  194.8 4.6 %fusion.14 = bf16[8,1024,2,1,128]{4,1,2,3,0:T(8,128)(2,1)} fusion(bf16[8,1024,2,128]{3,1,2,0:T(8,128)(2,1)} %gather_fusion, pred[8]{0:T(512)(128)(4,1)S(1)} %get-tuple-element.72), kind=kLoop, calls=%fused_computation.27 | loop fusion | flops 2097152 | bytes 8388616 | tf_op jit(solution)/shard_map/while | solution.py:107
  199.3 17.9 %while.14 = (s32[]{:T(128)}, f32[128,1,3]{0,2,1:T(4,128)S(1)}, f32[128,1,3]{0,2,1:T(4,128)S(1)}, f32[128,1,3,128]{0,3,2,1:T(8,128)S(1)}, bf16[8,1024,2,1,128]{4,...) while((s32[]{:T(128)}, f32[128,1,3]{0,2,1:T(4,128)S(1)}, f32[128,1,3]{0,2,1:T(4,128)S(1)}, ...), condition=%wide.region_6.7_spmd, body=%wide.region_3.0_spmd.sunk | while | flops 203835264 | bytes 6813777 | solution.py:107
  199.3 1.1 dynamic-slice_bitcast_fusion.2
  200.4 0.4 bitcast_reduce_fusion.2
  200.8 0.2 fusion.63
  201.1 0.5 fusion.65
  201.6 1.1 dynamic-slice_bitcast_fusion.2
  202.7 0.4 bitcast_reduce_fusion.2
  203.3 0.5 fusion.65
  203.8 1.1 dynamic-slice_bitcast_fusion.2
  204.9 0.4 bitcast_reduce_fusion.2
  205.5 0.5 fusion.65
  206.1 1.1 dynamic-slice_bitcast_fusion.2
  207.1 0.4 bitcast_reduce_fusion.2
  207.5 0.2 fusion.63
  207.8 0.5 fusion.65
  208.3 1.1 dynamic-slice_bitcast_fusion.2
  209.4 0.4 bitcast_reduce_fusion.2
  210.0 0.5 fusion.65
  210.5 1.1 dynamic-slice_bitcast_fusion.2
  211.6 0.4 bitcast_reduce_fusion.2
  212.3 0.5 fusion.65
  212.8 1.1 dynamic-slice_bitcast_fusion.2
  213.9 0.4 bitcast_reduce_fusion.2
  214.2 0.2 fusion.63
  214.5 0.5 fusion.65
  215.0 1.1 dynamic-slice_bitcast_fusion.2
  216.1 0.4 bitcast_reduce_fusion.2
  216.8 0.5 fusion.65
  217.3 3.0 %convolution_convert_fusion = bf16[128,5120]{1,0:T(8,128)(2,1)S(1)} fusion(bf16[128,384]{0,1:T(8,128)(2,1)S(1)} %bitcast.150, bf16[384,5120]{1,0:T(8,128)(2,1)} %param.23), kind=kOutput, calls=%fused_computation.25 | convolution fusion | flops 503971840 | bytes 5341184 | tf_op jit(solution)/shard_map/dot_general | solution.py:110
  220.3 1.4 copy.58
  222.4 42.5 %reduce-scatter.4.cloned.1.call-done = bf16[640,128]{1,0:T(8,128)(2,1)} async-done(((bf16[5120,128]{1,0:T(8,128)(2,1)}), bf16[640,128]{1,0:T(8,128)(2,1)}) %reduce-scatter.4.cloned.1.call-update) | async-done | bytes 163856
  264.9 1.1 copy.59
  266.0 0.8 select_convert_fusion
  (68 shorter events, 2.5 us)
Async XLA Ops:
  6.5 56.9 %copy-start = (bf16[5120,128]{1,0:T(8,128)(2,1)S(1)}, bf16[5120,128]{1,0:T(8,128)(2,1)}, u32[]{:S(2)}) copy-start(bf16[5120,128]{1,0:T(8,128)(2,1)} %param.21) | copy-start | bytes 3932164
  6.5 2.8 %copy-start.2 = (bf16[640]{0:T(1024)(128)(2,1)S(1)}, bf16[640]{0:T(1024)(128)(2,1)}, u32[]{:S(2)}) copy-start(bf16[640]{0:T(1024)(128)(2,1)} %param.16) | copy-start | bytes 3844
  6.5 26.2 %copy-start.3 = (bf16[384]{0:T(512)(128)(2,1)S(1)}, bf16[384]{0:T(512)(128)(2,1)}, u32[]{:S(2)}) copy-start(bf16[384]{0:T(512)(128)(2,1)} %param.18) | copy-start | bytes 2308
  6.5 26.2 %copy-start.5 = (bf16[128]{0:T(256)(128)(2,1)S(1)}, bf16[128]{0:T(256)(128)(2,1)}, u32[]{:S(2)}) copy-start(bf16[128]{0:T(256)(128)(2,1)} %param.20) | copy-start | bytes 772
  6.5 26.3 %copy-start.6 = (bf16[128]{0:T(256)(128)(2,1)S(1)}, bf16[128]{0:T(256)(128)(2,1)}, u32[]{:S(2)}) copy-start(bf16[128]{0:T(256)(128)(2,1)} %param.22) | copy-start | bytes 772
  6.5 27.0 %copy-start.4 = (s32[32]{0:T(128)S(1)}, s32[32]{0:T(128)}, u32[]{:S(2)}) copy-start(s32[32]{0:T(128)} %param.27) | copy-start | bytes 388
  6.6 47.8 %all-gather.4.cloned.1.call-start = ((), (), s32[]{:S(2)}) async-start(), calls=%async_computation.1 | async-start | bytes 1474560 | tf_op jit(solution)/shard_map/all_gather | solution.py:75
  7.3 164.9 %all-gather.6.cloned.1.call-start = ((), (), s32[]{:S(2)}) async-start(), calls=%async_computation.2 | async-start | bytes 17301504 | tf_op jit(solution)/shard_map/all_gather | solution.py:103
  9.3 255.6 %reduce-scatter.4.cloned.1.call-start = ((), (), s32[]{:S(2)}) async-start(), calls=%async_computation.3 | async-start | bytes 1474560
  59.5 1.3 copy-start.1
Sparse Core Ops, SparseCore 0:
  9.2 45.1 all-gather.3
  57.0 115.2 all-gather.5
  221.9 42.9 reduce-scatter.3
where the time goes:
time: 278 us; the launch traced here: 273 us
  waiting for transfers between devices  172 us (62%)
  local copies, waits for them, and re-layouts  36.8 us (13%)
  blocking collectives  23.4 us (8%)
  matrix products  16.4 us (6%)
  between operations  14.6 us (5%)
  other arithmetic  9.93 us (4%)
    all_gather x1, waiting for transfers between devices, shards(): everything = lax.all_gather(prefix_kv, 'req', axis=0, tiled=True)  108 us
    unnamed x4, waiting for transfers between devices  43.2 us
    all_gather x1, blocking collectives, shards(): lax.all_gather(norm_gain, 'tp', axis=0, tiled=True)  23.4 us
    all_gather x1, waiting for transfers between devices, shards(): lax.all_gather(hidden_in, 'tp', axis=1, tiled=True)  20.4 us
    reshape x1, local copies, waits for them, and re-layouts, shards(): stacked = everything.reshape(devices, block, 2, kv_heads, HD)  13.8 us
    gather x1, local copies, waits for them, and re-layouts, shards(): chosen = jnp.take(stacked, owners, axis=0)  8.79 us
    squeeze x8, local copies, waits for them, and re-layouts, shards(): state, unused = lax.scan(advance, state, chosen)  8.64 us
  transfers between devices with their start and end apart: 3, of which 3 were waited for; matrix products, arithmetic and copies ran while one was open for 4% of the time, Pallas kernels for 0%

commit v1 on v0

v1 whole, which is shorter than its diff:
```python
import jax
import jax.numpy as jnp
from jax import lax
from jax.sharding import PartitionSpec as P

HD = 128
NPREF = 4


THETA = 1000000.0
EPSILON = 1e-06
ROWS = 144


def rotate(heads, positions):
    half = HD // 2
    freqs = THETA ** (-(jnp.arange(half, dtype=jnp.float32) * 2.0) / HD)
    angles = positions.astype(jnp.float32)[:, None] * freqs[None, :]
    cosine = jnp.cos(angles)[:, None, :]
    sine = jnp.sin(angles)[:, None, :]
    first = heads[..., :half]
    second = heads[..., half:]
    return jnp.concatenate(
        [first * cosine - second * sine, second * cosine + first * sine], axis=-1
    )


def split16(x):
    high = x.astype(jnp.bfloat16)
    low = (x - high.astype(jnp.float32)).astype(jnp.bfloat16)
    return high, low


def join16(high, low):
    return high.astype(jnp.float32) + low.astype(jnp.float32)


def shards(
    hidden_in,
    norm_gain,
    q_weight,
    q_bias,
    k_weight,
    k_bias,
    v_weight,
    v_bias,
    o_weight,
    prefix_kv,
    suffix_len,
    req_prefix,
    block_owner,
):
    length = hidden_in.shape[0]
    devices = lax.axis_size("req")
    owned = devices // NPREF
    block = prefix_kv.shape[0]
    prefix_len = block * owned
    kv_heads = k_weight.shape[1] // HD
    q_heads = q_weight.shape[1] // HD
    group = q_heads // kv_heads
    width = q_heads * HD
    scale = HD ** (-0.5)

    feat = hidden_in.shape[1]
    packed = jnp.concatenate(
        [hidden_in, norm_gain[None, :], jnp.zeros((ROWS - length - 1, feat), hidden_in.dtype)],
        axis=0,
    )
    full = lax.all_gather(packed, "tp", axis=1, tiled=True)
    tokens = full[:length].astype(jnp.float32)
    gain = full[length]
    meansq = jnp.mean(tokens * tokens, axis=-1, keepdims=True)
    normed = (tokens * lax.rsqrt(meansq + EPSILON) * gain.astype(jnp.float32)).astype(jnp.bfloat16)
    positions = prefix_len + jnp.arange(length, dtype=jnp.int32)
    queries = jnp.dot(normed, q_weight, preferred_element_type=jnp.float32) + q_bias.astype(
        jnp.float32
    )
    queries = rotate(queries.reshape(length, q_heads, HD), positions).astype(jnp.bfloat16)
    keys = jnp.dot(normed, k_weight, preferred_element_type=jnp.float32) + k_bias.astype(
        jnp.float32
    )
    keys = rotate(keys.reshape(length, kv_heads, HD), positions).astype(jnp.bfloat16)
    values = jnp.dot(normed, v_weight, preferred_element_type=jnp.float32) + v_bias.astype(
        jnp.float32
    )
    values = values.astype(jnp.bfloat16).reshape(length, kv_heads, HD)

    flat_q = queries.reshape(length, width)
    tag = jnp.full((1, width), req_prefix[0], jnp.int32).astype(jnp.bfloat16)
    qpack = jnp.concatenate(
        [flat_q, tag, jnp.zeros((ROWS - length - 1, width), jnp.bfloat16)], axis=0
    )
    qall = lax.all_gather(qpack, "req", axis=0, tiled=False)
    prefix_of = qall[:, length, 0].astype(jnp.int32)

    me = lax.axis_index("req")
    slots = jnp.arange(devices, dtype=jnp.int32)
    my_block = jnp.sum(jnp.where(block_owner == me, slots, 0))
    my_prefix = my_block // owned
    mine = prefix_of == my_prefix
    rank = jnp.cumsum(mine.astype(jnp.int32)) - 1
    picks = jnp.arange(owned, dtype=jnp.int32)
    chosen = jnp.sum(
        jnp.where(mine[None, :] & (rank[None, :] == picks[:, None]), slots[None, :], 0), axis=1
    )
    qsel = jnp.take(qall[:, :length], chosen, axis=0).reshape(owned, length, q_heads, HD)

    cached_k = prefix_kv[:, 0].reshape(block, HD)
    cached_v = prefix_kv[:, 1].reshape(block, HD)
    scores = jnp.einsum(
        "rshd,kd->rshk", qsel, cached_k, preferred_element_type=jnp.float32
    ) * scale
    peak = jnp.max(scores, axis=-1)
    weights = jnp.exp(scores - peak[..., None])
    total = jnp.sum(weights, axis=-1)
    mixed = jnp.einsum(
        "rshk,kd->rshd", weights.astype(jnp.bfloat16), cached_v, preferred_element_type=jnp.float32
    )
    peak_hi, peak_lo = split16(peak.reshape(owned, 1, width))
    total_hi, total_lo = split16(total.reshape(owned, 1, width))
    chunk = jnp.concatenate(
        [
            mixed.reshape(owned, length, width).astype(jnp.bfloat16),
            peak_hi,
            peak_lo,
            total_hi,
            total_lo,
            jnp.zeros((owned, ROWS - length - 4, width), jnp.bfloat16),
        ],
        axis=1,
    )
    outgoing = jnp.zeros((devices, ROWS, width), jnp.bfloat16).at[chosen].set(chunk)
    incoming = lax.all_to_all(outgoing, "req", 0, 0, tiled=True)

    slot_index = jnp.arange(length, dtype=jnp.int32)
    causal = slot_index[None, :] <= slot_index[:, None]
    grouped = queries.reshape(length, kv_heads, group, HD)
    own_scores = jnp.einsum(
        "sghd,kgd->sghk", grouped, keys, preferred_element_type=jnp.float32
    ) * scale
    own_scores = jnp.where(causal[:, None, None, :], own_scores, -jnp.inf)
    own_peak = jnp.max(own_scores, axis=-1).reshape(length, width // HD)
    own_weights = jnp.exp(own_scores - jnp.max(own_scores, axis=-1)[..., None])
    own_total = jnp.sum(own_weights, axis=-1).reshape(length, width // HD)
    own_mixed = jnp.einsum(
        "sghk,kgd->sghd", own_weights.astype(jnp.bfloat16), values, preferred_element_type=jnp.float32
    ).reshape(length, width // HD, HD)

    owners = lax.dynamic_slice_in_dim(block_owner, req_prefix[0] * owned, owned)
    got = jnp.take(incoming, owners, axis=0)
    got_mixed = got[:, :length].astype(jnp.float32).reshape(owned, length, width // HD, HD)
    got_peak = join16(got[:, length], got[:, length + 1]).reshape(owned, length, width // HD)
    got_total = join16(got[:, length + 2], got[:, length + 3]).reshape(owned, length, width // HD)
    best = jnp.maximum(own_peak, jnp.max(got_peak, axis=0))
    own_scale = jnp.exp(own_peak - best)
    got_scale = jnp.exp(got_peak - best[None])
    summed_total = own_total * own_scale + jnp.sum(got_total * got_scale, axis=0)
    summed_mixed = own_mixed * own_scale[..., None] + jnp.sum(
        got_mixed * got_scale[..., None], axis=0
    )
    context = (summed_mixed / summed_total[..., None]).astype(jnp.bfloat16).reshape(length, width)
    partial_value = jnp.dot(context, o_weight, preferred_element_type=jnp.float32)
    summed = lax.psum_scatter(
        partial_value.astype(jnp.bfloat16), "tp", scatter_dimension=1, tiled=True
    ).astype(jnp.float32)
    valid = slot_index < suffix_len[0]
    return jnp.where(valid[:, None], summed, jnp.float32(0.0)).astype(jnp.bfloat16)


def solution(mesh):
    placed = (
        P("req", "tp"),
        P("tp"),
        P(None, "tp"),
        P("tp"),
        P(None, "tp"),
        P("tp"),
        P(None, "tp"),
        P("tp"),
        P("tp", None),
        P("req", None, "tp"),
        P("req"),
        P("req"),
        P(),
    )
    return jax.shard_map(
        shards, mesh=mesh, in_specs=placed, out_specs=P("req", "tp"), check_vma=False
    )
```

time: 278 us -> 312 us (1.12)
  waiting for transfers between devices: 172 us -> 216 us
  blocking collectives: 23.4 us -> 0 us
  local copies, waits for them, and re-layouts: 36.8 us -> 28.1 us
  other arithmetic: 9.93 us -> 17.6 us
  matrix products: 16.4 us -> 23 us
  starting transfers between devices: 0.12 us -> 6.05 us
    all_to_all x0 -> x1, waiting for transfers between devices: none -> 66.9 us  [shards(): incoming = lax.all_to_all(outgoing, 'req', 0, 0, tiled=True)]
    all_gather x2, waiting for transfers between devices: 128 us -> 101 us  [the longest x1 56.2 us: shards(): qall = lax.all_gather(qpack, 'req', axis=0, tiled=False)]
    all_gather x1 -> x0, blocking collectives: 23.4 us -> none  [shards(): lax.all_gather(norm_gain, 'tp', axis=0, tiled=True)]
    reshape x1 -> x5, local copies, waits for them, and re-layouts: 13.8 us -> 0.46 us  [the longest x2 0.17 us: shards(): total_hi, total_lo = split16(total.reshape(owned, 1, width))]
    squeeze x8 -> x0, local copies, waits for them, and re-layouts: 8.64 us -> none  [shards(): state, unused = lax.scan(advance, state, chosen)]
    reduce_sum x9 -> x6, other arithmetic: 1.87 us -> 8.75 us  [the longest x1 6.28 us: shards(): total = jnp.sum(weights, axis=-1)]
    dot_general x18 -> x4, matrix products: 7.93 us -> 14.6 us  [the longest x1 7.15 us: shards(): jnp.einsum('rshk,kd->rshd', weights.astype(jnp.bfloat16), cached_v, prefe...]
    all_to_all x0 -> x1, starting transfers between devices: none -> 5.96 us  [shards(): incoming = lax.all_to_all(outgoing, 'req', 0, 0, tiled=True)]
  transfers between devices with their start and end apart: 3 -> 4, of which waited for: 3 -> 4; matrix products, arithmetic and copies ran while one was open for 4% -> 2% of each run, Pallas kernels for 0% -> 0%
where the time goes in v1:
time: 312 us; the launch traced here: 308 us
  waiting for transfers between devices  216 us (69%)
  local copies, waits for them, and re-layouts  28.1 us (9%)
  matrix products  23 us (7%)
  other arithmetic  17.6 us (6%)
  between operations  17.2 us (6%)
  starting transfers between devices  6.05 us (2%)
    all_to_all x1, waiting for transfers between devices, shards(): incoming = lax.all_to_all(outgoing, 'req', 0, 0, tiled=True)  66.9 us
    all_gather x1, waiting for transfers between devices, shards(): qall = lax.all_gather(qpack, 'req', axis=0, tiled=False)  56.2 us
    unnamed x4, waiting for transfers between devices  48.1 us
    all_gather x1, waiting for transfers between devices, shards(): full = lax.all_gather(packed, 'tp', axis=1, tiled=True)  44.5 us
    dot_general x1, matrix products, shards(): jnp.einsum('rshk,kd->rshd', weights.astype(jnp.bfloat16), cached_v, prefe...  7.15 us
    dot_general x1, matrix products, shards(): jnp.einsum('rshd,kd->rshk', qsel, cached_k, preferred_element_type=jnp.fl...  6.41 us
    reduce_sum x1, other arithmetic, shards(): total = jnp.sum(weights, axis=-1)  6.28 us
  transfers between devices with their start and end apart: 4, of which 4 were waited for; matrix products, arithmetic and copies ran while one was open for 2% of the time, Pallas kernels for 0%

profile of v1, /device:TPU:1, one launch (start us, length us, event | category | flops | bytes accessed | tf_op | source)
XLA Modules:
  0.0 307.6 jit_solution(4490249992341466335)
XLA Ops:
  6.5 0.8 broadcast_in_dim.109
  7.4 1.7 maximum_maximum_fusion.1
  9.2 0.7 convert_element_type.235
  10.5 0.3 multiply_cosine_fusion
  10.9 44.5 %all-gather.4.cloned.1.call-done = bf16[144,5120]{1,0:T(8,128)(2,1)} async-done(((bf16[144,640]{1,0:T(8,128)(2,1)}), bf16[144,5120]{1,0:T(8,128)(2,1)}) %all-gather.4.cloned.1.call-update) | async-done | bytes 1474576 | tf_op jit(solution)/shard_map/all_gather | solution.py:69
  55.3 1.6 fusion.6
  57.0 0.9 slice_convert_fusion
  57.9 3.4 %convolution_add_fusion = f32[128,384]{1,0:T(8,128)S(1)} fusion(bf16[5120,384]{1,0:T(8,128)(2,1)} %param.15, f32[384]{0:T(512)S(1)} %convert_element_type.235, f32[5120]{0:T(1024)S(1)} %bitcast.90, f32[128]{0:T(128)S(1)} %add_rsqrt_fusion, bf16[144,5120]{1,0:T(8,128)(2,1)} %all-gather.4.cloned.1.call-done), kind=kOutput, calls=%fused_computation.20 | convolution fusion | flops 505987072 | bytes 5462016 | tf_op jit(solution)/shard_map/dot_general | solution.py:75
  61.6 0.1 copy.244
  62.1 0.8 copy.203
  62.9 0.6 fusion.39
  65.8 0.7 fusion.48
  66.6 1.0 copy.246
  67.6 56.2 %all-gather.6.cloned.1.call-done = bf16[4608,384]{1,0:T(8,128)(2,1)} async-done(((bf16[144,384]{1,0:T(8,128)(2,1)}), bf16[4608,384]{1,0:T(8,128)(2,1)}) %all-gather.6.cloned.1.call-update) | async-done | bytes 3538960 | tf_op jit(solution)/shard_map/all_gather | solution.py:93
  123.7 4.1 %slice.71 = bf16[32,128,384]{2,1,0:T(8,128)(2,1)} slice(bf16[32,144,384]{2,1,0:T(8,128)(2,1)} %bitcast.81), slice={[0:32], [0:128], [0:384]} | slice | bytes 6291456 | tf_op jit(solution)/shard_map/slice | solution.py:106
  127.8 1.5 compare_reduce_fusion
  129.6 2.6 gather_fusion
  132.2 0.2 broadcast_select_fusion
  132.4 0.4 copy.205
  132.8 6.4 %multiply_reduce_fusion = (f32[8,128,3]{1,2,0:T(4,128)S(1)}, f32[8,128,3,1024]{3,1,2,0:T(8,128)}) fusion(bf16[8,128,3,128]{1,3,2,0:T(8,128)(2,1)S(1)} %bitcast.78, bf16[1024,1,128]{2,1,0:T(2,128)(2,1)S(1)} %get-tuple-element.19), kind=kOutput, calls=%fused_computation.4 | convolution fusion | flops 811594752 | bytes 13643776 | tf_op jit(solution)/shard_map/rshd,kd->rshk/dot_general | solution.py:110
  139.2 0.2 copy.209
  139.4 6.3 %fusion = f32[8,128,3]{1,2,0:T(4,128)S(1)} fusion(f32[8,128,3,1024]{3,1,2,0:T(8,128)} %get-tuple-element.29, f32[8,128,3]{1,2,0:T(4,128)S(1)} %get-tuple-element.28), kind=kLoop, calls=%fused_computation.5 | loop fusion | flops 9434112 | bytes 12607488 | tf_op jit(solution)/shard_map/reduce_sum | solution.py:115
  145.7 0.2 copy.212
  146.1 7.2 %fusion.9 = bf16[8,128,3,128]{1,3,2,0:T(8,128)(2,1)S(1)} fusion(f32[8,128,3,1024]{3,1,2,0:T(8,128)} %get-tuple-element.29, f32[8,128,3]{1,2,0:T(4,128)S(1)} %get-tuple-element.28, bf16[1024,1,128]{0,2,1:T(8,128)(2,1)S(1)} %copy-done.4), kind=kOutput, calls=%fused_computation.17 | convolution fusion | flops 815136768 | bytes 13643776 | tf_op jit(solution)/shard_map/rshk,kd->rshd/dot_general | solution.py:116
  153.2 0.4 copy.215
  153.9 0.8 concatenate.31
  154.7 2.1 broadcast_in_dim.114
  156.8 2.8 scatter_fusion
  159.6 6.0 %all-to-all-start = ((bf16[32,144,384]{2,1,0:T(8,128)(2,1)}), bf16[32,144,384]{2,1,0:T(8,128)(2,1)}, u32[]{:S(2)}, u32[]{:S(2)}) async-start(bf16[32,144,384]{2,1,0:T(8,128)(2,1)} %scatter_fusion), calls=%async_computation | async-start | bytes 7077888 | tf_op jit(solution)/shard_map/all_to_all | solution.py:133
  165.8 2.1 fusion.14
  167.9 0.2 fusion.37
  168.1 0.2 fusion.50
  168.4 0.2 reduce_max.39
  168.7 0.8 fusion.17
  169.6 66.9 %all-to-all-done = bf16[32,144,384]{2,1,0:T(8,128)(2,1)} async-done(((bf16[32,144,384]{2,1,0:T(8,128)(2,1)}), bf16[32,144,384]{2,1,0:T(8,128)(2,1)}, u32[]{:S(2)}, u32[]{:S(2)}) %all-to-all-start) | async-done | bytes 3538976 | tf_op jit(solution)/shard_map/all_to_all | solution.py:133
  236.5 2.7 gather_fusion.1
  239.2 0.2 copy_select_fusion
  239.5 0.2 reduce_max.38
  239.7 0.2 reduce_sum.75
  240.5 0.2 subtract_exponential_fusion.1
  240.8 1.3 mul.257
  242.1 2.0 copy.227
  244.1 1.6 multiply_reduce_fusion.1
  246.0 3.0 convolution_convert_fusion
  249.0 1.5 copy.240
  251.2 48.1 %reduce-scatter.4.cloned.1.call-done = bf16[640,128]{1,0:T(8,128)(2,1)} async-done(((bf16[5120,128]{1,0:T(8,128)(2,1)}), bf16[640,128]{1,0:T(8,128)(2,1)}) %reduce-scatter.4.cloned.1.call-update) | async-done | bytes 163856
  299.2 1.1 copy.241
  300.3 0.8 select_convert_fusion
  (75 shorter events, 3.0 us)
Async XLA Ops:
  6.5 162.1 %copy-start = (bf16[5120,128]{1,0:T(8,128)(2,1)S(1)}, bf16[5120,128]{1,0:T(8,128)(2,1)}, u32[]{:S(2)}) copy-start(bf16[5120,128]{1,0:T(8,128)(2,1)} %param.19) | copy-start | bytes 3932164
  6.5 48.8 %all-gather.4.cloned.1.call-start = ((), (), s32[]{:S(2)}) async-start(), calls=%async_computation.2 | async-start | bytes 1658880 | tf_op jit(solution)/shard_map/all_gather | solution.py:69
  9.1 114.6 %all-gather.6.cloned.1.call-start = ((), (), s32[]{:S(2)}) async-start(), calls=%async_computation.3 | async-start | bytes 3649536 | tf_op jit(solution)/shard_map/all_gather | solution.py:93
  61.3 1.6 copy-start.5
  61.3 4.5 %copy-start.2 = (bf16[1024,2,128]{2,1,0:T(2,128)(2,1)S(1)}, bf16[1024,2,128]{2,1,0:T(2,128)(2,1)}, u32[]{:S(2)}) copy-start(bf16[1024,2,128]{2,1,0:T(2,128)(2,1)} %param.22) | copy-start | bytes 1572868
  139.4 6.7 %copy-start.4 = (bf16[1024,1,128]{0,2,1:T(8,128)(2,1)S(1)}, bf16[1024,1,128]{0,2,1:T(8,128)(2,1)}, u32[]{:S(2)}) copy-start(bf16[1024,1,128]{0,2,1:T(8,128)(2,1)} %copy.246) | copy-start | bytes 786436
  159.6 6.0 %copy-start.6 = (bf16[128]{0:T(256)(128)(2,1)S(1)}, bf16[128]{0:T(256)(128)(2,1)}, u32[]{:S(2)}) copy-start(bf16[128]{0:T(256)(128)(2,1)} %param.18) | copy-start | bytes 772
  159.6 6.1 %copy-start.7 = (bf16[128]{0:T(256)(128)(2,1)S(1)}, bf16[128]{0:T(256)(128)(2,1)}, u32[]{:S(2)}) copy-start(bf16[128]{0:T(256)(128)(2,1)} %param.20) | copy-start | bytes 772
  159.6 6.2 %copy-start.3 = (bf16[144,5120]{1,0:T(8,128)(2,1)S(1)}, bf16[144,5120]{1,0:T(8,128)(2,1)}, u32[]{:S(2)}) copy-start(bf16[144,5120]{1,0:T(8,128)(2,1)} %all-gather.4.cloned.1.call-done) | copy-start | bytes 4423684
  159.6 76.9 %all-to-all-start = ((bf16[32,144,384]{2,1,0:T(8,128)(2,1)}), bf16[32,144,384]{2,1,0:T(8,128)(2,1)}, u32[]{:S(2)}, u32[]{:S(2)}) async-start(bf16[32,144,384]{2,1,0:T(8,128)(2,1)} %scatter_fusion), calls=%async_computation | async-start | bytes 7077888 | tf_op jit(solution)/shard_map/all_to_all | solution.py:133
  165.6 133.6 %reduce-scatter.4.cloned.1.call-start = ((), (), s32[]{:S(2)}) async-start(), calls=%async_computation.4 | async-start | bytes 1474560
  239.5 2.6 copy-start.1
Sparse Core Ops, SparseCore 0:
  9.2 46.0 all-gather.3
  63.0 60.6 all-gather.5
  250.6 48.5 reduce-scatter.3

commit v2 on v1

--- a/solution.py
+++ b/solution.py
@@ -26,13 +26,25 @@
 
 
 def split16(x):
-    high = x.astype(jnp.bfloat16)
-    low = (x - high.astype(jnp.float32)).astype(jnp.bfloat16)
-    return high, low
+    high = lax.reduce_precision(x, exponent_bits=8, mantissa_bits=7)
+    low = x - high
+    return high.astype(jnp.bfloat16), low.astype(jnp.bfloat16)
 
 
 def join16(high, low):
     return high.astype(jnp.float32) + low.astype(jnp.float32)
+
+
+def shifted(x, axis, n, shift):
+    return lax.ppermute(x, axis, [(i, (i + shift) % n) for i in range(n)])
+
+
+def gather_by_shift(x, axis, n):
+    return jnp.stack([x] + [shifted(x, axis, n, s) for s in range(1, n)])
+
+
+def exchange_by_shift(x, axis, n):
+    return jnp.stack([x[0]] + [shifted(x[s], axis, n, s) for s in range(1, n)])
 
 
 def shards(
@@ -66,7 +78,11 @@
         [hidden_in, norm_gain[None, :], jnp.zeros((ROWS - length - 1, feat), hidden_in.dtype)],
         axis=0,
     )
-    full = lax.all_gather(packed, "tp", axis=1, tiled=True)
+    n_tp = lax.axis_size("tp")
+    me_tp = lax.axis_index("tp")
+    by_shift = gather_by_shift(packed, "tp", n_tp)
+    ordered = jnp.take(by_shift, (me_tp - jnp.arange(n_tp, dtype=jnp.int32)) % n_tp, axis=0)
+    full = ordered.transpose(1, 0, 2).reshape(ROWS, n_tp * feat)
     tokens = full[:length].astype(jnp.float32)
     gain = full[length]
     meansq = jnp.mean(tokens * tokens, axis=-1, keepdims=True)
@@ -90,11 +106,10 @@
     qpack = jnp.concatenate(
         [flat_q, tag, jnp.zeros((ROWS - length - 1, width), jnp.bfloat16)], axis=0
     )
-    qall = lax.all_gather(qpack, "req", axis=0, tiled=False)
-    prefix_of = qall[:, length, 0].astype(jnp.int32)
-
+    qall = gather_by_shift(qpack, "req", devices)
     me = lax.axis_index("req")
     slots = jnp.arange(devices, dtype=jnp.int32)
+    prefix_of = jnp.take(qall[:, length, 0].astype(jnp.int32), (me - slots) % devices)
     my_block = jnp.sum(jnp.where(block_owner == me, slots, 0))
     my_prefix = my_block // owned
     mine = prefix_of == my_prefix
@@ -103,7 +118,7 @@
     chosen = jnp.sum(
         jnp.where(mine[None, :] & (rank[None, :] == picks[:, None]), slots[None, :], 0), axis=1
     )
-    qsel = jnp.take(qall[:, :length], chosen, axis=0).reshape(owned, length, q_heads, HD)
+    qsel = jnp.take(qall[:, :length], (me - chosen) % devices, axis=0).reshape(owned, length, q_heads, HD)
 
     cached_k = prefix_kv[:, 0].reshape(block, HD)
     cached_v = prefix_kv[:, 1].reshape(block, HD)
@@ -129,8 +144,8 @@
         ],
         axis=1,
     )
-    outgoing = jnp.zeros((devices, ROWS, width), jnp.bfloat16).at[chosen].set(chunk)
-    incoming = lax.all_to_all(outgoing, "req", 0, 0, tiled=True)
+    outgoing = jnp.zeros((devices, ROWS, width), jnp.bfloat16).at[(chosen - me) % devices].set(chunk)
+    incoming = exchange_by_shift(outgoing, "req", devices)
 
     slot_index = jnp.arange(length, dtype=jnp.int32)
     causal = slot_index[None, :] <= slot_index[:, None]
@@ -147,7 +162,7 @@
     ).reshape(length, width // HD, HD)
 
     owners = lax.dynamic_slice_in_dim(block_owner, req_prefix[0] * owned, owned)
-    got = jnp.take(incoming, owners, axis=0)
+    got = jnp.take(incoming, (me - owners) % devices, axis=0)
     got_mixed = got[:, :length].astype(jnp.float32).reshape(owned, length, width // HD, HD)
     got_peak = join16(got[:, length], got[:, length + 1]).reshape(owned, length, width // HD)
     got_total = join16(got[:, length + 2], got[:, length + 3]).reshape(owned, length, width // HD)
@@ -160,9 +175,9 @@
     )
     context = (summed_mixed / summed_total[..., None]).astype(jnp.bfloat16).reshape(length, width)
     partial_value = jnp.dot(context, o_weight, preferred_element_type=jnp.float32)
-    summed = lax.psum_scatter(
-        partial_value.astype(jnp.bfloat16), "tp", scatter_dimension=1, tiled=True
-    ).astype(jnp.float32)
+    pieces = partial_value.astype(jnp.bfloat16).reshape(length, n_tp, feat).transpose(1, 0, 2)
+    pieces = jnp.take(pieces, (me_tp + jnp.arange(n_tp, dtype=jnp.int32)) % n_tp, axis=0)
+    summed = jnp.sum(exchange_by_shift(pieces, "tp", n_tp).astype(jnp.float32), axis=0)
     valid = slot_index < suffix_len[0]
     return jnp.where(valid[:, None], summed, jnp.float32(0.0)).astype(jnp.bfloat16)
 

time: 312 us -> 505 us (1.62)
  the two profiles are of different devices: /device:TPU:1 before, /device:TPU:184 now
where the time goes in v2:
time: 505 us; the launch traced here: 496 us
  starting transfers between devices  281 us (56%)
  local copies, waits for them, and re-layouts  91.8 us (18%)
  waiting for transfers between devices  66.5 us (13%)
  other arithmetic  30.9 us (6%)
  matrix products  21 us (4%)
    ppermute x76, starting transfers between devices, shifted(): return lax.ppermute(x, axis, [(i, (i + shift) % n) for i in range(n)])  281 us
    ppermute x76, waiting for transfers between devices, shifted(): return lax.ppermute(x, axis, [(i, (i + shift) % n) for i in range(n)])  66.5 us
    unnamed x115, local copies, waits for them, and re-layouts  51.1 us
  transfers between devices with their start and end apart: 76, of which 14 were waited for; matrix products, arithmetic and copies ran while one was open for 14% of the time, Pallas kernels for 0%

profile of v2, /device:TPU:184, one launch (start us, length us, event | category | flops | bytes accessed | tf_op | source)
XLA Modules:
  0.0 496.0 jit_solution(3057414304516735038)
XLA Ops:
  28.1 2.5 collective-permute-start.6
  41.5 3.2 copy.245
  44.7 3.6 fusion.7
  57.6 2.6 collective-permute-start.9
  70.8 4.8 collective-permute-start.13
  81.8 6.5 %collective-permute-start.16 = (bf16[144,384]{1,0:T(8,128)(2,1)}, bf16[144,384]{1,0:T(8,128)(2,1)S(1)}, u32[]{:S(2)}, u32[]{:S(2)}) collective-permute-start(bf16[144,384]{1,0:T(8,128)(2,1)} %maximum_maximum_fusion.1), channel_id=1, source_target_pairs={{0,80},{8,88},{16,96},{24,104},{32,112},{40,120},{48,128},{56,136}... | collective-permute-start | bytes 331784 | tf_op jit(solution)/shard_map/ppermute | solution.py:39
  89.9 2.5 collective-permute-start.17
  95.2 5.2 %collective-permute-start.19 = (bf16[144,384]{1,0:T(8,128)(2,1)}, bf16[144,384]{1,0:T(8,128)(2,1)S(1)}, u32[]{:S(2)}, u32[]{:S(2)}) collective-permute-start(bf16[144,384]{1,0:T(8,128)(2,1)} %maximum_maximum_fusion.1), channel_id=1, source_target_pairs={{0,104},{8,112},{16,120},{24,128},{32,136},{40,144},{48,152},{56,1... | collective-permute-start | bytes 331784 | tf_op jit(solution)/shard_map/ppermute | solution.py:39
  101.1 14.6 %collective-permute-done.15 = bf16[144,384]{1,0:T(8,128)(2,1)S(1)} collective-permute-done((bf16[144,384]{1,0:T(8,128)(2,1)}, bf16[144,384]{1,0:T(8,128)(2,1)S(1)}, u32[]{:S(2)}, u32[]{:S(2)}) %collective-permute-start.15) | collective-permute-done | bytes 110624 | tf_op jit(solution)/shard_map/ppermute | solution.py:39
  118.2 26.7 %collective-permute-start.23 = (bf16[144,384]{1,0:T(8,128)(2,1)}, bf16[144,384]{1,0:T(8,128)(2,1)S(1)}, u32[]{:S(2)}, u32[]{:S(2)}) collective-permute-start(bf16[144,384]{1,0:T(8,128)(2,1)} %maximum_maximum_fusion.1), channel_id=1, source_target_pairs={{0,136},{8,144},{16,152},{24,160},{32,168},{40,176},{48,184},{56,1... | collective-permute-start | bytes 331784 | tf_op jit(solution)/shard_map/ppermute | solution.py:39
  145.5 5.9 %collective-permute-start.24 = (bf16[144,384]{1,0:T(8,128)(2,1)}, bf16[144,384]{1,0:T(8,128)(2,1)S(1)}, u32[]{:S(2)}, u32[]{:S(2)}) collective-permute-start(bf16[144,384]{1,0:T(8,128)(2,1)} %maximum_maximum_fusion.1), channel_id=1, source_target_pairs={{0,144},{8,152},{16,160},{24,168},{32,176},{40,184},{48,192},{56,2... | collective-permute-start | bytes 331784 | tf_op jit(solution)/shard_map/ppermute | solution.py:39
  152.1 7.2 %collective-permute-start.25 = (bf16[144,384]{1,0:T(8,128)(2,1)}, bf16[144,384]{1,0:T(8,128)(2,1)S(1)}, u32[]{:S(2)}, u32[]{:S(2)}) collective-permute-start(bf16[144,384]{1,0:T(8,128)(2,1)} %maximum_maximum_fusion.1), channel_id=1, source_target_pairs={{0,152},{8,160},{16,168},{24,176},{32,184},{40,192},{48,200},{56,2... | collective-permute-start | bytes 331784 | tf_op jit(solution)/shard_map/ppermute | solution.py:39
  160.8 3.2 collective-permute-start.27
  164.7 5.6 %collective-permute-start.28 = (bf16[144,384]{1,0:T(8,128)(2,1)}, bf16[144,384]{1,0:T(8,128)(2,1)S(1)}, u32[]{:S(2)}, u32[]{:S(2)}) collective-permute-start(bf16[144,384]{1,0:T(8,128)(2,1)} %maximum_maximum_fusion.1), channel_id=1, source_target_pairs={{0,176},{8,184},{16,192},{24,200},{32,208},{40,216},{48,224},{56,2... | collective-permute-start | bytes 331784 | tf_op jit(solution)/shard_map/ppermute | solution.py:39
  172.6 12.6 %collective-permute-done.25 = bf16[144,384]{1,0:T(8,128)(2,1)S(1)} collective-permute-done((bf16[144,384]{1,0:T(8,128)(2,1)}, bf16[144,384]{1,0:T(8,128)(2,1)S(1)}, u32[]{:S(2)}, u32[]{:S(2)}) %collective-permute-start.25) | collective-permute-done | bytes 110624 | tf_op jit(solution)/shard_map/ppermute | solution.py:39
  188.9 4.7 collective-permute-start.31
  197.1 4.1 collective-permute-done.28
  204.8 12.1 %collective-permute-start.36 = (bf16[144,384]{1,0:T(8,128)(2,1)}, bf16[144,384]{1,0:T(8,128)(2,1)S(1)}, u32[]{:S(2)}, u32[]{:S(2)}) collective-permute-start(bf16[144,384]{1,0:T(8,128)(2,1)} %maximum_maximum_fusion.1), channel_id=1, source_target_pairs={{0,240},{8,248},{16,0},{24,8},{32,16},{40,24},{48,32},{56,40},{64,... | collective-permute-start | bytes 331784 | tf_op jit(solution)/shard_map/ppermute | solution.py:39
  217.6 12.0 %collective-permute-start.37 = (bf16[144,384]{1,0:T(8,128)(2,1)}, bf16[144,384]{1,0:T(8,128)(2,1)S(1)}, u32[]{:S(2)}, u32[]{:S(2)}) collective-permute-start(bf16[144,384]{1,0:T(8,128)(2,1)} %maximum_maximum_fusion.1), channel_id=1, source_target_pairs={{0,248},{8,0},{16,8},{24,16},{32,24},{40,32},{48,40},{56,48},{64,5... | collective-permute-start | bytes 331784 | tf_op jit(solution)/shard_map/ppermute | solution.py:39
  233.6 4.1 slice.239
  240.5 2.6 gather_fusion.2
  243.6 6.4 %multiply_reduce_fusion = (f32[8,128,3]{1,2,0:T(4,128)S(1)}, f32[8,128,3,1024]{3,1,2,0:T(8,128)}) fusion(bf16[8,128,3,128]{1,3,2,0:T(8,128)(2,1)S(1)} %bitcast.338, bf16[1024,1,128]{2,1,0:T(2,128)(2,1)S(1)} %get-tuple-element.53), kind=kOutput, calls=%fused_computation.7 | convolution fusion | flops 811594752 | bytes 13643776 | tf_op jit(solution)/shard_map/rshd,kd->rshk/dot_general | solution.py:125
  250.2 6.3 %fusion = f32[8,128,3]{1,2,0:T(4,128)S(1)} fusion(f32[8,128,3,1024]{3,1,2,0:T(8,128)} %get-tuple-element.69, f32[8,128,3]{1,2,0:T(4,128)S(1)} %get-tuple-element.68), kind=kLoop, calls=%fused_computation.8 | loop fusion | flops 9434112 | bytes 12607488 | tf_op jit(solution)/shard_map/reduce_sum | solution.py:130
  256.9 7.2 %fusion.8 = bf16[8,128,3,128]{1,3,2,0:T(8,128)(2,1)S(1)} fusion(f32[8,128,3,1024]{3,1,2,0:T(8,128)} %get-tuple-element.69, f32[8,128,3]{1,2,0:T(4,128)S(1)} %get-tuple-element.68, bf16[1024,1,128]{0,2,1:T(8,128)(2,1)S(1)} %copy-done.5), kind=kOutput, calls=%fused_computation.21 | convolution fusion | flops 815136768 | bytes 13643776 | tf_op jit(solution)/shard_map/rshk,kd->rshd/dot_general | solution.py:131
  267.6 2.8 scatter_fusion
  281.2 2.5 collective-permute-start.43
  284.4 2.8 collective-permute-start.44
  290.8 4.1 collective-permute-done.42
  294.9 4.1 collective-permute-start.47
  299.6 3.3 collective-permute-start.48
  303.6 2.6 collective-permute-done.44
  308.6 2.5 collective-permute-done.45
  311.7 5.6 %collective-permute-start.51 = (bf16[144,384]{1,0:T(8,128)(2,1)S(1)}, bf16[144,384]{1,0:T(8,128)(2,1)S(1)}, u32[]{:S(2)}, u32[]{:S(2)}) collective-permute-start(bf16[144,384]{1,0:T(8,128)(2,1)S(1)} %get-tuple-element.27), channel_id=1, source_target_pairs={{0,112},{8,120},{16,128},{24,136},{32,144},{40,152},{48,160},{56,1... | collective-permute-start | bytes 331784 | tf_op jit(solution)/shard_map/ppermute | solution.py:39
  318.7 3.4 collective-permute-start.53
  322.8 4.3 collective-permute-start.54
  327.8 2.9 collective-permute-start.55
  331.3 3.4 collective-permute-start.56
  335.3 2.7 collective-permute-start.57
  338.7 3.7 collective-permute-start.58
  343.0 15.1 %collective-permute-start.59 = (bf16[144,384]{1,0:T(8,128)(2,1)S(1)}, bf16[144,384]{1,0:T(8,128)(2,1)S(1)}, u32[]{:S(2)}, u32[]{:S(2)}) collective-permute-start(bf16[144,384]{1,0:T(8,128)(2,1)S(1)} %get-tuple-element.19), channel_id=1, source_target_pairs={{0,176},{8,184},{16,192},{24,200},{32,208},{40,216},{48,224},{56,2... | collective-permute-start | bytes 331784 | tf_op jit(solution)/shard_map/ppermute | solution.py:39
  361.3 7.5 %collective-permute-start.63 = (bf16[144,384]{1,0:T(8,128)(2,1)S(1)}, bf16[144,384]{1,0:T(8,128)(2,1)S(1)}, u32[]{:S(2)}, u32[]{:S(2)}) collective-permute-start(bf16[144,384]{1,0:T(8,128)(2,1)S(1)} %get-tuple-element.15), channel_id=1, source_target_pairs={{0,208},{8,216},{16,224},{24,232},{32,240},{40,248},{48,0},{56,8},... | collective-permute-start | bytes 331784 | tf_op jit(solution)/shard_map/ppermute | solution.py:39
  373.7 4.5 collective-permute-start.66
  378.9 57.6 %collective-permute-start.67 = (bf16[144,384]{1,0:T(8,128)(2,1)S(1)}, bf16[144,384]{1,0:T(8,128)(2,1)S(1)}, u32[]{:S(2)}, u32[]{:S(2)}) collective-permute-start(bf16[144,384]{1,0:T(8,128)(2,1)S(1)} %get-tuple-element.11), channel_id=1, source_target_pairs={{0,240},{8,248},{16,0},{24,8},{32,16},{40,24},{48,32},{56,40},{64,... | collective-permute-start | bytes 331784 | tf_op jit(solution)/shard_map/ppermute | solution.py:39
  437.1 11.8 %collective-permute-start.68 = (bf16[144,384]{1,0:T(8,128)(2,1)S(1)}, bf16[144,384]{1,0:T(8,128)(2,1)S(1)}, u32[]{:S(2)}, u32[]{:S(2)}) collective-permute-start(bf16[144,384]{1,0:T(8,128)(2,1)S(1)} %get-tuple-element.10), channel_id=1, source_target_pairs={{0,248},{8,0},{16,8},{24,16},{32,24},{40,32},{48,40},{56,48},{64,5... | collective-permute-start | bytes 331784 | tf_op jit(solution)/shard_map/ppermute | solution.py:39
  452.9 2.9 gather_fusion.3
  461.6 3.0 convolution_convert_fusion
  476.7 11.0 %collective-permute-done.70 = bf16[128,640]{1,0:T(8,128)(2,1)S(1)} collective-permute-done((bf16[128,640]{1,0:T(8,128)(2,1)S(1)}, bf16[128,640]{1,0:T(8,128)(2,1)S(1)}, u32[]{:S(2)}, u32[]{:S(2)}) %collective-permute-start.70) | collective-permute-done | bytes 163872 | tf_op jit(solution)/shard_map/ppermute | solution.py:39
  487.9 6.9 %collective-permute-done.75 = bf16[128,640]{1,0:T(8,128)(2,1)S(1)} collective-permute-done((bf16[128,640]{1,0:T(8,128)(2,1)S(1)}, bf16[128,640]{1,0:T(8,128)(2,1)S(1)}, u32[]{:S(2)}, u32[]{:S(2)}) %collective-permute-start.75) | collective-permute-done | bytes 163872 | tf_op jit(solution)/shard_map/ppermute | solution.py:39
  (339 shorter events, 153.7 us)
Async XLA Ops:
  1.9 24.6 %collective-permute-start = (bf16[144,640]{1,0:T(8,128)(2,1)S(1)}, bf16[144,640]{1,0:T(8,128)(2,1)S(1)}, u32[]{:S(2)}, u32[]{:S(2)}) collective-permute-start(bf16[144,640]{1,0:T(8,128)(2,1)S(1)} %maximum_maximum_fusion), channel_id=1, source_target_pairs={{0,1},{1,2},{2,3},{3,4},{4,5},{5,6},{6,7},{7,0},{8,9},{9,10},{10,1... | collective-permute-start | bytes 552968 | tf_op jit(solution)/shard_map/ppermute | solution.py:39
  3.9 24.2 %collective-permute-start.1 = (bf16[144,640]{1,0:T(8,128)(2,1)S(1)}, bf16[144,640]{1,0:T(8,128)(2,1)S(1)}, u32[]{:S(2)}, u32[]{:S(2)}) collective-permute-start(bf16[144,640]{1,0:T(8,128)(2,1)S(1)} %maximum_maximum_fusion), channel_id=1, source_target_pairs={{0,2},{1,3},{2,4},{3,5},{4,6},{5,7},{6,0},{7,1},{8,10},{9,11},{10,... | collective-permute-start | bytes 552968 | tf_op jit(solution)/shard_map/ppermute | solution.py:39
  5.4 25.9 %collective-permute-start.2 = (bf16[144,640]{1,0:T(8,128)(2,1)S(1)}, bf16[144,640]{1,0:T(8,128)(2,1)S(1)}, u32[]{:S(2)}, u32[]{:S(2)}) collective-permute-start(bf16[144,640]{1,0:T(8,128)(2,1)S(1)} %maximum_maximum_fusion), channel_id=1, source_target_pairs={{0,3},{1,4},{2,5},{3,6},{4,7},{5,0},{6,1},{7,2},{8,11},{9,12},{10,... | collective-permute-start | bytes 552968 | tf_op jit(solution)/shard_map/ppermute | solution.py:39
  7.7 24.3 %collective-permute-start.3 = (bf16[144,640]{1,0:T(8,128)(2,1)S(1)}, bf16[144,640]{1,0:T(8,128)(2,1)S(1)}, u32[]{:S(2)}, u32[]{:S(2)}) collective-permute-start(bf16[144,640]{1,0:T(8,128)(2,1)S(1)} %maximum_maximum_fusion), channel_id=1, source_target_pairs={{0,4},{1,5},{2,6},{3,7},{4,0},{5,1},{6,2},{7,3},{8,12},{9,13},{10,... | collective-permute-start | bytes 552968 | tf_op jit(solution)/shard_map/ppermute | solution.py:39
  8.5 24.2 %collective-permute-start.4 = (bf16[144,640]{1,0:T(8,128)(2,1)S(1)}, bf16[144,640]{1,0:T(8,128)(2,1)S(1)}, u32[]{:S(2)}, u32[]{:S(2)}) collective-permute-start(bf16[144,640]{1,0:T(8,128)(2,1)S(1)} %maximum_maximum_fusion), channel_id=1, source_target_pairs={{0,5},{1,6},{2,7},{3,0},{4,1},{5,2},{6,3},{7,4},{8,13},{9,14},{10,... | collective-permute-start | bytes 552968 | tf_op jit(solution)/shard_map/ppermute | solution.py:39
  57.6 19.6 %collective-permute-start.9 = (bf16[144,384]{1,0:T(8,128)(2,1)}, bf16[144,384]{1,0:T(8,128)(2,1)}, u32[]{:S(2)}, u32[]{:S(2)}) collective-permute-start(bf16[144,384]{1,0:T(8,128)(2,1)} %maximum_maximum_fusion.1), channel_id=1, source_target_pairs={{0,24},{8,32},{16,40},{24,48},{32,56},{40,64},{48,72},{56,80},{64,... | collective-permute-start | bytes 331784 | tf_op jit(solution)/shard_map/ppermute | solution.py:39
  60.2 20.0 %collective-permute-start.10 = (bf16[144,384]{1,0:T(8,128)(2,1)}, bf16[144,384]{1,0:T(8,128)(2,1)}, u32[]{:S(2)}, u32[]{:S(2)}) collective-permute-start(bf16[144,384]{1,0:T(8,128)(2,1)} %maximum_maximum_fusion.1), channel_id=1, source_target_pairs={{0,32},{8,40},{16,48},{24,56},{32,64},{40,72},{48,80},{56,88},{64,... | collective-permute-start | bytes 331784 | tf_op jit(solution)/shard_map/ppermute | solution.py:39
  61.3 20.5 %collective-permute-start.11 = (bf16[144,384]{1,0:T(8,128)(2,1)}, bf16[144,384]{1,0:T(8,128)(2,1)}, u32[]{:S(2)}, u32[]{:S(2)}) collective-permute-start(bf16[144,384]{1,0:T(8,128)(2,1)} %maximum_maximum_fusion.1), channel_id=1, source_target_pairs={{0,40},{8,48},{16,56},{24,64},{32,72},{40,80},{48,88},{56,96},{64,... | collective-permute-start | bytes 331784 | tf_op jit(solution)/shard_map/ppermute | solution.py:39
  67.2 22.6 %collective-permute-start.12 = (bf16[144,384]{1,0:T(8,128)(2,1)}, bf16[144,384]{1,0:T(8,128)(2,1)S(1)}, u32[]{:S(2)}, u32[]{:S(2)}) collective-permute-start(bf16[144,384]{1,0:T(8,128)(2,1)} %maximum_maximum_fusion.1), channel_id=1, source_target_pairs={{0,48},{8,56},{16,64},{24,72},{32,80},{40,88},{48,96},{56,104},{64... | collective-permute-start | bytes 331784 | tf_op jit(solution)/shard_map/ppermute | solution.py:39
  70.8 22.2 %collective-permute-start.13 = (bf16[144,384]{1,0:T(8,128)(2,1)}, bf16[144,384]{1,0:T(8,128)(2,1)S(1)}, u32[]{:S(2)}, u32[]{:S(2)}) collective-permute-start(bf16[144,384]{1,0:T(8,128)(2,1)} %maximum_maximum_fusion.1), channel_id=1, source_target_pairs={{0,56},{8,64},{16,72},{24,80},{32,88},{40,96},{48,104},{56,112},{6... | collective-permute-start | bytes 331784 | tf_op jit(solution)/shard_map/ppermute | solution.py:39
  80.2 35.5 %collective-permute-start.15 = (bf16[144,384]{1,0:T(8,128)(2,1)}, bf16[144,384]{1,0:T(8,128)(2,1)S(1)}, u32[]{:S(2)}, u32[]{:S(2)}) collective-permute-start(bf16[144,384]{1,0:T(8,128)(2,1)} %maximum_maximum_fusion.1), channel_id=1, source_target_pairs={{0,72},{8,80},{16,88},{24,96},{32,104},{40,112},{48,120},{56,128},... | collective-permute-start | bytes 331784 | tf_op jit(solution)/shard_map/ppermute | solution.py:39
  81.8 34.6 %collective-permute-start.16 = (bf16[144,384]{1,0:T(8,128)(2,1)}, bf16[144,384]{1,0:T(8,128)(2,1)S(1)}, u32[]{:S(2)}, u32[]{:S(2)}) collective-permute-start(bf16[144,384]{1,0:T(8,128)(2,1)} %maximum_maximum_fusion.1), channel_id=1, source_target_pairs={{0,80},{8,88},{16,96},{24,104},{32,112},{40,120},{48,128},{56,136}... | collective-permute-start | bytes 331784 | tf_op jit(solution)/shard_map/ppermute | solution.py:39
  89.9 27.2 %collective-permute-start.17 = (bf16[144,384]{1,0:T(8,128)(2,1)}, bf16[144,384]{1,0:T(8,128)(2,1)S(1)}, u32[]{:S(2)}, u32[]{:S(2)}) collective-permute-start(bf16[144,384]{1,0:T(8,128)(2,1)} %maximum_maximum_fusion.1), channel_id=1, source_target_pairs={{0,88},{8,96},{16,104},{24,112},{32,120},{40,128},{48,136},{56,144... | collective-permute-start | bytes 331784 | tf_op jit(solution)/shard_map/ppermute | solution.py:39
  93.0 25.1 %collective-permute-start.18 = (bf16[144,384]{1,0:T(8,128)(2,1)}, bf16[144,384]{1,0:T(8,128)(2,1)S(1)}, u32[]{:S(2)}, u32[]{:S(2)}) collective-permute-start(bf16[144,384]{1,0:T(8,128)(2,1)} %maximum_maximum_fusion.1), channel_id=1, source_target_pairs={{0,96},{8,104},{16,112},{24,120},{32,128},{40,136},{48,144},{56,15... | collective-permute-start | bytes 331784 | tf_op jit(solution)/shard_map/ppermute | solution.py:39
  95.2 50.3 %collective-permute-start.19 = (bf16[144,384]{1,0:T(8,128)(2,1)}, bf16[144,384]{1,0:T(8,128)(2,1)S(1)}, u32[]{:S(2)}, u32[]{:S(2)}) collective-permute-start(bf16[144,384]{1,0:T(8,128)(2,1)} %maximum_maximum_fusion.1), channel_id=1, source_target_pairs={{0,104},{8,112},{16,120},{24,128},{32,136},{40,144},{48,152},{56,1... | collective-permute-start | bytes 331784 | tf_op jit(solution)/shard_map/ppermute | solution.py:39
  115.7 36.4 %collective-permute-start.20 = (bf16[144,384]{1,0:T(8,128)(2,1)}, bf16[144,384]{1,0:T(8,128)(2,1)S(1)}, u32[]{:S(2)}, u32[]{:S(2)}) collective-permute-start(bf16[144,384]{1,0:T(8,128)(2,1)} %maximum_maximum_fusion.1), channel_id=1, source_target_pairs={{0,112},{8,120},{16,128},{24,136},{32,144},{40,152},{48,160},{56,1... | collective-permute-start | bytes 331784 | tf_op jit(solution)/shard_map/ppermute | solution.py:39
  116.4 43.5 %collective-permute-start.21 = (bf16[144,384]{1,0:T(8,128)(2,1)}, bf16[144,384]{1,0:T(8,128)(2,1)S(1)}, u32[]{:S(2)}, u32[]{:S(2)}) collective-permute-start(bf16[144,384]{1,0:T(8,128)(2,1)} %maximum_maximum_fusion.1), channel_id=1, source_target_pairs={{0,120},{8,128},{16,136},{24,144},{32,152},{40,160},{48,168},{56,1... | collective-permute-start | bytes 331784 | tf_op jit(solution)/shard_map/ppermute | solution.py:39
  117.0 43.8 %collective-permute-start.22 = (bf16[144,384]{1,0:T(8,128)(2,1)}, bf16[144,384]{1,0:T(8,128)(2,1)S(1)}, u32[]{:S(2)}, u32[]{:S(2)}) collective-permute-start(bf16[144,384]{1,0:T(8,128)(2,1)} %maximum_maximum_fusion.1), channel_id=1, source_target_pairs={{0,128},{8,136},{16,144},{24,152},{32,160},{40,168},{48,176},{56,1... | collective-permute-start | bytes 331784 | tf_op jit(solution)/shard_map/ppermute | solution.py:39
  118.2 46.5 %collective-permute-start.23 = (bf16[144,384]{1,0:T(8,128)(2,1)}, bf16[144,384]{1,0:T(8,128)(2,1)S(1)}, u32[]{:S(2)}, u32[]{:S(2)}) collective-permute-start(bf16[144,384]{1,0:T(8,128)(2,1)} %maximum_maximum_fusion.1), channel_id=1, source_target_pairs={{0,136},{8,144},{16,152},{24,160},{32,168},{40,176},{48,184},{56,1... | collective-permute-start | bytes 331784 | tf_op jit(solution)/shard_map/ppermute | solution.py:39
  145.5 26.4 %collective-permute-start.24 = (bf16[144,384]{1,0:T(8,128)(2,1)}, bf16[144,384]{1,0:T(8,128)(2,1)S(1)}, u32[]{:S(2)}, u32[]{:S(2)}) collective-permute-start(bf16[144,384]{1,0:T(8,128)(2,1)} %maximum_maximum_fusion.1), channel_id=1, source_target_pairs={{0,144},{8,152},{16,160},{24,168},{32,176},{40,184},{48,192},{56,2... | collective-permute-start | bytes 331784 | tf_op jit(solution)/shard_map/ppermute | solution.py:39
  152.1 33.2 %collective-permute-start.25 = (bf16[144,384]{1,0:T(8,128)(2,1)}, bf16[144,384]{1,0:T(8,128)(2,1)S(1)}, u32[]{:S(2)}, u32[]{:S(2)}) collective-permute-start(bf16[144,384]{1,0:T(8,128)(2,1)} %maximum_maximum_fusion.1), channel_id=1, source_target_pairs={{0,152},{8,160},{16,168},{24,176},{32,184},{40,192},{48,200},{56,2... | collective-permute-start | bytes 331784 | tf_op jit(solution)/shard_map/ppermute | solution.py:39
  159.9 29.0 %collective-permute-start.26 = (bf16[144,384]{1,0:T(8,128)(2,1)}, bf16[144,384]{1,0:T(8,128)(2,1)S(1)}, u32[]{:S(2)}, u32[]{:S(2)}) collective-permute-start(bf16[144,384]{1,0:T(8,128)(2,1)} %maximum_maximum_fusion.1), channel_id=1, source_target_pairs={{0,160},{8,168},{16,176},{24,184},{32,192},{40,200},{48,208},{56,2... | collective-permute-start | bytes 331784 | tf_op jit(solution)/shard_map/ppermute | solution.py:39
  160.8 35.7 %collective-permute-start.27 = (bf16[144,384]{1,0:T(8,128)(2,1)}, bf16[144,384]{1,0:T(8,128)(2,1)S(1)}, u32[]{:S(2)}, u32[]{:S(2)}) collective-permute-start(bf16[144,384]{1,0:T(8,128)(2,1)} %maximum_maximum_fusion.1), channel_id=1, source_target_pairs={{0,168},{8,176},{16,184},{24,192},{32,200},{40,208},{48,216},{56,2... | collective-permute-start | bytes 331784 | tf_op jit(solution)/shard_map/ppermute | solution.py:39
  164.7 36.5 %collective-permute-start.28 = (bf16[144,384]{1,0:T(8,128)(2,1)}, bf16[144,384]{1,0:T(8,128)(2,1)S(1)}, u32[]{:S(2)}, u32[]{:S(2)}) collective-permute-start(bf16[144,384]{1,0:T(8,128)(2,1)} %maximum_maximum_fusion.1), channel_id=1, source_target_pairs={{0,176},{8,184},{16,192},{24,200},{32,208},{40,216},{48,224},{56,2... | collective-permute-start | bytes 331784 | tf_op jit(solution)/shard_map/ppermute | solution.py:39
  171.9 29.9 %collective-permute-start.29 = (bf16[144,384]{1,0:T(8,128)(2,1)}, bf16[144,384]{1,0:T(8,128)(2,1)S(1)}, u32[]{:S(2)}, u32[]{:S(2)}) collective-permute-start(bf16[144,384]{1,0:T(8,128)(2,1)} %maximum_maximum_fusion.1), channel_id=1, source_target_pairs={{0,184},{8,192},{16,200},{24,208},{32,216},{40,224},{48,232},{56,2... | collective-permute-start | bytes 331784 | tf_op jit(solution)/shard_map/ppermute | solution.py:39
  196.5 21.1 %collective-permute-start.32 = (bf16[144,384]{1,0:T(8,128)(2,1)}, bf16[144,384]{1,0:T(8,128)(2,1)S(1)}, u32[]{:S(2)}, u32[]{:S(2)}) collective-permute-start(bf16[144,384]{1,0:T(8,128)(2,1)} %maximum_maximum_fusion.1), channel_id=1, source_target_pairs={{0,208},{8,216},{16,224},{24,232},{32,240},{40,248},{48,0},{56,8},... | collective-permute-start | bytes 331784 | tf_op jit(solution)/shard_map/ppermute | solution.py:39
  201.2 29.1 %collective-permute-start.33 = (bf16[144,384]{1,0:T(8,128)(2,1)}, bf16[144,384]{1,0:T(8,128)(2,1)S(1)}, u32[]{:S(2)}, u32[]{:S(2)}) collective-permute-start(bf16[144,384]{1,0:T(8,128)(2,1)} %maximum_maximum_fusion.1), channel_id=1, source_target_pairs={{0,216},{8,224},{16,232},{24,240},{32,248},{40,0},{48,8},{56,16},{... | collective-permute-start | bytes 331784 | tf_op jit(solution)/shard_map/ppermute | solution.py:39
  201.9 29.1 %collective-permute-start.34 = (bf16[144,384]{1,0:T(8,128)(2,1)}, bf16[144,384]{1,0:T(8,128)(2,1)S(1)}, u32[]{:S(2)}, u32[]{:S(2)}) collective-permute-start(bf16[144,384]{1,0:T(8,128)(2,1)} %maximum_maximum_fusion.1), channel_id=1, source_target_pairs={{0,224},{8,232},{16,240},{24,248},{32,0},{40,8},{48,16},{56,24},{6... | collective-permute-start | bytes 331784 | tf_op jit(solution)/shard_map/ppermute | solution.py:39
  202.5 29.1 %collective-permute-start.35 = (bf16[144,384]{1,0:T(8,128)(2,1)}, bf16[144,384]{1,0:T(8,128)(2,1)S(1)}, u32[]{:S(2)}, u32[]{:S(2)}) collective-permute-start(bf16[144,384]{1,0:T(8,128)(2,1)} %maximum_maximum_fusion.1), channel_id=1, source_target_pairs={{0,232},{8,240},{16,248},{24,0},{32,8},{40,16},{48,24},{56,32},{64... | collective-permute-start | bytes 331784 | tf_op jit(solution)/shard_map/ppermute | solution.py:39
  204.8 27.4 %collective-permute-start.36 = (bf16[144,384]{1,0:T(8,128)(2,1)}, bf16[144,384]{1,0:T(8,128)(2,1)S(1)}, u32[]{:S(2)}, u32[]{:S(2)}) collective-permute-start(bf16[144,384]{1,0:T(8,128)(2,1)} %maximum_maximum_fusion.1), channel_id=1, source_target_pairs={{0,240},{8,248},{16,0},{24,8},{32,16},{40,24},{48,32},{56,40},{64,... | collective-permute-start | bytes 331784 | tf_op jit(solution)/shard_map/ppermute | solution.py:39
  284.4 21.8 %collective-permute-start.44 = (bf16[144,384]{1,0:T(8,128)(2,1)S(1)}, bf16[144,384]{1,0:T(8,128)(2,1)S(1)}, u32[]{:S(2)}, u32[]{:S(2)}) collective-permute-start(bf16[144,384]{1,0:T(8,128)(2,1)S(1)} %get-tuple-element.34), channel_id=1, source_target_pairs={{0,56},{8,64},{16,72},{24,80},{32,88},{40,96},{48,104},{56,112},{6... | collective-permute-start | bytes 331784 | tf_op jit(solution)/shard_map/ppermute | solution.py:39
  287.9 23.2 %collective-permute-start.45 = (bf16[144,384]{1,0:T(8,128)(2,1)S(1)}, bf16[144,384]{1,0:T(8,128)(2,1)S(1)}, u32[]{:S(2)}, u32[]{:S(2)}) collective-permute-start(bf16[144,384]{1,0:T(8,128)(2,1)S(1)} %get-tuple-element.33), channel_id=1, source_target_pairs={{0,64},{8,72},{16,80},{24,88},{32,96},{40,104},{48,112},{56,120},{... | collective-permute-start | bytes 331784 | tf_op jit(solution)/shard_map/ppermute | solution.py:39
  290.2 21.6 %collective-permute-start.46 = (bf16[144,384]{1,0:T(8,128)(2,1)S(1)}, bf16[144,384]{1,0:T(8,128)(2,1)S(1)}, u32[]{:S(2)}, u32[]{:S(2)}) collective-permute-start(bf16[144,384]{1,0:T(8,128)(2,1)S(1)} %get-tuple-element.32), channel_id=1, source_target_pairs={{0,72},{8,80},{16,88},{24,96},{32,104},{40,112},{48,120},{56,128},... | collective-permute-start | bytes 331784 | tf_op jit(solution)/shard_map/ppermute | solution.py:39
  294.9 23.1 %collective-permute-start.47 = (bf16[144,384]{1,0:T(8,128)(2,1)S(1)}, bf16[144,384]{1,0:T(8,128)(2,1)S(1)}, u32[]{:S(2)}, u32[]{:S(2)}) collective-permute-start(bf16[144,384]{1,0:T(8,128)(2,1)S(1)} %get-tuple-element.31), channel_id=1, source_target_pairs={{0,80},{8,88},{16,96},{24,104},{32,112},{40,120},{48,128},{56,136}... | collective-permute-start | bytes 331784 | tf_op jit(solution)/shard_map/ppermute | solution.py:39
  299.6 19.1 %collective-permute-start.48 = (bf16[144,384]{1,0:T(8,128)(2,1)S(1)}, bf16[144,384]{1,0:T(8,128)(2,1)S(1)}, u32[]{:S(2)}, u32[]{:S(2)}) collective-permute-start(bf16[144,384]{1,0:T(8,128)(2,1)S(1)} %get-tuple-element.30), channel_id=1, source_target_pairs={{0,88},{8,96},{16,104},{24,112},{32,120},{40,128},{48,136},{56,144... | collective-permute-start | bytes 331784 | tf_op jit(solution)/shard_map/ppermute | solution.py:39
  311.7 19.5 %collective-permute-start.51 = (bf16[144,384]{1,0:T(8,128)(2,1)S(1)}, bf16[144,384]{1,0:T(8,128)(2,1)S(1)}, u32[]{:S(2)}, u32[]{:S(2)}) collective-permute-start(bf16[144,384]{1,0:T(8,128)(2,1)S(1)} %get-tuple-element.27), channel_id=1, source_target_pairs={{0,112},{8,120},{16,128},{24,136},{32,144},{40,152},{48,160},{56,1... | collective-permute-start | bytes 331784 | tf_op jit(solution)/shard_map/ppermute | solution.py:39
  318.7 20.0 %collective-permute-start.53 = (bf16[144,384]{1,0:T(8,128)(2,1)S(1)}, bf16[144,384]{1,0:T(8,128)(2,1)S(1)}, u32[]{:S(2)}, u32[]{:S(2)}) collective-permute-start(bf16[144,384]{1,0:T(8,128)(2,1)S(1)} %get-tuple-element.25), channel_id=1, source_target_pairs={{0,128},{8,136},{16,144},{24,152},{32,160},{40,168},{48,176},{56,1... | collective-permute-start | bytes 331784 | tf_op jit(solution)/shard_map/ppermute | solution.py:39
  322.8 20.2 %collective-permute-start.54 = (bf16[144,384]{1,0:T(8,128)(2,1)S(1)}, bf16[144,384]{1,0:T(8,128)(2,1)S(1)}, u32[]{:S(2)}, u32[]{:S(2)}) collective-permute-start(bf16[144,384]{1,0:T(8,128)(2,1)S(1)} %get-tuple-element.24), channel_id=1, source_target_pairs={{0,136},{8,144},{16,152},{24,160},{32,168},{40,176},{48,184},{56,1... | collective-permute-start | bytes 331784 | tf_op jit(solution)/shard_map/ppermute | solution.py:39
  327.8 31.0 %collective-permute-start.55 = (bf16[144,384]{1,0:T(8,128)(2,1)S(1)}, bf16[144,384]{1,0:T(8,128)(2,1)S(1)}, u32[]{:S(2)}, u32[]{:S(2)}) collective-permute-start(bf16[144,384]{1,0:T(8,128)(2,1)S(1)} %get-tuple-element.23), channel_id=1, source_target_pairs={{0,144},{8,152},{16,160},{24,168},{32,176},{40,184},{48,192},{56,2... | collective-permute-start | bytes 331784 | tf_op jit(solution)/shard_map/ppermute | solution.py:39
  331.3 28.2 %collective-permute-start.56 = (bf16[144,384]{1,0:T(8,128)(2,1)S(1)}, bf16[144,384]{1,0:T(8,128)(2,1)S(1)}, u32[]{:S(2)}, u32[]{:S(2)}) collective-permute-start(bf16[144,384]{1,0:T(8,128)(2,1)S(1)} %get-tuple-element.22), channel_id=1, source_target_pairs={{0,152},{8,160},{16,168},{24,176},{32,184},{40,192},{48,200},{56,2... | collective-permute-start | bytes 331784 | tf_op jit(solution)/shard_map/ppermute | solution.py:39
  335.3 24.8 %collective-permute-start.57 = (bf16[144,384]{1,0:T(8,128)(2,1)S(1)}, bf16[144,384]{1,0:T(8,128)(2,1)S(1)}, u32[]{:S(2)}, u32[]{:S(2)}) collective-permute-start(bf16[144,384]{1,0:T(8,128)(2,1)S(1)} %get-tuple-element.21), channel_id=1, source_target_pairs={{0,160},{8,168},{16,176},{24,184},{32,192},{40,200},{48,208},{56,2... | collective-permute-start | bytes 331784 | tf_op jit(solution)/shard_map/ppermute | solution.py:39
  338.7 22.6 %collective-permute-start.58 = (bf16[144,384]{1,0:T(8,128)(2,1)S(1)}, bf16[144,384]{1,0:T(8,128)(2,1)S(1)}, u32[]{:S(2)}, u32[]{:S(2)}) collective-permute-start(bf16[144,384]{1,0:T(8,128)(2,1)S(1)} %get-tuple-element.20), channel_id=1, source_target_pairs={{0,168},{8,176},{16,184},{24,192},{32,200},{40,208},{48,216},{56,2... | collective-permute-start | bytes 331784 | tf_op jit(solution)/shard_map/ppermute | solution.py:39
  343.0 26.4 %collective-permute-start.59 = (bf16[144,384]{1,0:T(8,128)(2,1)S(1)}, bf16[144,384]{1,0:T(8,128)(2,1)S(1)}, u32[]{:S(2)}, u32[]{:S(2)}) collective-permute-start(bf16[144,384]{1,0:T(8,128)(2,1)S(1)} %get-tuple-element.19), channel_id=1, source_target_pairs={{0,176},{8,184},{16,192},{24,200},{32,208},{40,216},{48,224},{56,2... | collective-permute-start | bytes 331784 | tf_op jit(solution)/shard_map/ppermute | solution.py:39
  361.3 75.9 %collective-permute-start.63 = (bf16[144,384]{1,0:T(8,128)(2,1)S(1)}, bf16[144,384]{1,0:T(8,128)(2,1)S(1)}, u32[]{:S(2)}, u32[]{:S(2)}) collective-permute-start(bf16[144,384]{1,0:T(8,128)(2,1)S(1)} %get-tuple-element.15), channel_id=1, source_target_pairs={{0,208},{8,216},{16,224},{24,232},{32,240},{40,248},{48,0},{56,8},... | collective-permute-start | bytes 331784 | tf_op jit(solution)/shard_map/ppermute | solution.py:39
  369.5 80.2 %collective-permute-start.64 = (bf16[144,384]{1,0:T(8,128)(2,1)S(1)}, bf16[144,384]{1,0:T(8,128)(2,1)S(1)}, u32[]{:S(2)}, u32[]{:S(2)}) collective-permute-start(bf16[144,384]{1,0:T(8,128)(2,1)S(1)} %get-tuple-element.14), channel_id=1, source_target_pairs={{0,216},{8,224},{16,232},{24,240},{32,248},{40,0},{48,8},{56,16},{... | collective-permute-start | bytes 331784 | tf_op jit(solution)/shard_map/ppermute | solution.py:39
  371.0 79.3 %collective-permute-start.65 = (bf16[144,384]{1,0:T(8,128)(2,1)S(1)}, bf16[144,384]{1,0:T(8,128)(2,1)S(1)}, u32[]{:S(2)}, u32[]{:S(2)}) collective-permute-start(bf16[144,384]{1,0:T(8,128)(2,1)S(1)} %get-tuple-element.13), channel_id=1, source_target_pairs={{0,224},{8,232},{16,240},{24,248},{32,0},{40,8},{48,16},{56,24},{6... | collective-permute-start | bytes 331784 | tf_op jit(solution)/shard_map/ppermute | solution.py:39
  373.7 77.2 %collective-permute-start.66 = (bf16[144,384]{1,0:T(8,128)(2,1)S(1)}, bf16[144,384]{1,0:T(8,128)(2,1)S(1)}, u32[]{:S(2)}, u32[]{:S(2)}) collective-permute-start(bf16[144,384]{1,0:T(8,128)(2,1)S(1)} %get-tuple-element.12), channel_id=1, source_target_pairs={{0,232},{8,240},{16,248},{24,0},{32,8},{40,16},{48,24},{56,32},{64... | collective-permute-start | bytes 331784 | tf_op jit(solution)/shard_map/ppermute | solution.py:39
  378.9 72.7 %collective-permute-start.67 = (bf16[144,384]{1,0:T(8,128)(2,1)S(1)}, bf16[144,384]{1,0:T(8,128)(2,1)S(1)}, u32[]{:S(2)}, u32[]{:S(2)}) collective-permute-start(bf16[144,384]{1,0:T(8,128)(2,1)S(1)} %get-tuple-element.11), channel_id=1, source_target_pairs={{0,240},{8,248},{16,0},{24,8},{32,16},{40,24},{48,32},{56,40},{64,... | collective-permute-start | bytes 331784 | tf_op jit(solution)/shard_map/ppermute | solution.py:39
  (48 other events, 942.8 us)

commit v3 on v0

--- a/solution.py
+++ b/solution.py
@@ -9,6 +9,7 @@
 
 THETA = 1000000.0
 EPSILON = 1e-06
+ROWS = 144
 
 
 def rotate(heads, positions):
@@ -71,11 +72,17 @@
     kv_heads = k_weight.shape[1] // HD
     q_heads = q_weight.shape[1] // HD
     group = q_heads // kv_heads
-    full, gain = (
-        lax.all_gather(hidden_in, "tp", axis=1, tiled=True),
-        lax.all_gather(norm_gain, "tp", axis=0, tiled=True),
+    feat = hidden_in.shape[1]
+    n_tp = lax.axis_size("tp")
+    packed = jnp.concatenate(
+        [hidden_in, norm_gain[None, :], jnp.zeros((ROWS - length - 1, feat), hidden_in.dtype)],
+        axis=0,
     )
-    tokens = full.astype(jnp.float32)
+    spread = jnp.broadcast_to(packed[None], (n_tp,) + packed.shape)
+    pieces_in = lax.all_to_all(spread, "tp", 0, 0, tiled=True)
+    full = pieces_in.transpose(1, 0, 2).reshape(ROWS, n_tp * feat)
+    tokens = full[:length].astype(jnp.float32)
+    gain = full[length]
     meansq = jnp.mean(tokens * tokens, axis=-1, keepdims=True)
     normed = (tokens * lax.rsqrt(meansq + EPSILON) * gain.astype(jnp.float32)).astype(jnp.bfloat16)
     positions = prefix_len + jnp.arange(length, dtype=jnp.int32)
@@ -108,9 +115,8 @@
     peak, total, mixed = state
     context = (mixed / total[..., None]).astype(jnp.bfloat16).reshape(length, q_heads * HD)
     partial_value = jnp.dot(context, o_weight, preferred_element_type=jnp.float32)
-    summed = lax.psum_scatter(
-        partial_value.astype(jnp.bfloat16), "tp", scatter_dimension=1, tiled=True
-    ).astype(jnp.float32)
+    pieces_out = partial_value.astype(jnp.bfloat16).reshape(length, n_tp, feat).transpose(1, 0, 2)
+    summed = jnp.sum(lax.all_to_all(pieces_out, "tp", 0, 0, tiled=True).astype(jnp.float32), axis=0)
     valid = slot_index < suffix_len[0]
     return jnp.where(valid[:, None], summed, jnp.float32(0.0)).astype(jnp.bfloat16)
 

time: 278 us -> 221 us (0.79); the launches traced: 273 us -> 220 us
  waiting for transfers between devices: 172 us -> 119 us
  blocking collectives: 23.4 us -> 0 us
  starting transfers between devices: 0.12 us -> 17.2 us
  other arithmetic: 9.93 us -> 16 us
    all_to_all x0 -> x2, waiting for transfers between devices: none -> 44.5 us  [the longest x1 26.9 us: shards(): pieces_in = lax.all_to_all(spread, 'tp', 0, 0, tiled=True)]
    unnamed x4 -> x1, waiting for transfers between devices: 43.2 us -> 0.02 us
    all_gather x1, waiting for transfers between devices: 108 us -> 74.1 us  [shards(): everything = lax.all_gather(prefix_kv, 'req', axis=0, tiled=True)]
    all_gather x1 -> x0, blocking collectives: 23.4 us -> none  [shards(): lax.all_gather(norm_gain, 'tp', axis=0, tiled=True)]
    all_gather x1 -> x0, waiting for transfers between devices: 20.4 us -> none  [shards(): lax.all_gather(hidden_in, 'tp', axis=1, tiled=True)]
    all_to_all x0 -> x2, starting transfers between devices: none -> 17.2 us  [the longest x1 10.9 us: shards(): lax.all_to_all(pieces_out, 'tp', 0, 0, tiled=True).astype(jnp.float32)]
    convert_element_type x0 -> x2, other arithmetic: none -> 3.71 us  [the longest x1 2.19 us: shards(): (tokens * lax.rsqrt(meansq + EPSILON) * gain.astype(jnp.float32)).astype(...]
    unnamed x20 -> x21, local copies, waits for them, and re-layouts: 5.43 us -> 2.33 us
  transfers between devices with their start and end apart: 3 -> 3, of which waited for: 3 -> 3; matrix products, arithmetic and copies ran while one was open for 4% -> 8% of each run, Pallas kernels for 0% -> 0%
where the time goes in v3:
time: 221 us; the launch traced here: 220 us
  waiting for transfers between devices  119 us (54%)
  local copies, waits for them, and re-layouts  39.1 us (18%)
  starting transfers between devices  17.2 us (8%)
  other arithmetic  16 us (7%)
  between operations  15 us (7%)
  matrix products  13.7 us (6%)
    all_gather x1, waiting for transfers between devices, shards(): everything = lax.all_gather(prefix_kv, 'req', axis=0, tiled=True)  74.1 us
    all_to_all x1, waiting for transfers between devices, shards(): pieces_in = lax.all_to_all(spread, 'tp', 0, 0, tiled=True)  26.9 us
    all_to_all x1, waiting for transfers between devices, shards(): lax.all_to_all(pieces_out, 'tp', 0, 0, tiled=True).astype(jnp.float32)  17.5 us
    reshape x1, local copies, waits for them, and re-layouts, shards(): stacked = everything.reshape(devices, block, 2, kv_heads, HD)  13.8 us
    all_to_all x1, starting transfers between devices, shards(): lax.all_to_all(pieces_out, 'tp', 0, 0, tiled=True).astype(jnp.float32)  10.9 us
    gather x1, local copies, waits for them, and re-layouts, shards(): chosen = jnp.take(stacked, owners, axis=0)  8.78 us
    squeeze x8, local copies, waits for them, and re-layouts, shards(): state, unused = lax.scan(advance, state, chosen)  8.64 us
    all_to_all x1, starting transfers between devices, shards(): pieces_in = lax.all_to_all(spread, 'tp', 0, 0, tiled=True)  6.35 us
  transfers between devices with their start and end apart: 3, of which 3 were waited for; matrix products, arithmetic and copies ran while one was open for 8% of the time, Pallas kernels for 0%

profile of v3, /device:TPU:1, one launch (start us, length us, event | category | flops | bytes accessed | tf_op | source)
XLA Modules:
  0.0 219.9 jit_solution(15486559629320425801)
XLA Ops:
  6.5 2.0 copy.50
  8.8 1.2 broadcast_in_dim.45
  10.1 6.3 %all-to-all-start = ((bf16[8,144,640]{2,1,0:T(8,128)(2,1)}), bf16[8,144,640]{2,1,0:T(8,128)(2,1)S(1)}, u32[]{:S(2)}, u32[]{:S(2)}) async-start(bf16[8,144,640]{2,1,0:T(8,128)(2,1)} %broadcast_in_dim.45), calls=%async_computation | async-start | bytes 2949120 | tf_op jit(solution)/shard_map/all_to_all | solution.py:82
  17.3 0.3 multiply_cosine_fusion
  17.6 26.9 %all-to-all-done = bf16[8,144,640]{2,1,0:T(8,128)(2,1)S(1)} async-done(((bf16[8,144,640]{2,1,0:T(8,128)(2,1)}), bf16[8,144,640]{2,1,0:T(8,128)(2,1)S(1)}, u32[]{:S(2)}, u32[]{:S(2)}) %all-to-all-start) | async-done | bytes 1474592 | tf_op jit(solution)/shard_map/all_to_all | solution.py:82
  44.5 2.9 %copy.43 = bf16[8,144,640]{1,2,0:T(8,128)(2,1)} copy(bf16[8,144,640]{2,1,0:T(8,128)(2,1)S(1)} %all-to-all-done) | data formatting | bytes 2949120 | tf_op jit(solution)/shard_map/all_to_all | solution.py:82
  47.4 1.7 convert_reduce_fusion
  49.1 2.0 multiply_reduce_fusion
  51.2 1.5 slice_convert_fusion
  52.7 2.2 fusion.16
  54.9 0.9 convolution_add_fusion
  56.4 1.9 fusion.19
  58.5 0.3 fusion.45
  58.9 0.7 convolution_bitcast_fusion.1
  59.6 74.1 %all-gather.2.cloned.1.call-done = bf16[32768,2,128]{2,0,1:T(8,128)(2,1)} async-done(((bf16[1024,2,128]{2,0,1:T(8,128)(2,1)}), bf16[32768,2,128]{2,0,1:T(8,128)(2,1)}) %all-gather.2.cloned.1.call-update) | async-done | bytes 16777232 | tf_op jit(solution)/shard_map/all_gather | solution.py:110
  133.7 13.8 %copy.51 = bf16[32,1024,2,128]{3,1,2,0:T(8,128)(2,1)} copy(bf16[32,1024,2,128]{3,1,0,2:T(8,128)(2,1)} %bitcast.159) | data formatting | bytes 33554432 | tf_op jit(solution)/shard_map/reshape | solution.py:111
  147.5 8.8 %gather_fusion = bf16[8,1024,2,128]{3,1,2,0:T(8,128)(2,1)} fusion(bf16[32,1024,2,128]{3,1,2,0:T(8,128)(2,1)} %copy.51, s32[1024]{0:T(1024)S(1)} %pad_clamp_fusion), kind=kCustom, calls=%fused_computation | custom fusion | bytes 8388640 | tf_op jit(solution)/shard_map/jit(_take)/gather | solution.py:113
  156.3 4.6 %fusion.14 = bf16[8,1024,2,1,128]{4,1,2,3,0:T(8,128)(2,1)} fusion(bf16[8,1024,2,128]{3,1,2,0:T(8,128)(2,1)} %gather_fusion, pred[8]{0:T(512)(128)(4,1)S(1)} %get-tuple-element.72), kind=kLoop, calls=%fused_computation.27 | loop fusion | flops 2097152 | bytes 8388616 | tf_op jit(solution)/shard_map/while | solution.py:114
  160.9 18.0 %while.14 = (s32[]{:T(128)}, f32[128,1,3]{0,2,1:T(4,128)S(1)}, f32[128,1,3]{0,2,1:T(4,128)S(1)}, f32[128,1,3,128]{0,3,2,1:T(8,128)S(1)}, bf16[8,1024,2,1,128]{4,...) while((s32[]{:T(128)}, f32[128,1,3]{0,2,1:T(4,128)S(1)}, f32[128,1,3]{0,2,1:T(4,128)S(1)}, ...), condition=%wide.region_6.7_spmd, body=%wide.region_3.0_spmd.sunk | while | flops 203835264 | bytes 6813777 | solution.py:114
  160.9 1.1 dynamic-slice_bitcast_fusion.2
  161.9 0.4 bitcast_reduce_fusion.2
  162.6 0.5 fusion.63
  163.1 1.1 dynamic-slice_bitcast_fusion.2
  164.2 0.4 bitcast_reduce_fusion.2
  164.8 0.5 fusion.63
  165.3 1.1 dynamic-slice_bitcast_fusion.2
  166.4 0.4 bitcast_reduce_fusion.2
  167.1 0.5 fusion.63
  167.6 1.1 dynamic-slice_bitcast_fusion.2
  168.7 0.4 bitcast_reduce_fusion.2
  169.3 0.5 fusion.63
  169.8 1.1 dynamic-slice_bitcast_fusion.2
  170.9 0.4 bitcast_reduce_fusion.2
  171.6 0.5 fusion.63
  172.1 1.1 dynamic-slice_bitcast_fusion.2
  173.2 0.4 bitcast_reduce_fusion.2
  173.8 0.5 fusion.63
  174.3 1.1 dynamic-slice_bitcast_fusion.2
  175.4 0.4 bitcast_reduce_fusion.2
  176.1 0.5 fusion.63
  176.6 1.1 dynamic-slice_bitcast_fusion.2
  177.7 0.4 bitcast_reduce_fusion.2
  178.3 0.5 fusion.63
  178.9 3.0 %convolution_convert_fusion = bf16[128,5120]{1,0:T(8,128)(2,1)S(1)} fusion(bf16[128,384]{0,1:T(8,128)(2,1)S(1)} %bitcast.168, bf16[384,5120]{1,0:T(8,128)(2,1)} %param.23), kind=kOutput, calls=%fused_computation.25 | convolution fusion | flops 503971840 | bytes 5341184 | tf_op jit(solution)/shard_map/dot_general | solution.py:117
  181.9 1.2 copy.66
  183.1 10.9 %all-to-all-start.1 = ((bf16[8,128,640]{2,1,0:T(8,128)(2,1)}), bf16[8,128,640]{2,1,0:T(8,128)(2,1)S(1)}, u32[]{:S(2)}, u32[]{:S(2)}) async-start(bf16[8,128,640]{2,1,0:T(8,128)(2,1)} %bitcast.163), calls=%async_computation.1 | async-start | bytes 2621440 | tf_op jit(solution)/shard_map/all_to_all | solution.py:119
  194.6 17.5 %all-to-all-done.1 = bf16[8,128,640]{2,1,0:T(8,128)(2,1)S(1)} async-done(((bf16[8,128,640]{2,1,0:T(8,128)(2,1)}), bf16[8,128,640]{2,1,0:T(8,128)(2,1)S(1)}, u32[]{:S(2)}, u32[]{:S(2)}) %all-to-all-start.1) | async-done | bytes 1310752 | tf_op jit(solution)/shard_map/all_to_all | solution.py:119
  212.3 0.8 select_convert_fusion
  (77 shorter events, 3.4 us)
Async XLA Ops:
  6.5 52.3 %copy-start = (bf16[5120,128]{1,0:T(8,128)(2,1)S(1)}, bf16[5120,128]{1,0:T(8,128)(2,1)}, u32[]{:S(2)}) copy-start(bf16[5120,128]{1,0:T(8,128)(2,1)} %param.21) | copy-start | bytes 3932164
  6.5 2.1 copy-start.4
  6.5 2.2 copy-start.3
  6.5 127.2 %all-gather.2.cloned.1.call-start = ((), (), s32[]{:S(2)}) async-start(), calls=%async_computation.2 | async-start | bytes 17301504 | tf_op jit(solution)/shard_map/all_gather | solution.py:110
  10.1 6.4 %copy-start.5 = (bf16[384]{0:T(512)(128)(2,1)S(1)}, bf16[384]{0:T(512)(128)(2,1)}, u32[]{:S(2)}) copy-start(bf16[384]{0:T(512)(128)(2,1)} %param.18) | copy-start | bytes 2308
  10.1 6.4 %copy-start.7 = (bf16[128]{0:T(256)(128)(2,1)S(1)}, bf16[128]{0:T(256)(128)(2,1)}, u32[]{:S(2)}) copy-start(bf16[128]{0:T(256)(128)(2,1)} %param.20) | copy-start | bytes 772
  10.1 6.4 %copy-start.8 = (bf16[128]{0:T(256)(128)(2,1)S(1)}, bf16[128]{0:T(256)(128)(2,1)}, u32[]{:S(2)}) copy-start(bf16[128]{0:T(256)(128)(2,1)} %param.22) | copy-start | bytes 772
  10.1 7.1 %copy-start.6 = (s32[32]{0:T(128)S(1)}, s32[32]{0:T(128)}, u32[]{:S(2)}) copy-start(s32[32]{0:T(128)} %param.27) | copy-start | bytes 388
  10.1 34.5 %all-to-all-start = ((bf16[8,144,640]{2,1,0:T(8,128)(2,1)}), bf16[8,144,640]{2,1,0:T(8,128)(2,1)S(1)}, u32[]{:S(2)}, u32[]{:S(2)}) async-start(bf16[8,144,640]{2,1,0:T(8,128)(2,1)} %broadcast_in_dim.45), calls=%async_computation | async-start | bytes 2949120 | tf_op jit(solution)/shard_map/all_to_all | solution.py:82
  52.7 2.2 %copy-start.2 = (bf16[5120,384]{1,0:T(8,128)(2,1)S(1)}, bf16[5120,384]{1,0:T(8,128)(2,1)}, u32[]{:S(2)}) copy-start(bf16[5120,384]{1,0:T(8,128)(2,1)} %param.17) | copy-start | bytes 11796484
  183.1 30.0 %copy-start.1 = (bf16[5120,128]{1,0:T(8,128)(2,1)S(1)}, bf16[5120,128]{1,0:T(8,128)(2,1)}, u32[]{:S(2)}) copy-start(bf16[5120,128]{1,0:T(8,128)(2,1)} %param.21) | copy-start | bytes 3932164
  183.1 29.0 %all-to-all-start.1 = ((bf16[8,128,640]{2,1,0:T(8,128)(2,1)}), bf16[8,128,640]{2,1,0:T(8,128)(2,1)S(1)}, u32[]{:S(2)}, u32[]{:S(2)}) async-start(bf16[8,128,640]{2,1,0:T(8,128)(2,1)} %bitcast.163), calls=%async_computation.1 | async-start | bytes 2621440 | tf_op jit(solution)/shard_map/all_to_all | solution.py:119
Sparse Core Ops, SparseCore 0:
  10.0 123.7 all-gather.1

commit v4 on v3

--- a/solution.py
+++ b/solution.py
@@ -1,6 +1,8 @@
 import jax
 import jax.numpy as jnp
 from jax import lax
+from jax.experimental import pallas as pl
+from jax.experimental.pallas import tpu as pltpu
 from jax.sharding import PartitionSpec as P
 
 HD = 128
@@ -47,6 +49,77 @@
     total = first[1] * left + second[1] * right
     mixed = first[2] * left[..., None] + second[2] * right[..., None]
     return (peak, total, mixed)
+
+
+def prefix_kernel(own_ref, q_ref, k_ref, v_ref, m0_ref, l0_ref, a0_ref, o_ref, m_sc, l_sc, acc_sc):
+    step = pl.program_id(0)
+    group = q_ref.shape[1] // HD
+
+    @pl.when(step == 0)
+    def _():
+        m_sc[...] = m0_ref[...]
+        l_sc[...] = l0_ref[...]
+        acc_sc[...] = a0_ref[...]
+
+    q = q_ref[...]
+    stacked = jnp.concatenate([q[:, h * HD:(h + 1) * HD] for h in range(group)], axis=0)
+    keys = k_ref[0]
+    values = v_ref[0]
+    scores = lax.dot_general(
+        stacked, keys, (((1,), (1,)), ((), ())), preferred_element_type=jnp.float32
+    ) * HD ** (-0.5)
+    old = m_sc[...]
+    new = jnp.maximum(old, jnp.max(scores, axis=-1, keepdims=True))
+    alpha = jnp.exp(old - new)
+    weights = jnp.exp(scores - new)
+    l_sc[...] = alpha * l_sc[...] + jnp.sum(weights, axis=-1, keepdims=True)
+    acc_sc[...] = alpha * acc_sc[...] + jnp.dot(
+        weights.astype(jnp.bfloat16), values, preferred_element_type=jnp.float32
+    )
+    m_sc[...] = new
+
+    @pl.when(step == pl.num_programs(0) - 1)
+    def _():
+        context = acc_sc[...] / l_sc[...]
+        rows = q_ref.shape[0]
+        for h in range(group):
+            o_ref[:, h * HD:(h + 1) * HD] = context[h * rows:(h + 1) * rows].astype(o_ref.dtype)
+
+
+def prefix_attention(owners, flat_q, kv, peak0, total0, mixed0):
+    length, width = flat_q.shape
+    steps = owners.shape[0]
+    block = kv.shape[1]
+    rows = peak0.shape[0]
+    cost = pl.CostEstimate(
+        flops=4 * rows * block * HD * steps,
+        transcendentals=rows * block * steps,
+        bytes_accessed=2 * steps * block * HD * 2 + length * width * 4 + rows * HD * 4,
+    )
+    return pl.pallas_call(
+        prefix_kernel,
+        out_shape=jax.ShapeDtypeStruct((length, width), jnp.bfloat16),
+        grid_spec=pltpu.PrefetchScalarGridSpec(
+            num_scalar_prefetch=1,
+            grid=(steps,),
+            in_specs=[
+                pl.BlockSpec((length, width), lambda j, own: (0, 0)),
+                pl.BlockSpec((1, block, HD), lambda j, own: (own[j], 0, 0)),
+                pl.BlockSpec((1, block, HD), lambda j, own: (own[j], 0, 1)),
+                pl.BlockSpec((rows, 1), lambda j, own: (0, 0)),
+                pl.BlockSpec((rows, 1), lambda j, own: (0, 0)),
+                pl.BlockSpec((rows, HD), lambda j, own: (0, 0)),
+            ],
+            out_specs=pl.BlockSpec((length, width), lambda j, own: (0, 0)),
+            scratch_shapes=[
+                pltpu.VMEM((rows, 1), jnp.float32),
+                pltpu.VMEM((rows, 1), jnp.float32),
+                pltpu.VMEM((rows, HD), jnp.float32),
+            ],
+        ),
+        compiler_params=pltpu.CompilerParams(dimension_semantics=("arbitrary",)),
+        cost_estimate=cost,
+    )(owners, flat_q, kv, kv, peak0, total0, mixed0)
 
 
 def shards(
@@ -101,19 +174,19 @@
     values = values.astype(jnp.bfloat16).reshape(length, kv_heads, HD)
     slot_index = jnp.arange(length, dtype=jnp.int32)
     causal = slot_index[None, :] <= slot_index[:, None]
-    state = block_stats(queries, keys, values, causal)
+    peak, total, mixed = block_stats(queries, keys, values, causal)
+    rows = length * q_heads
+    peak0 = peak.reshape(length, q_heads).T.reshape(rows, 1)
+    total0 = total.reshape(length, q_heads).T.reshape(rows, 1)
+    mixed0 = mixed.reshape(length, q_heads, HD).transpose(1, 0, 2).reshape(rows, HD)
     which = req_prefix[0]
-
-    def advance(current, cached):
-        return (combine(current, block_stats(queries, cached[:, 0], cached[:, 1], None)), None)
-
-    everything = lax.all_gather(prefix_kv, "req", axis=0, tiled=True)
-    stacked = everything.reshape(devices, block, 2, kv_heads, HD)
+    rowwise = prefix_kv.reshape(block, 2 * kv_heads * HD)
+    gathered = lax.all_gather(rowwise, "req", axis=0, tiled=True)
+    stacked = gathered.reshape(devices, block, 2 * kv_heads * HD)
     owners = lax.dynamic_slice_in_dim(block_owner, which * owned, owned)
-    chosen = jnp.take(stacked, owners, axis=0)
-    state, unused = lax.scan(advance, state, chosen)
-    peak, total, mixed = state
-    context = (mixed / total[..., None]).astype(jnp.bfloat16).reshape(length, q_heads * HD)
+    context = prefix_attention(
+        owners, queries.reshape(length, q_heads * HD), stacked, peak0, total0, mixed0
+    )
     partial_value = jnp.dot(context, o_weight, preferred_element_type=jnp.float32)
     pieces_out = partial_value.astype(jnp.bfloat16).reshape(length, n_tp, feat).transpose(1, 0, 2)
     summed = jnp.sum(lax.all_to_all(pieces_out, "tp", 0, 0, tiled=True).astype(jnp.float32), axis=0)

time: 221 us -> 186 us (0.84)
  local copies, waits for them, and re-layouts: 39.1 us -> 11 us
  Pallas kernels: 0 us -> 11.5 us
  other arithmetic: 16 us -> 9.26 us
  matrix products: 13.7 us -> 7.41 us
  waiting for transfers between devices: 119 us -> 115 us
    reshape x1 -> x0, local copies, waits for them, and re-layouts: 13.8 us -> none  [shards(): stacked = everything.reshape(devices, block, 2, kv_heads, HD)]
    pallas_call x0 -> x1, Pallas kernels: none -> 11.5 us  [prefix_attention(): pl.pallas_call(prefix_kernel, out_shape=jax.ShapeDtypeStruct((length, wid...]
    gather x1 -> x0, local copies, waits for them, and re-layouts: 8.78 us -> none  [shards(): chosen = jnp.take(stacked, owners, axis=0)]
    squeeze x8 -> x0, local copies, waits for them, and re-layouts: 8.64 us -> none  [shards(): state, unused = lax.scan(advance, state, chosen)]
    while x1 -> x0, other arithmetic: 4.58 us -> none  [shards(): state, unused = lax.scan(advance, state, chosen)]
    all_gather x1, waiting for transfers between devices: 74.1 us -> 70.8 us  [shards(): gathered = lax.all_gather(rowwise, 'req', axis=0, tiled=True)]
    dot_general x9 -> x1, matrix products: 4.59 us -> 1.38 us  [block_stats(): jnp.einsum('sghk,kgd->sghd', weights.astype(jnp.bfloat16), values, prefer...]
    dot_general x9 -> x1, matrix products: 3.36 us -> 0.23 us  [block_stats(): jnp.einsum('sghd,kgd->sghk', grouped, keys, preferred_element_type=jnp.fl...]
  transfers between devices with their start and end apart: 3 -> 3, of which waited for: 3 -> 3; matrix products, arithmetic and copies ran while one was open for 8% -> 11% of each run, Pallas kernels for 0% -> 0%
where the time goes in v4:
time: 186 us
  waiting for transfers between devices  115 us (62%)
  starting transfers between devices  16.9 us (9%)
  between operations  14.9 us (8%)
  Pallas kernels  11.5 us (6%)
  local copies, waits for them, and re-layouts  11 us (6%)
  other arithmetic  9.26 us (5%)
  matrix products  7.41 us (4%)
    all_gather x1, waiting for transfers between devices, shards(): gathered = lax.all_gather(rowwise, 'req', axis=0, tiled=True)  70.8 us
    all_to_all x1, waiting for transfers between devices, shards(): pieces_in = lax.all_to_all(spread, 'tp', 0, 0, tiled=True)  26.5 us
    all_to_all x1, waiting for transfers between devices, shards(): lax.all_to_all(pieces_out, 'tp', 0, 0, tiled=True).astype(jnp.float32)  17.5 us
    pallas_call x1, Pallas kernels, prefix_attention(): pl.pallas_call(prefix_kernel, out_shape=jax.ShapeDtypeStruct((length, wid...  11.5 us
    all_to_all x1, starting transfers between devices, shards(): lax.all_to_all(pieces_out, 'tp', 0, 0, tiled=True).astype(jnp.float32)  10.6 us
    all_to_all x1, starting transfers between devices, shards(): pieces_in = lax.all_to_all(spread, 'tp', 0, 0, tiled=True)  6.35 us
    unnamed x23, local copies, waits for them, and re-layouts  3.99 us
  transfers between devices with their start and end apart: 3, of which 3 were waited for; matrix products, arithmetic and copies ran while one was open for 11% of the time, Pallas kernels for 0%

profile of v4, /device:TPU:1, one launch (start us, length us, event | category | flops | bytes accessed | tf_op | source)
XLA Modules:
  0.0 185.8 jit_solution(1101252422348355369)
XLA Ops:
  6.5 0.0 copy-start
  6.5 0.0 all-gather.2.cloned.1.call-start
  6.5 2.0 %copy.66 = bf16[128,8,2,128]{3,1,2,0:T(8,128)(2,1)} copy(bf16[128,8,2,128]{3,2,1,0:T(2,128)(2,1)} %bitcast.92) | data formatting | bytes 1048576
  8.6 0.0 all-gather.2.cloned.1.call-update
  8.6 0.0 copy-done.3
  8.6 0.1 pad.6.clone
  8.7 0.0 copy-done.2
  8.7 0.1 maximum_maximum_fusion
  8.8 1.2 broadcast_in_dim.25
  10.1 6.3 %all-to-all-start = ((bf16[8,144,640]{2,1,0:T(8,128)(2,1)}), bf16[8,144,640]{2,1,0:T(8,128)(2,1)S(1)}, u32[]{:S(2)}, u32[]{:S(2)}) async-start(bf16[8,144,640]{2,1,0:T(8,128)(2,1)} %broadcast_in_dim.25), calls=%async_computation | async-start | bytes 2949120 | tf_op jit(solution)/shard_map/all_to_all | solution.py:155
  16.4 0.0 copy-done.4
  16.4 0.0 copy-done.5
  16.5 0.0 copy-done.6
  17.1 0.0 copy-done.7
  17.2 0.6 dynamic_slice.3.own_ref
  17.8 0.3 multiply_cosine_fusion
  18.1 26.5 %all-to-all-done = bf16[8,144,640]{2,1,0:T(8,128)(2,1)S(1)} async-done(((bf16[8,144,640]{2,1,0:T(8,128)(2,1)}), bf16[8,144,640]{2,1,0:T(8,128)(2,1)S(1)}, u32[]{:S(2)}, u32[]{:S(2)}) %all-to-all-start) | async-done | bytes 1474592 | tf_op jit(solution)/shard_map/all_to_all | solution.py:155
  44.6 2.9 %copy.39 = bf16[8,144,640]{1,2,0:T(8,128)(2,1)} copy(bf16[8,144,640]{2,1,0:T(8,128)(2,1)S(1)} %all-to-all-done) | data formatting | bytes 2949120 | tf_op jit(solution)/shard_map/all_to_all | solution.py:155
  47.5 1.7 convert_reduce_fusion
  49.2 2.0 %multiply_reduce_fusion = f32[128]{0:T(128)S(1)} fusion(bf16[144,8,640]{0,2,1:T(8,128)(2,1)} %bitcast.83), kind=kLoop, calls=%fused_computation.6 | loop fusion | flops 1965952 | bytes 1311232 | tf_op jit(solution)/shard_map/reduce_sum | solution.py:159
  51.2 1.5 slice_convert_fusion
  52.8 0.0 copy-start.1
  52.8 2.2 %fusion.1 = bf16[128,5120]{0,1:T(8,128)(2,1)S(1)} fusion(f32[128,8,640]{0,2,1:T(8,128)S(1)} %slice_convert_fusion, f32[5120]{0:T(1024)S(1)} %reshape.231, f32[128]{0:T(128)S(1)} %add_rsqrt_fusion), kind=kLoop, calls=%fused_computation.3 | loop fusion | flops 1966080 | bytes 3953152 | tf_op jit(solution)/shard_map/convert_element_type | solution.py:160
  55.0 0.0 copy-done.1
  55.0 0.9 convolution_add_fusion
  55.9 0.1 copy.40
  56.1 0.1 copy.53
  56.2 0.1 copy.54
  56.3 0.1 multiply_subtract_fusion
  56.4 0.1 maximum_convert_fusion
  56.5 0.1 copy.43
  56.6 1.9 %fusion.4 = f32[128,1,128]{0,2,1:T(8,128)S(1)} fusion(bf16[128,5120]{0,1:T(8,128)(2,1)S(1)} %fusion.1, bf16[5120,128]{1,0:T(8,128)(2,1)} %param.17, f32[128]{0:T(128)S(1)} %convert_element_type.91), kind=kOutput, calls=%fused_computation.15 | convolution fusion | flops 167788544 | bytes 2687488 | tf_op jit(solution)/shard_map/dot_general | solution.py:167
  58.5 0.2 fusion.25
  58.7 0.2 fusion.28
  58.9 0.1 fusion.9
  59.0 0.8 copy.60
  59.8 0.8 copy.58
  60.7 0.8 copy.46.q_ref
  61.4 0.0 copy-done
  61.4 1.4 fusion.7
  62.8 70.8 %all-gather.2.cloned.1.call-done = bf16[32768,256]{1,0:T(8,128)(2,1)} async-done(((bf16[1024,256]{1,0:T(8,128)(2,1)}), bf16[32768,256]{1,0:T(8,128)(2,1)}) %all-gather.2.cloned.1.call-update) | async-done | bytes 16777232 | tf_op jit(solution)/shard_map/all_gather | solution.py:184
  133.6 11.5 %shard_map.127 = bf16[128,384]{1,0:T(8,128)(2,1)} custom-call(s32[8]{0:T(128)} %dynamic_slice.3.own_ref, bf16[128,384]{1,0:T(8,128)(2,1)} %copy.46.q_ref, bf16[32,1024,256]{2,1,0:T(8,128)(2,1)} %bitcast.80, bf16[32,1024,256]{2,1,0:T(8,128)(2,1)} %bitcast.81, f32[384,1]{1,0:T(8,128)} %bitcast.90, f32[384,1]{1,0:T(8,128)} %bitcast.89, f32[384,128]{1,0:T(8,128)} %bitcast.88), custom_call_target="tpu_custom_call" | custom-call | flops 1610612736 | bytes 4587520 | tf_op jit(solution)/shard_map/pallas_call | solution.py:99
  145.1 3.0 %convolution_convert_fusion = bf16[128,5120]{1,0:T(8,128)(2,1)S(1)} fusion(bf16[128,384]{1,0:T(8,128)(2,1)} %shard_map.127, bf16[384,5120]{1,0:T(8,128)(2,1)} %param.21), kind=kOutput, calls=%fused_computation | convolution fusion | flops 503971840 | bytes 5341184 | tf_op jit(solution)/shard_map/dot_general | solution.py:190
  148.1 1.2 copy.65
  149.3 10.6 %all-to-all-start.1 = ((bf16[8,128,640]{2,1,0:T(8,128)(2,1)}), bf16[8,128,640]{2,1,0:T(8,128)(2,1)S(1)}, u32[]{:S(2)}, u32[]{:S(2)}) async-start(bf16[8,128,640]{2,1,0:T(8,128)(2,1)} %bitcast.85), calls=%async_computation.1 | async-start | bytes 2621440 | tf_op jit(solution)/shard_map/all_to_all | solution.py:192
  160.5 17.5 %all-to-all-done.1 = bf16[8,128,640]{2,1,0:T(8,128)(2,1)S(1)} async-done(((bf16[8,128,640]{2,1,0:T(8,128)(2,1)}), bf16[8,128,640]{2,1,0:T(8,128)(2,1)S(1)}, u32[]{:S(2)}, u32[]{:S(2)}) %all-to-all-start.1) | async-done | bytes 1310752 | tf_op jit(solution)/shard_map/all_to_all | solution.py:192
  178.0 0.2 convert_reduce_fusion.1
  178.2 0.8 select_convert_fusion
  (20 shorter events, 0.1 us)
Async XLA Ops:
  6.5 54.9 %copy-start = (bf16[5120,128]{1,0:T(8,128)(2,1)S(1)}, bf16[5120,128]{1,0:T(8,128)(2,1)}, u32[]{:S(2)}) copy-start(bf16[5120,128]{1,0:T(8,128)(2,1)} %param.19) | copy-start | bytes 3932164
  6.5 2.1 %copy-start.3 = (bf16[640]{0:T(1024)(128)(2,1)S(1)}, bf16[640]{0:T(1024)(128)(2,1)}, u32[]{:S(2)}) copy-start(bf16[640]{0:T(1024)(128)(2,1)} %param.14) | copy-start | bytes 3844
  6.5 2.2 %copy-start.2 = (bf16[128,640]{1,0:T(8,128)(2,1)S(1)}, bf16[128,640]{1,0:T(8,128)(2,1)}, u32[]{:S(2)}) copy-start(bf16[128,640]{1,0:T(8,128)(2,1)} %param.13) | copy-start | bytes 491524
  6.5 127.1 %all-gather.2.cloned.1.call-start = ((), (), s32[]{:S(2)}) async-start(), calls=%async_computation.2 | async-start | bytes 17301504 | tf_op jit(solution)/shard_map/all_gather | solution.py:184
  10.1 6.4 %copy-start.4 = (bf16[384]{0:T(512)(128)(2,1)S(1)}, bf16[384]{0:T(512)(128)(2,1)}, u32[]{:S(2)}) copy-start(bf16[384]{0:T(512)(128)(2,1)} %param.16) | copy-start | bytes 2308
  10.1 6.4 %copy-start.5 = (bf16[128]{0:T(256)(128)(2,1)S(1)}, bf16[128]{0:T(256)(128)(2,1)}, u32[]{:S(2)}) copy-start(bf16[128]{0:T(256)(128)(2,1)} %param.18) | copy-start | bytes 772
  10.1 6.4 %copy-start.6 = (bf16[128]{0:T(256)(128)(2,1)S(1)}, bf16[128]{0:T(256)(128)(2,1)}, u32[]{:S(2)}) copy-start(bf16[128]{0:T(256)(128)(2,1)} %param.20) | copy-start | bytes 772
  10.1 7.1 %copy-start.7 = (s32[32]{0:T(128)S(1)}, s32[32]{0:T(128)}, u32[]{:S(2)}) copy-start(s32[32]{0:T(128)} %param.25) | copy-start | bytes 388
  10.1 34.5 %all-to-all-start = ((bf16[8,144,640]{2,1,0:T(8,128)(2,1)}), bf16[8,144,640]{2,1,0:T(8,128)(2,1)S(1)}, u32[]{:S(2)}, u32[]{:S(2)}) async-start(bf16[8,144,640]{2,1,0:T(8,128)(2,1)} %broadcast_in_dim.25), calls=%async_computation | async-start | bytes 2949120 | tf_op jit(solution)/shard_map/all_to_all | solution.py:155
  52.8 2.2 %copy-start.1 = (bf16[5120,384]{1,0:T(8,128)(2,1)S(1)}, bf16[5120,384]{1,0:T(8,128)(2,1)}, u32[]{:S(2)}) copy-start(bf16[5120,384]{1,0:T(8,128)(2,1)} %param.15) | copy-start | bytes 11796484
  149.3 28.7 %all-to-all-start.1 = ((bf16[8,128,640]{2,1,0:T(8,128)(2,1)}), bf16[8,128,640]{2,1,0:T(8,128)(2,1)S(1)}, u32[]{:S(2)}, u32[]{:S(2)}) async-start(bf16[8,128,640]{2,1,0:T(8,128)(2,1)} %bitcast.85), calls=%async_computation.1 | async-start | bytes 2621440 | tf_op jit(solution)/shard_map/all_to_all | solution.py:192
Sparse Core Ops, SparseCore 0:
  9.9 123.6 all-gather.1

commit v5 on v4

--- a/solution.py
+++ b/solution.py
@@ -51,7 +51,10 @@
     return (peak, total, mixed)
 
 
-def prefix_kernel(own_ref, q_ref, k_ref, v_ref, m0_ref, l0_ref, a0_ref, o_ref, m_sc, l_sc, acc_sc):
+def prefix_kernel(
+    local_ref, use_ref, q_ref, ka_ref, va_ref, kb_ref, vb_ref, m0_ref, l0_ref, a0_ref,
+    o_ref, m_sc, l_sc, acc_sc,
+):
     step = pl.program_id(0)
     group = q_ref.shape[1] // HD
 
@@ -63,8 +66,9 @@
 
     q = q_ref[...]
     stacked = jnp.concatenate([q[:, h * HD:(h + 1) * HD] for h in range(group)], axis=0)
-    keys = k_ref[0]
-    values = v_ref[0]
+    here = use_ref[step] == 1
+    keys = jnp.where(here, ka_ref[0], kb_ref[0])
+    values = jnp.where(here, va_ref[0], vb_ref[0])
     scores = lax.dot_general(
         stacked, keys, (((1,), (1,)), ((), ())), preferred_element_type=jnp.float32
     ) * HD ** (-0.5)
@@ -86,31 +90,33 @@
             o_ref[:, h * HD:(h + 1) * HD] = context[h * rows:(h + 1) * rows].astype(o_ref.dtype)
 
 
-def prefix_attention(owners, flat_q, kv, peak0, total0, mixed0):
+def prefix_attention(local, use, flat_q, mine, received, peak0, total0, mixed0):
     length, width = flat_q.shape
-    steps = owners.shape[0]
-    block = kv.shape[1]
+    steps = local.shape[0]
+    block = mine.shape[1]
     rows = peak0.shape[0]
     cost = pl.CostEstimate(
         flops=4 * rows * block * HD * steps,
         transcendentals=rows * block * steps,
-        bytes_accessed=2 * steps * block * HD * 2 + length * width * 4 + rows * HD * 4,
+        bytes_accessed=4 * steps * block * HD * 2 + length * width * 4 + rows * HD * 4,
     )
     return pl.pallas_call(
         prefix_kernel,
         out_shape=jax.ShapeDtypeStruct((length, width), jnp.bfloat16),
         grid_spec=pltpu.PrefetchScalarGridSpec(
-            num_scalar_prefetch=1,
+            num_scalar_prefetch=2,
             grid=(steps,),
             in_specs=[
-                pl.BlockSpec((length, width), lambda j, own: (0, 0)),
-                pl.BlockSpec((1, block, HD), lambda j, own: (own[j], 0, 0)),
-                pl.BlockSpec((1, block, HD), lambda j, own: (own[j], 0, 1)),
-                pl.BlockSpec((rows, 1), lambda j, own: (0, 0)),
-                pl.BlockSpec((rows, 1), lambda j, own: (0, 0)),
-                pl.BlockSpec((rows, HD), lambda j, own: (0, 0)),
+                pl.BlockSpec((length, width), lambda j, loc, use: (0, 0)),
+                pl.BlockSpec((1, block, HD), lambda j, loc, use: (loc[j], 0, 0)),
+                pl.BlockSpec((1, block, HD), lambda j, loc, use: (loc[j], 0, 1)),
+                pl.BlockSpec((1, block, HD), lambda j, loc, use: (j, 0, 0)),
+                pl.BlockSpec((1, block, HD), lambda j, loc, use: (j, 0, 1)),
+                pl.BlockSpec((rows, 1), lambda j, loc, use: (0, 0)),
+                pl.BlockSpec((rows, 1), lambda j, loc, use: (0, 0)),
+                pl.BlockSpec((rows, HD), lambda j, loc, use: (0, 0)),
             ],
-            out_specs=pl.BlockSpec((length, width), lambda j, own: (0, 0)),
+            out_specs=pl.BlockSpec((length, width), lambda j, loc, use: (0, 0)),
             scratch_shapes=[
                 pltpu.VMEM((rows, 1), jnp.float32),
                 pltpu.VMEM((rows, 1), jnp.float32),
@@ -119,7 +125,7 @@
         ),
         compiler_params=pltpu.CompilerParams(dimension_semantics=("arbitrary",)),
         cost_estimate=cost,
-    )(owners, flat_q, kv, kv, peak0, total0, mixed0)
+    )(local, use, flat_q, mine, mine, received, received, peak0, total0, mixed0)
 
 
 def shards(
@@ -180,12 +186,22 @@
     total0 = total.reshape(length, q_heads).T.reshape(rows, 1)
     mixed0 = mixed.reshape(length, q_heads, HD).transpose(1, 0, 2).reshape(rows, HD)
     which = req_prefix[0]
+    me = lax.axis_index("req")
+    parity = me % 2
+    pairs = [(i, i ^ 1) for i in range(devices)]
+    partner_prefix = lax.ppermute(req_prefix, "req", pairs)[0]
     rowwise = prefix_kv.reshape(block, 2 * kv_heads * HD)
-    gathered = lax.all_gather(rowwise, "req", axis=0, tiled=True)
-    stacked = gathered.reshape(devices, block, 2 * kv_heads * HD)
+    halves = [list(range(c, devices, 2)) for c in range(2)]
+    gathered = lax.all_gather(rowwise, "req", axis=0, tiled=True, axis_index_groups=halves)
+    mine = gathered.reshape(devices // 2, block, 2 * kv_heads * HD)
+    wanted = lax.dynamic_slice_in_dim(block_owner, partner_prefix * owned, owned)
+    offer = jnp.where(wanted % 2 == parity, wanted // 2, 0)
+    received = lax.ppermute(jnp.take(mine, offer, axis=0), "req", pairs)
     owners = lax.dynamic_slice_in_dim(block_owner, which * owned, owned)
+    use = (owners % 2 == parity).astype(jnp.int32)
+    local = jnp.where(use == 1, owners // 2, 0)
     context = prefix_attention(
-        owners, queries.reshape(length, q_heads * HD), stacked, peak0, total0, mixed0
+        local, use, queries.reshape(length, q_heads * HD), mine, received, peak0, total0, mixed0
     )
     partial_value = jnp.dot(context, o_weight, preferred_element_type=jnp.float32)
     pieces_out = partial_value.astype(jnp.bfloat16).reshape(length, n_tp, feat).transpose(1, 0, 2)

time: 186 us -> 212 us (1.14)
  waiting for transfers between devices: 115 us -> 126 us
  local copies, waits for them, and re-layouts: 11 us -> 17.3 us
  other arithmetic: 9.26 us -> 14.3 us
    all_gather x1, waiting for transfers between devices: 70.8 us -> 79.8 us  [shards(): lax.all_gather(rowwise, 'req', axis=0, tiled=True, axis_index_groups=halves)]
    gather x0 -> x1, local copies, waits for them, and re-layouts: none -> 6.13 us  [shards(): received = lax.ppermute(jnp.take(mine, offer, axis=0), 'req', pairs)]
    select_n x0 -> x2, other arithmetic: none -> 5.4 us  [the longest x1 4.73 us: shards(): received = lax.ppermute(jnp.take(mine, offer, axis=0), 'req', pairs)]
  transfers between devices with their start and end apart: 3 -> 5, of which waited for: 3 -> 3; matrix products, arithmetic and copies ran while one was open for 11% -> 10% of each run, Pallas kernels for 0% -> 0%
where the time goes in v5:
time: 212 us; the launch traced here: 211 us
  waiting for transfers between devices  126 us (59%)
  starting transfers between devices  18.8 us (9%)
  local copies, waits for them, and re-layouts  17.3 us (8%)
  between operations  15.6 us (7%)
  other arithmetic  14.3 us (7%)
  Pallas kernels  12.1 us (6%)
  matrix products  7.4 us (3%)
    all_gather x1, waiting for transfers between devices, shards(): lax.all_gather(rowwise, 'req', axis=0, tiled=True, axis_index_groups=halves)  79.8 us
    all_to_all x1, waiting for transfers between devices, shards(): pieces_in = lax.all_to_all(spread, 'tp', 0, 0, tiled=True)  28.1 us
    all_to_all x1, waiting for transfers between devices, shards(): lax.all_to_all(pieces_out, 'tp', 0, 0, tiled=True).astype(jnp.float32)  17.8 us
    pallas_call x1, Pallas kernels, prefix_attention(): pl.pallas_call(prefix_kernel, out_shape=jax.ShapeDtypeStruct((length, wid...  12.1 us
    all_to_all x1, starting transfers between devices, shards(): lax.all_to_all(pieces_out, 'tp', 0, 0, tiled=True).astype(jnp.float32)  11 us
    all_to_all x1, starting transfers between devices, shards(): pieces_in = lax.all_to_all(spread, 'tp', 0, 0, tiled=True)  6.2 us
    gather x1, local copies, waits for them, and re-layouts, shards(): received = lax.ppermute(jnp.take(mine, offer, axis=0), 'req', pairs)  6.13 us
    select_n x1, other arithmetic, shards(): received = lax.ppermute(jnp.take(mine, offer, axis=0), 'req', pairs)  4.73 us
  transfers between devices with their start and end apart: 5, of which 3 were waited for; matrix products, arithmetic and copies ran while one was open for 10% of the time, Pallas kernels for 0%

profile of v5, /device:TPU:1, one launch (start us, length us, event | category | flops | bytes accessed | tf_op | source)
XLA Modules:
  0.0 211.2 jit_solution(8301014291296496388)
XLA Ops:
  6.5 2.0 copy.66
  8.5 0.0 all-gather.2.cloned.1.call-update
  8.6 0.0 copy-start.4
  8.6 0.0 copy-start.5
  8.6 0.0 copy-start.6
  8.6 0.0 copy-start.3
  8.6 0.7 broadcast_in_dim.42
  9.3 0.1 pad.6.clone
  9.4 1.0 maximum_maximum_fusion
  10.4 1.3 broadcast_in_dim.72
  11.7 6.2 %all-to-all-start = ((bf16[8,144,640]{2,1,0:T(8,128)(2,1)}), bf16[8,144,640]{2,1,0:T(8,128)(2,1)S(1)}, u32[]{:S(2)}, u32[]{:S(2)}) async-start(bf16[8,144,640]{2,1,0:T(8,128)(2,1)} %broadcast_in_dim.72), calls=%async_computation | async-start | bytes 2949120 | tf_op jit(solution)/shard_map/all_to_all | solution.py:161
  17.9 1.0 collective-permute-start
  19.7 0.7 compare_select_fusion.2
  20.3 0.3 multiply_cosine_fusion
  21.3 0.1 compare_and_fusion
  21.4 28.1 %all-to-all-done = bf16[8,144,640]{2,1,0:T(8,128)(2,1)S(1)} async-done(((bf16[8,144,640]{2,1,0:T(8,128)(2,1)}), bf16[8,144,640]{2,1,0:T(8,128)(2,1)S(1)}, u32[]{:S(2)}, u32[]{:S(2)}) %all-to-all-start) | async-done | bytes 1474592 | tf_op jit(solution)/shard_map/all_to_all | solution.py:161
  49.5 2.9 %copy.39 = bf16[8,144,640]{1,2,0:T(8,128)(2,1)} copy(bf16[8,144,640]{2,1,0:T(8,128)(2,1)S(1)} %all-to-all-done) | data formatting | bytes 2949120 | tf_op jit(solution)/shard_map/all_to_all | solution.py:161
  52.4 79.8 %all-gather.2.cloned.1.call-done = bf16[16384,256]{1,0:T(8,128)(2,1)} async-done(((bf16[1024,256]{1,0:T(8,128)(2,1)}), bf16[16384,256]{1,0:T(8,128)(2,1)}) %all-gather.2.cloned.1.call-update) | async-done | bytes 8388624 | tf_op jit(solution)/shard_map/all_gather | solution.py:195
  132.2 6.1 %gather_fusion = bf16[8,1024,256]{2,1,0:T(8,128)(2,1)} fusion(bf16[16,1024,256]{2,1,0:T(8,128)(2,1)} %bitcast.81, s32[1024]{0:T(1024)S(1)} %pad_clamp_fusion), kind=kCustom, calls=%fused_computation | custom fusion | bytes 8388640 | tf_op jit(solution)/shard_map/jit(_take)/gather | solution.py:199
  138.3 4.7 %broadcast_select_fusion = bf16[8,1024,256]{2,1,0:T(8,128)(2,1)} fusion(bf16[8,1024,256]{2,1,0:T(8,128)(2,1)} %gather_fusion, pred[8]{0:T(512)(128)(4,1)S(1)} %get-tuple-element.5), kind=kLoop, calls=%fused_computation.2 | loop fusion | flops 2097152 | bytes 8388616 | tf_op jit(solution)/shard_map/jit(_take)/select_n | solution.py:199
  143.1 0.7 collective-permute-start.1
  143.8 0.4 convert_reduce_fusion
  144.2 2.0 multiply_reduce_fusion
  146.2 1.5 slice_convert_fusion
  147.7 0.0 copy-start.2
  147.7 2.2 %fusion.1 = bf16[128,5120]{0,1:T(8,128)(2,1)S(1)} fusion(f32[128,8,640]{0,2,1:T(8,128)S(1)} %slice_convert_fusion, f32[5120]{0:T(1024)S(1)} %reshape.238, f32[128]{0:T(128)S(1)} %add_rsqrt_fusion), kind=kLoop, calls=%fused_computation.5 | loop fusion | flops 1966080 | bytes 3953152 | tf_op jit(solution)/shard_map/convert_element_type | solution.py:166
  149.9 0.9 convolution_add_fusion
  150.9 0.1 copy.40
  151.0 0.1 copy.53
  151.1 0.1 copy.54
  151.3 0.1 multiply_subtract_fusion
  151.3 0.1 maximum_convert_fusion
  151.5 0.1 copy.43
  151.6 1.9 fusion.4
  153.5 0.2 fusion.25
  153.7 0.2 fusion.28
  153.9 0.1 fusion.9
  154.0 0.8 copy.60
  154.8 0.8 copy.58
  155.6 0.8 copy.46.q_ref
  156.4 1.4 fusion.7
  157.7 12.1 %shard_map.127 = bf16[128,384]{1,0:T(8,128)(2,1)} custom-call(s32[8]{0:T(128)} %get-tuple-element.7.local_ref, s32[8]{0:T(128)} %get-tuple-element.8.use_ref, bf16[128,384]{1,0:T(8,128)(2,1)} %copy.46.q_ref, bf16[16,1024,256]{2,1,0:T(8,128)(2,1)} %bitcast.82, bf16[16,1024,256]{2,1,0:T(8,128)(2,1)} %bitcast.83, ...), custom_call_target="tpu_custom_call" | custom-call | flops 1610612736 | bytes 8781824 | tf_op jit(solution)/shard_map/pallas_call | solution.py:103
  169.8 3.0 %convolution_convert_fusion = bf16[128,5120]{1,0:T(8,128)(2,1)S(1)} fusion(bf16[128,384]{1,0:T(8,128)(2,1)} %shard_map.127, bf16[384,5120]{1,0:T(8,128)(2,1)} %param.21), kind=kOutput, calls=%fused_computation.1 | convolution fusion | flops 503971840 | bytes 5341184 | tf_op jit(solution)/shard_map/dot_general | solution.py:206
  172.8 1.2 copy.65
  174.0 11.0 %all-to-all-start.1 = ((bf16[8,128,640]{2,1,0:T(8,128)(2,1)}), bf16[8,128,640]{2,1,0:T(8,128)(2,1)S(1)}, u32[]{:S(2)}, u32[]{:S(2)}) async-start(bf16[8,128,640]{2,1,0:T(8,128)(2,1)} %bitcast.87), calls=%async_computation.1 | async-start | bytes 2621440 | tf_op jit(solution)/shard_map/all_to_all | solution.py:208
  185.7 17.8 %all-to-all-done.1 = bf16[8,128,640]{2,1,0:T(8,128)(2,1)S(1)} async-done(((bf16[8,128,640]{2,1,0:T(8,128)(2,1)}), bf16[8,128,640]{2,1,0:T(8,128)(2,1)S(1)}, u32[]{:S(2)}, u32[]{:S(2)}) %all-to-all-start.1) | async-done | bytes 1310752 | tf_op jit(solution)/shard_map/all_to_all | solution.py:208
  203.4 0.2 convert_reduce_fusion.1
  203.6 0.8 select_convert_fusion
  (26 shorter events, 0.1 us)
Async XLA Ops:
  6.5 149.8 %copy-start = (bf16[5120,128]{1,0:T(8,128)(2,1)S(1)}, bf16[5120,128]{1,0:T(8,128)(2,1)}, u32[]{:S(2)}) copy-start(bf16[5120,128]{1,0:T(8,128)(2,1)} %param.19) | copy-start | bytes 3932164
  6.5 125.7 %all-gather.2.cloned.1.call-start = ((), (), s32[]{:S(2)}) async-start(), calls=%async_computation.2 | async-start | bytes 8912896 | tf_op jit(solution)/shard_map/all_gather | solution.py:195
  8.6 11.0 %copy-start.4 = (bf16[384]{0:T(512)(128)(2,1)S(1)}, bf16[384]{0:T(512)(128)(2,1)}, u32[]{:S(2)}) copy-start(bf16[384]{0:T(512)(128)(2,1)} %param.16) | copy-start | bytes 2308
  8.6 11.0 %copy-start.5 = (bf16[128]{0:T(256)(128)(2,1)S(1)}, bf16[128]{0:T(256)(128)(2,1)}, u32[]{:S(2)}) copy-start(bf16[128]{0:T(256)(128)(2,1)} %param.18) | copy-start | bytes 772
  8.6 11.0 %copy-start.6 = (bf16[128]{0:T(256)(128)(2,1)S(1)}, bf16[128]{0:T(256)(128)(2,1)}, u32[]{:S(2)}) copy-start(bf16[128]{0:T(256)(128)(2,1)} %param.20) | copy-start | bytes 772
  8.6 11.1 %copy-start.3 = (s32[32]{0:T(128)S(1)}, s32[32]{0:T(128)}, u32[]{:S(2)}) copy-start(s32[32]{0:T(128)} %param.25) | copy-start | bytes 388
  11.7 37.8 %all-to-all-start = ((bf16[8,144,640]{2,1,0:T(8,128)(2,1)}), bf16[8,144,640]{2,1,0:T(8,128)(2,1)S(1)}, u32[]{:S(2)}, u32[]{:S(2)}) async-start(bf16[8,144,640]{2,1,0:T(8,128)(2,1)} %broadcast_in_dim.72), calls=%async_computation | async-start | bytes 2949120 | tf_op jit(solution)/shard_map/all_to_all | solution.py:161
  17.9 2.7 %collective-permute-start = (s32[1]{0:T(128)}, s32[1]{0:T(128)}, u32[]{:S(2)}, u32[]{:S(2)}) collective-permute-start(s32[1]{0:T(128)} %param.24), channel_id=1, source_target_pairs={{0,8},{8,0},{16,24},{24,16},{32,40},{40,32},{48,56},{56,48},{64,72... | collective-permute-start | bytes 20 | tf_op jit(solution)/shard_map/ppermute | solution.py:192
  138.3 5.4 %copy-start.1 = (bf16[8,144,640]{1,2,0:T(8,128)(2,1)S(1)}, bf16[8,144,640]{1,2,0:T(8,128)(2,1)}, u32[]{:S(2)}) copy-start(bf16[8,144,640]{1,2,0:T(8,128)(2,1)} %copy.39) | copy-start | bytes 4423684
  143.1 14.7 %collective-permute-start.1 = (bf16[8,1024,256]{2,1,0:T(8,128)(2,1)}, bf16[8,1024,256]{2,1,0:T(8,128)(2,1)}, u32[]{:S(2)}, u32[]{:S(2)}) collective-permute-start(bf16[8,1024,256]{2,1,0:T(8,128)(2,1)} %broadcast_select_fusion), channel_id=1, source_target_pairs={{0,8},{8,0},{16,24},{24,16},{32,40},{40,32},{48,56},{56,48},{64,72... | collective-permute-start | bytes 12582920 | tf_op jit(solution)/shard_map/ppermute | solution.py:199
  147.7 2.2 %copy-start.2 = (bf16[5120,384]{1,0:T(8,128)(2,1)S(1)}, bf16[5120,384]{1,0:T(8,128)(2,1)}, u32[]{:S(2)}) copy-start(bf16[5120,384]{1,0:T(8,128)(2,1)} %param.15) | copy-start | bytes 11796484
  174.0 29.4 %all-to-all-start.1 = ((bf16[8,128,640]{2,1,0:T(8,128)(2,1)}), bf16[8,128,640]{2,1,0:T(8,128)(2,1)S(1)}, u32[]{:S(2)}, u32[]{:S(2)}) async-start(bf16[8,128,640]{2,1,0:T(8,128)(2,1)} %bitcast.87), calls=%async_computation.1 | async-start | bytes 2621440 | tf_op jit(solution)/shard_map/all_to_all | solution.py:208
Sparse Core Ops, SparseCore 0:
  9.8 122.3 all-gather.1

commit v6 on v4

--- a/solution.py
+++ b/solution.py
@@ -51,12 +51,16 @@
     return (peak, total, mixed)
 
 
-def prefix_kernel(own_ref, q_ref, k_ref, v_ref, m0_ref, l0_ref, a0_ref, o_ref, m_sc, l_sc, acc_sc):
+def prefix_kernel(
+    own_ref, q_ref, k_ref, v_ref, m0_ref, l0_ref, a0_ref, w_hbm, o_ref, m_sc, l_sc, acc_sc, w_sc, sem
+):
     step = pl.program_id(0)
     group = q_ref.shape[1] // HD
+    fetch = pltpu.make_async_copy(w_hbm, w_sc, sem.at[0])
 
     @pl.when(step == 0)
     def _():
+        fetch.start()
         m_sc[...] = m0_ref[...]
         l_sc[...] = l0_ref[...]
         acc_sc[...] = a0_ref[...]
@@ -80,25 +84,32 @@
 
     @pl.when(step == pl.num_programs(0) - 1)
     def _():
-        context = acc_sc[...] / l_sc[...]
+        context = (acc_sc[...] / l_sc[...]).astype(jnp.bfloat16)
         rows = q_ref.shape[0]
-        for h in range(group):
-            o_ref[:, h * HD:(h + 1) * HD] = context[h * rows:(h + 1) * rows].astype(o_ref.dtype)
-
-
-def prefix_attention(owners, flat_q, kv, peak0, total0, mixed0):
+        flat = jnp.concatenate([context[h * rows:(h + 1) * rows] for h in range(group)], axis=1)
+        fetch.wait()
+        partial = jnp.dot(flat, w_sc[...], preferred_element_type=jnp.float32).astype(o_ref.dtype)
+        pieces = o_ref.shape[0]
+        span = o_ref.shape[2]
+        for t in range(pieces):
+            o_ref[t] = partial[:, t * span:(t + 1) * span]
+
+
+def prefix_attention(owners, flat_q, kv, peak0, total0, mixed0, o_weight, pieces):
     length, width = flat_q.shape
+    out_width = o_weight.shape[1]
     steps = owners.shape[0]
     block = kv.shape[1]
     rows = peak0.shape[0]
     cost = pl.CostEstimate(
         flops=4 * rows * block * HD * steps,
         transcendentals=rows * block * steps,
-        bytes_accessed=2 * steps * block * HD * 2 + length * width * 4 + rows * HD * 4,
+        bytes_accessed=2 * steps * block * HD * 2 + length * width * 4 + rows * HD * 4
+        + width * out_width * 2 + length * out_width * 2,
     )
     return pl.pallas_call(
         prefix_kernel,
-        out_shape=jax.ShapeDtypeStruct((length, width), jnp.bfloat16),
+        out_shape=jax.ShapeDtypeStruct((pieces, length, out_width // pieces), jnp.bfloat16),
         grid_spec=pltpu.PrefetchScalarGridSpec(
             num_scalar_prefetch=1,
             grid=(steps,),
@@ -109,17 +120,20 @@
                 pl.BlockSpec((rows, 1), lambda j, own: (0, 0)),
                 pl.BlockSpec((rows, 1), lambda j, own: (0, 0)),
                 pl.BlockSpec((rows, HD), lambda j, own: (0, 0)),
+                pl.BlockSpec(memory_space=pl.ANY),
             ],
-            out_specs=pl.BlockSpec((length, width), lambda j, own: (0, 0)),
+            out_specs=pl.BlockSpec((pieces, length, out_width // pieces), lambda j, own: (0, 0, 0)),
             scratch_shapes=[
                 pltpu.VMEM((rows, 1), jnp.float32),
                 pltpu.VMEM((rows, 1), jnp.float32),
                 pltpu.VMEM((rows, HD), jnp.float32),
+                pltpu.VMEM((width, out_width), jnp.bfloat16),
+                pltpu.SemaphoreType.DMA((1,)),
             ],
         ),
         compiler_params=pltpu.CompilerParams(dimension_semantics=("arbitrary",)),
         cost_estimate=cost,
-    )(owners, flat_q, kv, kv, peak0, total0, mixed0)
+    )(owners, flat_q, kv, kv, peak0, total0, mixed0, o_weight)
 
 
 def shards(
@@ -184,11 +198,10 @@
     gathered = lax.all_gather(rowwise, "req", axis=0, tiled=True)
     stacked = gathered.reshape(devices, block, 2 * kv_heads * HD)
     owners = lax.dynamic_slice_in_dim(block_owner, which * owned, owned)
-    context = prefix_attention(
-        owners, queries.reshape(length, q_heads * HD), stacked, peak0, total0, mixed0
-    )
-    partial_value = jnp.dot(context, o_weight, preferred_element_type=jnp.float32)
-    pieces_out = partial_value.astype(jnp.bfloat16).reshape(length, n_tp, feat).transpose(1, 0, 2)
+    pieces_out = prefix_attention(
+        owners, queries.reshape(length, q_heads * HD), stacked, peak0, total0, mixed0,
+        o_weight, n_tp,
+    )
     summed = jnp.sum(lax.all_to_all(pieces_out, "tp", 0, 0, tiled=True).astype(jnp.float32), axis=0)
     valid = slot_index < suffix_len[0]
     return jnp.where(valid[:, None], summed, jnp.float32(0.0)).astype(jnp.bfloat16)

time: 186 us -> 184 us (0.989)
  matrix products: 7.41 us -> 4.39 us
    dot_general x1 -> x0, matrix products: 3.02 us -> none  [shards(): jnp.dot(context, o_weight, preferred_element_type=jnp.float32)]
where the time goes in v6:
time: 184 us; the launch traced here: 183 us
  waiting for transfers between devices  115 us (62%)
  starting transfers between devices  17.2 us (9%)
  between operations  14.9 us (8%)
  Pallas kernels  13 us (7%)
  local copies, waits for them, and re-layouts  9.79 us (5%)
  other arithmetic  9.26 us (5%)
  matrix products  4.39 us (2%)
    all_gather x1, waiting for transfers between devices, shards(): gathered = lax.all_gather(rowwise, 'req', axis=0, tiled=True)  70.8 us
    all_to_all x1, waiting for transfers between devices, shards(): pieces_in = lax.all_to_all(spread, 'tp', 0, 0, tiled=True)  26.5 us
    all_to_all x1, waiting for transfers between devices, shards(): lax.all_to_all(pieces_out, 'tp', 0, 0, tiled=True).astype(jnp.float32)  17.5 us
    pallas_call x1, Pallas kernels, prefix_attention(): pl.pallas_call(prefix_kernel, out_shape=jax.ShapeDtypeStruct((pieces, len...  13 us
    all_to_all x1, starting transfers between devices, shards(): lax.all_to_all(pieces_out, 'tp', 0, 0, tiled=True).astype(jnp.float32)  10.9 us
    all_to_all x1, starting transfers between devices, shards(): pieces_in = lax.all_to_all(spread, 'tp', 0, 0, tiled=True)  6.35 us
    unnamed x23, local copies, waits for them, and re-layouts  4.01 us
  transfers between devices with their start and end apart: 3, of which 3 were waited for; matrix products, arithmetic and copies ran while one was open for 11% of the time, Pallas kernels for 0%

profile of v6, /device:TPU:1, one launch (start us, length us, event | category | flops | bytes accessed | tf_op | source)
XLA Modules:
  0.0 183.4 jit_solution(1248467225304223176)
XLA Ops:
  6.5 0.0 copy-start
  6.5 0.0 copy-start.3
  6.5 0.0 copy-start.2
  6.5 0.0 all-gather.2.cloned.1.call-start
  6.5 2.0 %copy.62 = bf16[128,8,2,128]{3,1,2,0:T(8,128)(2,1)} copy(bf16[128,8,2,128]{3,2,1,0:T(2,128)(2,1)} %bitcast.81) | data formatting | bytes 1048576
  8.6 0.0 all-gather.2.cloned.1.call-update
  8.6 0.0 copy-done.3
  8.6 0.1 pad.6.clone
  8.7 0.0 copy-done.2
  8.7 0.1 maximum_maximum_fusion
  8.8 1.2 broadcast_in_dim.25
  10.1 6.3 %all-to-all-start = ((bf16[8,144,640]{2,1,0:T(8,128)(2,1)}), bf16[8,144,640]{2,1,0:T(8,128)(2,1)S(1)}, u32[]{:S(2)}, u32[]{:S(2)}) async-start(bf16[8,144,640]{2,1,0:T(8,128)(2,1)} %broadcast_in_dim.25), calls=%async_computation | async-start | bytes 2949120 | tf_op jit(solution)/shard_map/all_to_all | solution.py:169
  16.4 0.0 copy-done.4
  16.4 0.0 copy-done.5
  16.5 0.0 copy-done.6
  17.1 0.0 copy-done.7
  17.2 0.6 dynamic_slice.3.own_ref
  17.8 0.3 multiply_cosine_fusion
  18.1 26.5 %all-to-all-done = bf16[8,144,640]{2,1,0:T(8,128)(2,1)S(1)} async-done(((bf16[8,144,640]{2,1,0:T(8,128)(2,1)}), bf16[8,144,640]{2,1,0:T(8,128)(2,1)S(1)}, u32[]{:S(2)}, u32[]{:S(2)}) %all-to-all-start) | async-done | bytes 1474592 | tf_op jit(solution)/shard_map/all_to_all | solution.py:169
  44.6 2.9 %copy.39 = bf16[8,144,640]{1,2,0:T(8,128)(2,1)} copy(bf16[8,144,640]{2,1,0:T(8,128)(2,1)S(1)} %all-to-all-done) | data formatting | bytes 2949120 | tf_op jit(solution)/shard_map/all_to_all | solution.py:169
  47.5 1.7 convert_reduce_fusion
  49.2 2.0 %multiply_reduce_fusion = f32[128]{0:T(128)S(1)} fusion(bf16[144,8,640]{0,2,1:T(8,128)(2,1)} %bitcast.74), kind=kLoop, calls=%fused_computation.5 | loop fusion | flops 1965952 | bytes 1311232 | tf_op jit(solution)/shard_map/reduce_sum | solution.py:173
  51.2 1.5 slice_convert_fusion
  52.8 0.0 copy-start.1
  52.8 2.2 %fusion.1 = bf16[128,5120]{0,1:T(8,128)(2,1)S(1)} fusion(f32[128,8,640]{0,2,1:T(8,128)S(1)} %slice_convert_fusion, f32[5120]{0:T(1024)S(1)} %reshape.227, f32[128]{0:T(128)S(1)} %add_rsqrt_fusion), kind=kLoop, calls=%fused_computation.2 | loop fusion | flops 1966080 | bytes 3953152 | tf_op jit(solution)/shard_map/convert_element_type | solution.py:174
  55.0 0.0 copy-done.1
  55.0 0.9 convolution_add_fusion
  55.9 0.1 copy.40
  56.1 0.1 copy.52
  56.2 0.1 copy.53
  56.3 0.1 multiply_subtract_fusion
  56.4 0.1 maximum_convert_fusion
  56.5 0.1 copy.43
  56.6 1.9 %fusion.4 = f32[128,1,128]{0,2,1:T(8,128)S(1)} fusion(bf16[128,5120]{0,1:T(8,128)(2,1)S(1)} %fusion.1, bf16[5120,128]{1,0:T(8,128)(2,1)} %param.17, f32[128]{0:T(128)S(1)} %convert_element_type.88), kind=kOutput, calls=%fused_computation.13 | convolution fusion | flops 167788544 | bytes 2687488 | tf_op jit(solution)/shard_map/dot_general | solution.py:181
  58.5 0.2 fusion.25
  58.7 0.2 fusion.28
  58.9 0.1 fusion.9
  59.0 0.8 copy.58
  59.8 0.8 copy.56
  60.7 0.8 copy.46.q_ref
  61.4 0.0 copy-done
  61.4 1.4 fusion.7
  62.8 70.8 %all-gather.2.cloned.1.call-done = bf16[32768,256]{1,0:T(8,128)(2,1)} async-done(((bf16[1024,256]{1,0:T(8,128)(2,1)}), bf16[32768,256]{1,0:T(8,128)(2,1)}) %all-gather.2.cloned.1.call-update) | async-done | bytes 16777232 | tf_op jit(solution)/shard_map/all_gather | solution.py:198
  133.6 13.0 %shard_map.127 = bf16[8,128,640]{2,1,0:T(8,128)(2,1)} custom-call(s32[8]{0:T(128)} %dynamic_slice.3.own_ref, bf16[128,384]{1,0:T(8,128)(2,1)} %copy.46.q_ref, bf16[32,1024,256]{2,1,0:T(8,128)(2,1)} %bitcast.71, bf16[32,1024,256]{2,1,0:T(8,128)(2,1)} %bitcast.72, f32[384,1]{1,0:T(8,128)} %bitcast.79, f32[384,1]{1,0:T(8,128)} %bitcast.78, ...), custom_call_target="tpu_custom_call" | custom-call | flops 1610612736 | bytes 9830400 | tf_op jit(solution)/shard_map/pallas_call | solution.py:110
  146.6 10.9 %all-to-all-start.1 = ((bf16[8,128,640]{2,1,0:T(8,128)(2,1)}), bf16[8,128,640]{2,1,0:T(8,128)(2,1)S(1)}, u32[]{:S(2)}, u32[]{:S(2)}) async-start(bf16[8,128,640]{2,1,0:T(8,128)(2,1)} %shard_map.127), calls=%async_computation.1 | async-start | bytes 2621440 | tf_op jit(solution)/shard_map/all_to_all | solution.py:205
  158.1 17.5 %all-to-all-done.1 = bf16[8,128,640]{2,1,0:T(8,128)(2,1)S(1)} async-done(((bf16[8,128,640]{2,1,0:T(8,128)(2,1)}), bf16[8,128,640]{2,1,0:T(8,128)(2,1)S(1)}, u32[]{:S(2)}, u32[]{:S(2)}) %all-to-all-start.1) | async-done | bytes 1310752 | tf_op jit(solution)/shard_map/all_to_all | solution.py:205
  175.6 0.2 convert_reduce_fusion.1
  175.8 0.8 select_convert_fusion
  (18 shorter events, 0.1 us)
Async XLA Ops:
  6.5 54.9 %copy-start = (bf16[5120,128]{1,0:T(8,128)(2,1)S(1)}, bf16[5120,128]{1,0:T(8,128)(2,1)}, u32[]{:S(2)}) copy-start(bf16[5120,128]{1,0:T(8,128)(2,1)} %param.19) | copy-start | bytes 3932164
  6.5 2.1 %copy-start.3 = (bf16[640]{0:T(1024)(128)(2,1)S(1)}, bf16[640]{0:T(1024)(128)(2,1)}, u32[]{:S(2)}) copy-start(bf16[640]{0:T(1024)(128)(2,1)} %param.14) | copy-start | bytes 3844
  6.5 2.2 %copy-start.2 = (bf16[128,640]{1,0:T(8,128)(2,1)S(1)}, bf16[128,640]{1,0:T(8,128)(2,1)}, u32[]{:S(2)}) copy-start(bf16[128,640]{1,0:T(8,128)(2,1)} %param.13) | copy-start | bytes 491524
  6.5 127.1 %all-gather.2.cloned.1.call-start = ((), (), s32[]{:S(2)}) async-start(), calls=%async_computation.2 | async-start | bytes 17301504 | tf_op jit(solution)/shard_map/all_gather | solution.py:198
  10.1 6.4 %copy-start.4 = (bf16[384]{0:T(512)(128)(2,1)S(1)}, bf16[384]{0:T(512)(128)(2,1)}, u32[]{:S(2)}) copy-start(bf16[384]{0:T(512)(128)(2,1)} %param.16) | copy-start | bytes 2308
  10.1 6.4 %copy-start.5 = (bf16[128]{0:T(256)(128)(2,1)S(1)}, bf16[128]{0:T(256)(128)(2,1)}, u32[]{:S(2)}) copy-start(bf16[128]{0:T(256)(128)(2,1)} %param.18) | copy-start | bytes 772
  10.1 6.4 %copy-start.6 = (bf16[128]{0:T(256)(128)(2,1)S(1)}, bf16[128]{0:T(256)(128)(2,1)}, u32[]{:S(2)}) copy-start(bf16[128]{0:T(256)(128)(2,1)} %param.20) | copy-start | bytes 772
  10.1 7.1 %copy-start.7 = (s32[32]{0:T(128)S(1)}, s32[32]{0:T(128)}, u32[]{:S(2)}) copy-start(s32[32]{0:T(128)} %param.25) | copy-start | bytes 388
  10.1 34.5 %all-to-all-start = ((bf16[8,144,640]{2,1,0:T(8,128)(2,1)}), bf16[8,144,640]{2,1,0:T(8,128)(2,1)S(1)}, u32[]{:S(2)}, u32[]{:S(2)}) async-start(bf16[8,144,640]{2,1,0:T(8,128)(2,1)} %broadcast_in_dim.25), calls=%async_computation | async-start | bytes 2949120 | tf_op jit(solution)/shard_map/all_to_all | solution.py:169
  52.8 2.2 %copy-start.1 = (bf16[5120,384]{1,0:T(8,128)(2,1)S(1)}, bf16[5120,384]{1,0:T(8,128)(2,1)}, u32[]{:S(2)}) copy-start(bf16[5120,384]{1,0:T(8,128)(2,1)} %param.15) | copy-start | bytes 11796484
  146.6 29.0 %all-to-all-start.1 = ((bf16[8,128,640]{2,1,0:T(8,128)(2,1)}), bf16[8,128,640]{2,1,0:T(8,128)(2,1)S(1)}, u32[]{:S(2)}, u32[]{:S(2)}) async-start(bf16[8,128,640]{2,1,0:T(8,128)(2,1)} %shard_map.127), calls=%async_computation.1 | async-start | bytes 2621440 | tf_op jit(solution)/shard_map/all_to_all | solution.py:205
Sparse Core Ops, SparseCore 0:
  9.9 123.6 all-gather.1

commit v7 on v6

--- a/solution.py
+++ b/solution.py
@@ -52,7 +52,8 @@
 
 
 def prefix_kernel(
-    own_ref, q_ref, k_ref, v_ref, m0_ref, l0_ref, a0_ref, w_hbm, o_ref, m_sc, l_sc, acc_sc, w_sc, sem
+    own_ref, q_ref, k0_ref, v0_ref, k1_ref, v1_ref, m0_ref, l0_ref, a0_ref, w_hbm,
+    o_ref, m_sc, l_sc, acc_sc, q_sc, w_sc, sem,
 ):
     step = pl.program_id(0)
     group = q_ref.shape[1] // HD
@@ -64,21 +65,31 @@
         m_sc[...] = m0_ref[...]
         l_sc[...] = l0_ref[...]
         acc_sc[...] = a0_ref[...]
-
-    q = q_ref[...]
-    stacked = jnp.concatenate([q[:, h * HD:(h + 1) * HD] for h in range(group)], axis=0)
-    keys = k_ref[0]
-    values = v_ref[0]
-    scores = lax.dot_general(
-        stacked, keys, (((1,), (1,)), ((), ())), preferred_element_type=jnp.float32
+        q = q_ref[...]
+        q_sc[...] = jnp.concatenate([q[:, h * HD:(h + 1) * HD] for h in range(group)], axis=0)
+
+    stacked = q_sc[...]
+    dims = (((1,), (1,)), ((), ()))
+    first = lax.dot_general(
+        stacked, k0_ref[0], dims, preferred_element_type=jnp.float32
+    ) * HD ** (-0.5)
+    second = lax.dot_general(
+        stacked, k1_ref[0], dims, preferred_element_type=jnp.float32
     ) * HD ** (-0.5)
     old = m_sc[...]
-    new = jnp.maximum(old, jnp.max(scores, axis=-1, keepdims=True))
+    new = jnp.maximum(
+        old,
+        jnp.maximum(jnp.max(first, axis=-1, keepdims=True), jnp.max(second, axis=-1, keepdims=True)),
+    )
     alpha = jnp.exp(old - new)
-    weights = jnp.exp(scores - new)
-    l_sc[...] = alpha * l_sc[...] + jnp.sum(weights, axis=-1, keepdims=True)
-    acc_sc[...] = alpha * acc_sc[...] + jnp.dot(
-        weights.astype(jnp.bfloat16), values, preferred_element_type=jnp.float32
+    w0 = jnp.exp(first - new)
+    w1 = jnp.exp(second - new)
+    l_sc[...] = alpha * l_sc[...] + (
+        jnp.sum(w0, axis=-1, keepdims=True) + jnp.sum(w1, axis=-1, keepdims=True)
+    )
+    acc_sc[...] = alpha * acc_sc[...] + (
+        jnp.dot(w0.astype(jnp.bfloat16), v0_ref[0], preferred_element_type=jnp.float32)
+        + jnp.dot(w1.astype(jnp.bfloat16), v1_ref[0], preferred_element_type=jnp.float32)
     )
     m_sc[...] = new
 
@@ -112,11 +123,13 @@
         out_shape=jax.ShapeDtypeStruct((pieces, length, out_width // pieces), jnp.bfloat16),
         grid_spec=pltpu.PrefetchScalarGridSpec(
             num_scalar_prefetch=1,
-            grid=(steps,),
+            grid=(steps // 2,),
             in_specs=[
                 pl.BlockSpec((length, width), lambda j, own: (0, 0)),
-                pl.BlockSpec((1, block, HD), lambda j, own: (own[j], 0, 0)),
-                pl.BlockSpec((1, block, HD), lambda j, own: (own[j], 0, 1)),
+                pl.BlockSpec((1, block, HD), lambda j, own: (own[2 * j], 0, 0)),
+                pl.BlockSpec((1, block, HD), lambda j, own: (own[2 * j], 0, 1)),
+                pl.BlockSpec((1, block, HD), lambda j, own: (own[2 * j + 1], 0, 0)),
+                pl.BlockSpec((1, block, HD), lambda j, own: (own[2 * j + 1], 0, 1)),
                 pl.BlockSpec((rows, 1), lambda j, own: (0, 0)),
                 pl.BlockSpec((rows, 1), lambda j, own: (0, 0)),
                 pl.BlockSpec((rows, HD), lambda j, own: (0, 0)),
@@ -127,13 +140,14 @@
                 pltpu.VMEM((rows, 1), jnp.float32),
                 pltpu.VMEM((rows, 1), jnp.float32),
                 pltpu.VMEM((rows, HD), jnp.float32),
+                pltpu.VMEM((rows, HD), jnp.bfloat16),
                 pltpu.VMEM((width, out_width), jnp.bfloat16),
                 pltpu.SemaphoreType.DMA((1,)),
             ],
         ),
         compiler_params=pltpu.CompilerParams(dimension_semantics=("arbitrary",)),
         cost_estimate=cost,
-    )(owners, flat_q, kv, kv, peak0, total0, mixed0, o_weight)
+    )(owners, flat_q, kv, kv, kv, kv, peak0, total0, mixed0, o_weight)
 
 
 def shards(

time: 184 us -> 182 us (0.989)
  Pallas kernels: 13 us -> 11 us
    pallas_call x1, Pallas kernels: 13 us -> 11 us  [prefix_attention(): pl.pallas_call(prefix_kernel, out_shape=jax.ShapeDtypeStruct((pieces, len...]
where the time goes in v7:
time: 182 us; the launch traced here: 181 us
  waiting for transfers between devices  115 us (63%)
  starting transfers between devices  17.2 us (9%)
  between operations  14.9 us (8%)
  Pallas kernels  11 us (6%)
  local copies, waits for them, and re-layouts  9.79 us (5%)
  other arithmetic  9.26 us (5%)
  matrix products  4.39 us (2%)
    all_gather x1, waiting for transfers between devices, shards(): gathered = lax.all_gather(rowwise, 'req', axis=0, tiled=True)  70.8 us
    all_to_all x1, waiting for transfers between devices, shards(): pieces_in = lax.all_to_all(spread, 'tp', 0, 0, tiled=True)  26.5 us
    all_to_all x1, waiting for transfers between devices, shards(): lax.all_to_all(pieces_out, 'tp', 0, 0, tiled=True).astype(jnp.float32)  17.5 us
    pallas_call x1, Pallas kernels, prefix_attention(): pl.pallas_call(prefix_kernel, out_shape=jax.ShapeDtypeStruct((pieces, len...  11 us
    all_to_all x1, starting transfers between devices, shards(): lax.all_to_all(pieces_out, 'tp', 0, 0, tiled=True).astype(jnp.float32)  10.9 us
    all_to_all x1, starting transfers between devices, shards(): pieces_in = lax.all_to_all(spread, 'tp', 0, 0, tiled=True)  6.35 us
    unnamed x23, local copies, waits for them, and re-layouts  4.01 us
  transfers between devices with their start and end apart: 3, of which 3 were waited for; matrix products, arithmetic and copies ran while one was open for 11% of the time, Pallas kernels for 0%

profile of v7, /device:TPU:1, one launch (start us, length us, event | category | flops | bytes accessed | tf_op | source)
XLA Modules:
  0.0 181.4 jit_solution(6868247491594544565)
XLA Ops:
  6.5 0.0 copy-start
  6.5 0.0 copy-start.3
  6.5 0.0 copy-start.2
  6.5 0.0 all-gather.2.cloned.1.call-start
  6.5 2.0 %copy.62 = bf16[128,8,2,128]{3,1,2,0:T(8,128)(2,1)} copy(bf16[128,8,2,128]{3,2,1,0:T(2,128)(2,1)} %bitcast.83) | data formatting | bytes 1048576
  8.6 0.0 all-gather.2.cloned.1.call-update
  8.6 0.0 copy-done.3
  8.6 0.1 pad.6.clone
  8.7 0.0 copy-done.2
  8.7 0.1 maximum_maximum_fusion
  8.8 1.2 broadcast_in_dim.25
  10.1 6.3 %all-to-all-start = ((bf16[8,144,640]{2,1,0:T(8,128)(2,1)}), bf16[8,144,640]{2,1,0:T(8,128)(2,1)S(1)}, u32[]{:S(2)}, u32[]{:S(2)}) async-start(bf16[8,144,640]{2,1,0:T(8,128)(2,1)} %broadcast_in_dim.25), calls=%async_computation | async-start | bytes 2949120 | tf_op jit(solution)/shard_map/all_to_all | solution.py:183
  16.4 0.0 copy-done.4
  16.4 0.0 copy-done.5
  16.5 0.0 copy-done.6
  17.1 0.0 copy-done.7
  17.2 0.6 dynamic_slice.3.own_ref
  17.8 0.3 multiply_cosine_fusion
  18.1 26.5 %all-to-all-done = bf16[8,144,640]{2,1,0:T(8,128)(2,1)S(1)} async-done(((bf16[8,144,640]{2,1,0:T(8,128)(2,1)}), bf16[8,144,640]{2,1,0:T(8,128)(2,1)S(1)}, u32[]{:S(2)}, u32[]{:S(2)}) %all-to-all-start) | async-done | bytes 1474592 | tf_op jit(solution)/shard_map/all_to_all | solution.py:183
  44.6 2.9 %copy.39 = bf16[8,144,640]{1,2,0:T(8,128)(2,1)} copy(bf16[8,144,640]{2,1,0:T(8,128)(2,1)S(1)} %all-to-all-done) | data formatting | bytes 2949120 | tf_op jit(solution)/shard_map/all_to_all | solution.py:183
  47.5 1.7 convert_reduce_fusion
  49.2 2.0 %multiply_reduce_fusion = f32[128]{0:T(128)S(1)} fusion(bf16[144,8,640]{0,2,1:T(8,128)(2,1)} %bitcast.76), kind=kLoop, calls=%fused_computation.5 | loop fusion | flops 1965952 | bytes 1311232 | tf_op jit(solution)/shard_map/reduce_sum | solution.py:187
  51.2 1.5 slice_convert_fusion
  52.8 0.0 copy-start.1
  52.8 2.2 %fusion.1 = bf16[128,5120]{0,1:T(8,128)(2,1)S(1)} fusion(f32[128,8,640]{0,2,1:T(8,128)S(1)} %slice_convert_fusion, f32[5120]{0:T(1024)S(1)} %reshape.227, f32[128]{0:T(128)S(1)} %add_rsqrt_fusion), kind=kLoop, calls=%fused_computation.2 | loop fusion | flops 1966080 | bytes 3953152 | tf_op jit(solution)/shard_map/convert_element_type | solution.py:188
  55.0 0.0 copy-done.1
  55.0 0.9 convolution_add_fusion
  55.9 0.1 copy.40
  56.1 0.1 copy.52
  56.2 0.1 copy.53
  56.3 0.1 multiply_subtract_fusion
  56.4 0.1 maximum_convert_fusion
  56.5 0.1 copy.43
  56.6 1.9 %fusion.4 = f32[128,1,128]{0,2,1:T(8,128)S(1)} fusion(bf16[128,5120]{0,1:T(8,128)(2,1)S(1)} %fusion.1, bf16[5120,128]{1,0:T(8,128)(2,1)} %param.17, f32[128]{0:T(128)S(1)} %convert_element_type.88), kind=kOutput, calls=%fused_computation.13 | convolution fusion | flops 167788544 | bytes 2687488 | tf_op jit(solution)/shard_map/dot_general | solution.py:195
  58.5 0.2 fusion.25
  58.7 0.2 fusion.28
  58.9 0.1 fusion.9
  59.0 0.8 copy.58
  59.8 0.8 copy.56
  60.7 0.8 copy.46.q_ref
  61.4 0.0 copy-done
  61.4 1.4 fusion.7
  62.8 70.8 %all-gather.2.cloned.1.call-done = bf16[32768,256]{1,0:T(8,128)(2,1)} async-done(((bf16[1024,256]{1,0:T(8,128)(2,1)}), bf16[32768,256]{1,0:T(8,128)(2,1)}) %all-gather.2.cloned.1.call-update) | async-done | bytes 16777232 | tf_op jit(solution)/shard_map/all_gather | solution.py:212
  133.6 11.0 %shard_map.127 = bf16[8,128,640]{2,1,0:T(8,128)(2,1)} custom-call(s32[8]{0:T(128)} %dynamic_slice.3.own_ref, bf16[128,384]{1,0:T(8,128)(2,1)} %copy.46.q_ref, bf16[32,1024,256]{2,1,0:T(8,128)(2,1)} %bitcast.71, bf16[32,1024,256]{2,1,0:T(8,128)(2,1)} %bitcast.72, bf16[32,1024,256]{2,1,0:T(8,128)(2,1)} %bitcast.73, bf16[32,1024,256]{2,1,0:T(8,128)(2,1)} %bitcast.74, ...), custom_call_target="tpu_custom_call" | custom-call | flops 1610612736 | bytes 9830400 | tf_op jit(solution)/shard_map/pallas_call | solution.py:121
  144.7 10.9 %all-to-all-start.1 = ((bf16[8,128,640]{2,1,0:T(8,128)(2,1)}), bf16[8,128,640]{2,1,0:T(8,128)(2,1)S(1)}, u32[]{:S(2)}, u32[]{:S(2)}) async-start(bf16[8,128,640]{2,1,0:T(8,128)(2,1)} %shard_map.127), calls=%async_computation.1 | async-start | bytes 2621440 | tf_op jit(solution)/shard_map/all_to_all | solution.py:219
  156.2 17.5 %all-to-all-done.1 = bf16[8,128,640]{2,1,0:T(8,128)(2,1)S(1)} async-done(((bf16[8,128,640]{2,1,0:T(8,128)(2,1)}), bf16[8,128,640]{2,1,0:T(8,128)(2,1)S(1)}, u32[]{:S(2)}, u32[]{:S(2)}) %all-to-all-start.1) | async-done | bytes 1310752 | tf_op jit(solution)/shard_map/all_to_all | solution.py:219
  173.6 0.2 convert_reduce_fusion.1
  173.8 0.8 select_convert_fusion
  (18 shorter events, 0.1 us)
Async XLA Ops:
  6.5 54.9 %copy-start = (bf16[5120,128]{1,0:T(8,128)(2,1)S(1)}, bf16[5120,128]{1,0:T(8,128)(2,1)}, u32[]{:S(2)}) copy-start(bf16[5120,128]{1,0:T(8,128)(2,1)} %param.19) | copy-start | bytes 3932164
  6.5 2.1 %copy-start.3 = (bf16[640]{0:T(1024)(128)(2,1)S(1)}, bf16[640]{0:T(1024)(128)(2,1)}, u32[]{:S(2)}) copy-start(bf16[640]{0:T(1024)(128)(2,1)} %param.14) | copy-start | bytes 3844
  6.5 2.2 %copy-start.2 = (bf16[128,640]{1,0:T(8,128)(2,1)S(1)}, bf16[128,640]{1,0:T(8,128)(2,1)}, u32[]{:S(2)}) copy-start(bf16[128,640]{1,0:T(8,128)(2,1)} %param.13) | copy-start | bytes 491524
  6.5 127.1 %all-gather.2.cloned.1.call-start = ((), (), s32[]{:S(2)}) async-start(), calls=%async_computation.2 | async-start | bytes 17301504 | tf_op jit(solution)/shard_map/all_gather | solution.py:212
  10.1 6.4 %copy-start.4 = (bf16[384]{0:T(512)(128)(2,1)S(1)}, bf16[384]{0:T(512)(128)(2,1)}, u32[]{:S(2)}) copy-start(bf16[384]{0:T(512)(128)(2,1)} %param.16) | copy-start | bytes 2308
  10.1 6.4 %copy-start.5 = (bf16[128]{0:T(256)(128)(2,1)S(1)}, bf16[128]{0:T(256)(128)(2,1)}, u32[]{:S(2)}) copy-start(bf16[128]{0:T(256)(128)(2,1)} %param.18) | copy-start | bytes 772
  10.1 6.4 %copy-start.6 = (bf16[128]{0:T(256)(128)(2,1)S(1)}, bf16[128]{0:T(256)(128)(2,1)}, u32[]{:S(2)}) copy-start(bf16[128]{0:T(256)(128)(2,1)} %param.20) | copy-start | bytes 772
  10.1 7.1 %copy-start.7 = (s32[32]{0:T(128)S(1)}, s32[32]{0:T(128)}, u32[]{:S(2)}) copy-start(s32[32]{0:T(128)} %param.25) | copy-start | bytes 388
  10.1 34.5 %all-to-all-start = ((bf16[8,144,640]{2,1,0:T(8,128)(2,1)}), bf16[8,144,640]{2,1,0:T(8,128)(2,1)S(1)}, u32[]{:S(2)}, u32[]{:S(2)}) async-start(bf16[8,144,640]{2,1,0:T(8,128)(2,1)} %broadcast_in_dim.25), calls=%async_computation | async-start | bytes 2949120 | tf_op jit(solution)/shard_map/all_to_all | solution.py:183
  52.8 2.2 %copy-start.1 = (bf16[5120,384]{1,0:T(8,128)(2,1)S(1)}, bf16[5120,384]{1,0:T(8,128)(2,1)}, u32[]{:S(2)}) copy-start(bf16[5120,384]{1,0:T(8,128)(2,1)} %param.15) | copy-start | bytes 11796484
  144.7 29.0 %all-to-all-start.1 = ((bf16[8,128,640]{2,1,0:T(8,128)(2,1)}), bf16[8,128,640]{2,1,0:T(8,128)(2,1)S(1)}, u32[]{:S(2)}, u32[]{:S(2)}) async-start(bf16[8,128,640]{2,1,0:T(8,128)(2,1)} %shard_map.127), calls=%async_computation.1 | async-start | bytes 2621440 | tf_op jit(solution)/shard_map/all_to_all | solution.py:219
Sparse Core Ops, SparseCore 0:
  9.9 123.6 all-gather.1

commit v8 on v7

--- a/solution.py
+++ b/solution.py
@@ -52,7 +52,7 @@
 
 
 def prefix_kernel(
-    own_ref, q_ref, k0_ref, v0_ref, k1_ref, v1_ref, m0_ref, l0_ref, a0_ref, w_hbm,
+    own_ref, q_ref, k0_ref, k1_ref, m0_ref, l0_ref, a0_ref, w_hbm,
     o_ref, m_sc, l_sc, acc_sc, q_sc, w_sc, sem,
 ):
     step = pl.program_id(0)
@@ -70,11 +70,13 @@
 
     stacked = q_sc[...]
     dims = (((1,), (1,)), ((), ()))
+    kv0 = k0_ref[...]
+    kv1 = k1_ref[...]
     first = lax.dot_general(
-        stacked, k0_ref[0], dims, preferred_element_type=jnp.float32
+        stacked, kv0[:, 0, :], dims, preferred_element_type=jnp.float32
     ) * HD ** (-0.5)
     second = lax.dot_general(
-        stacked, k1_ref[0], dims, preferred_element_type=jnp.float32
+        stacked, kv1[:, 0, :], dims, preferred_element_type=jnp.float32
     ) * HD ** (-0.5)
     old = m_sc[...]
     new = jnp.maximum(
@@ -88,8 +90,8 @@
         jnp.sum(w0, axis=-1, keepdims=True) + jnp.sum(w1, axis=-1, keepdims=True)
     )
     acc_sc[...] = alpha * acc_sc[...] + (
-        jnp.dot(w0.astype(jnp.bfloat16), v0_ref[0], preferred_element_type=jnp.float32)
-        + jnp.dot(w1.astype(jnp.bfloat16), v1_ref[0], preferred_element_type=jnp.float32)
+        jnp.dot(w0.astype(jnp.bfloat16), kv0[:, 1, :], preferred_element_type=jnp.float32)
+        + jnp.dot(w1.astype(jnp.bfloat16), kv1[:, 1, :], preferred_element_type=jnp.float32)
     )
     m_sc[...] = new
 
@@ -110,7 +112,7 @@
     length, width = flat_q.shape
     out_width = o_weight.shape[1]
     steps = owners.shape[0]
-    block = kv.shape[1]
+    block = kv.shape[0] // steps // NPREF
     rows = peak0.shape[0]
     cost = pl.CostEstimate(
         flops=4 * rows * block * HD * steps,
@@ -126,10 +128,8 @@
             grid=(steps // 2,),
             in_specs=[
                 pl.BlockSpec((length, width), lambda j, own: (0, 0)),
-                pl.BlockSpec((1, block, HD), lambda j, own: (own[2 * j], 0, 0)),
-                pl.BlockSpec((1, block, HD), lambda j, own: (own[2 * j], 0, 1)),
-                pl.BlockSpec((1, block, HD), lambda j, own: (own[2 * j + 1], 0, 0)),
-                pl.BlockSpec((1, block, HD), lambda j, own: (own[2 * j + 1], 0, 1)),
+                pl.BlockSpec((block, 2, HD), lambda j, own: (own[2 * j], 0, 0)),
+                pl.BlockSpec((block, 2, HD), lambda j, own: (own[2 * j + 1], 0, 0)),
                 pl.BlockSpec((rows, 1), lambda j, own: (0, 0)),
                 pl.BlockSpec((rows, 1), lambda j, own: (0, 0)),
                 pl.BlockSpec((rows, HD), lambda j, own: (0, 0)),
@@ -147,7 +147,7 @@
         ),
         compiler_params=pltpu.CompilerParams(dimension_semantics=("arbitrary",)),
         cost_estimate=cost,
-    )(owners, flat_q, kv, kv, kv, kv, peak0, total0, mixed0, o_weight)
+    )(owners, flat_q, kv, kv, peak0, total0, mixed0, o_weight)
 
 
 def shards(
@@ -208,9 +208,7 @@
     total0 = total.reshape(length, q_heads).T.reshape(rows, 1)
     mixed0 = mixed.reshape(length, q_heads, HD).transpose(1, 0, 2).reshape(rows, HD)
     which = req_prefix[0]
-    rowwise = prefix_kv.reshape(block, 2 * kv_heads * HD)
-    gathered = lax.all_gather(rowwise, "req", axis=0, tiled=True)
-    stacked = gathered.reshape(devices, block, 2 * kv_heads * HD)
+    stacked = lax.all_gather(prefix_kv, "req", axis=0, tiled=True)
     owners = lax.dynamic_slice_in_dim(block_owner, which * owned, owned)
     pieces_out = prefix_attention(
         owners, queries.reshape(length, q_heads * HD), stacked, peak0, total0, mixed0,

time: 182 us -> 190 us (1.044)
  Pallas kernels: 11 us -> 19.3 us
    pallas_call x1, Pallas kernels: 11 us -> 19.3 us  [prefix_attention(): pl.pallas_call(prefix_kernel, out_shape=jax.ShapeDtypeStruct((pieces, len...]
    unnamed x23 -> x18, local copies, waits for them, and re-layouts: 4.01 us -> 1.96 us
  transfers between devices with their start and end apart: 3 -> 3, of which waited for: 3 -> 3; matrix products, arithmetic and copies ran while one was open for 11% -> 12% of each run, Pallas kernels for 0% -> 0%
where the time goes in v8:
time: 190 us
  waiting for transfers between devices  116 us (61%)
  Pallas kernels  19.3 us (10%)
  starting transfers between devices  16.9 us (9%)
  between operations  14.9 us (8%)
  other arithmetic  10.2 us (5%)
  local copies, waits for them, and re-layouts  8.53 us (4%)
  matrix products  4.38 us (2%)
    all_gather x1, waiting for transfers between devices, shards(): stacked = lax.all_gather(prefix_kv, 'req', axis=0, tiled=True)  70 us
    all_to_all x1, waiting for transfers between devices, shards(): pieces_in = lax.all_to_all(spread, 'tp', 0, 0, tiled=True)  27.4 us
    pallas_call x1, Pallas kernels, prefix_attention(): pl.pallas_call(prefix_kernel, out_shape=jax.ShapeDtypeStruct((pieces, len...  19.3 us
    all_to_all x1, waiting for transfers between devices, shards(): lax.all_to_all(pieces_out, 'tp', 0, 0, tiled=True).astype(jnp.float32)  17.5 us
    all_to_all x1, starting transfers between devices, shards(): lax.all_to_all(pieces_out, 'tp', 0, 0, tiled=True).astype(jnp.float32)  10.6 us
    all_to_all x1, starting transfers between devices, shards(): pieces_in = lax.all_to_all(spread, 'tp', 0, 0, tiled=True)  6.35 us
  transfers between devices with their start and end apart: 3, of which 3 were waited for; matrix products, arithmetic and copies ran while one was open for 12% of the time, Pallas kernels for 0%

profile of v8, /device:TPU:1, one launch (start us, length us, event | category | flops | bytes accessed | tf_op | source)
XLA Modules:
  0.0 189.8 jit_solution(8231358040494000155)
XLA Ops:
  6.5 0.0 copy-start
  6.5 0.0 all-gather.2.cloned.1.call-start
  6.5 0.7 all-gather.2.cloned.1.call-update
  7.3 0.7 broadcast_in_dim.23
  7.9 0.1 pad.6.clone
  8.0 1.0 maximum_maximum_fusion
  9.0 1.3 broadcast_in_dim.25
  10.3 0.0 copy-start.2
  10.3 0.0 copy-start.3
  10.3 0.0 copy-start.4
  10.3 0.0 copy-start.5
  10.3 6.3 %all-to-all-start = ((bf16[8,144,640]{2,1,0:T(8,128)(2,1)}), bf16[8,144,640]{2,1,0:T(8,128)(2,1)S(1)}, u32[]{:S(2)}, u32[]{:S(2)}) async-start(bf16[8,144,640]{2,1,0:T(8,128)(2,1)} %broadcast_in_dim.25), calls=%async_computation | async-start | bytes 2949120 | tf_op jit(solution)/shard_map/all_to_all | solution.py:183
  16.7 0.0 copy-done.2
  16.7 0.0 copy-done.3
  16.7 0.0 copy-done.4
  17.4 0.0 copy-done.5
  17.4 0.7 dynamic_slice.3.own_ref
  18.1 0.3 multiply_cosine_fusion
  18.4 27.4 %all-to-all-done = bf16[8,144,640]{2,1,0:T(8,128)(2,1)S(1)} async-done(((bf16[8,144,640]{2,1,0:T(8,128)(2,1)}), bf16[8,144,640]{2,1,0:T(8,128)(2,1)S(1)}, u32[]{:S(2)}, u32[]{:S(2)}) %all-to-all-start) | async-done | bytes 1474592 | tf_op jit(solution)/shard_map/all_to_all | solution.py:183
  45.8 2.9 %copy.39 = bf16[8,144,640]{1,2,0:T(8,128)(2,1)} copy(bf16[8,144,640]{2,1,0:T(8,128)(2,1)S(1)} %all-to-all-done) | data formatting | bytes 2949120 | tf_op jit(solution)/shard_map/all_to_all | solution.py:183
  48.6 1.8 convert_reduce_fusion
  50.4 2.0 %multiply_reduce_fusion = f32[128]{0:T(128)S(1)} fusion(bf16[144,8,640]{0,2,1:T(8,128)(2,1)} %bitcast.67), kind=kLoop, calls=%fused_computation.5 | loop fusion | flops 1965952 | bytes 1311232 | tf_op jit(solution)/shard_map/reduce_sum | solution.py:187
  52.4 1.5 slice_convert_fusion
  53.9 0.0 copy-start.1
  54.0 2.2 %fusion.1 = bf16[128,5120]{0,1:T(8,128)(2,1)S(1)} fusion(f32[128,8,640]{0,2,1:T(8,128)S(1)} %slice_convert_fusion, f32[5120]{0:T(1024)S(1)} %reshape.219, f32[128]{0:T(128)S(1)} %add_rsqrt_fusion), kind=kLoop, calls=%fused_computation.2 | loop fusion | flops 1966080 | bytes 3953152 | tf_op jit(solution)/shard_map/convert_element_type | solution.py:188
  56.1 0.0 copy-done.1
  56.2 0.9 convolution_add_fusion
  57.1 0.1 copy.40
  57.2 0.1 copy.52
  57.4 0.1 copy.53
  57.5 0.1 multiply_subtract_fusion
  57.6 0.1 maximum_convert_fusion
  57.7 0.1 copy.43
  57.8 1.9 fusion.4
  59.7 0.2 fusion.25
  59.9 0.2 fusion.28
  60.1 0.1 fusion.9
  60.2 0.8 copy.57
  61.0 0.8 copy.55
  61.8 0.8 copy.46.q_ref
  62.6 0.0 copy-done
  62.6 1.4 fusion.7
  64.0 70.0 %all-gather.2.cloned.1.call-done.k0_ref.k1_ref = bf16[32768,2,128]{2,1,0:T(2,128)(2,1)} async-done(((bf16[1024,2,128]{2,1,0:T(2,128)(2,1)}), bf16[32768,2,128]{2,1,0:T(2,128)(2,1)}) %all-gather.2.cloned.1.call-update) | async-done | bytes 16777232 | tf_op jit(solution)/shard_map/all_gather | solution.py:211
  134.0 19.3 %shard_map.127 = bf16[8,128,640]{2,1,0:T(8,128)(2,1)} custom-call(s32[8]{0:T(128)} %dynamic_slice.3.own_ref, bf16[128,384]{1,0:T(8,128)(2,1)} %copy.46.q_ref, bf16[32768,2,128]{2,1,0:T(2,128)(2,1)} %all-gather.2.cloned.1.call-done.k0_ref.k1_ref, bf16[32768,2,128]{2,1,0:T(2,128)(2,1)} %all-gather.2.cloned.1.call-done.k0_ref.k1_ref, f32[384,1]{1,0:T(8,128)} %bitcast.71, ...), custom_call_target="tpu_custom_call" | custom-call | flops 1610612736 | bytes 9830400 | tf_op jit(solution)/shard_map/pallas_call | solution.py:123
  153.3 10.6 %all-to-all-start.1 = ((bf16[8,128,640]{2,1,0:T(8,128)(2,1)}), bf16[8,128,640]{2,1,0:T(8,128)(2,1)S(1)}, u32[]{:S(2)}, u32[]{:S(2)}) async-start(bf16[8,128,640]{2,1,0:T(8,128)(2,1)} %shard_map.127), calls=%async_computation.1 | async-start | bytes 2621440 | tf_op jit(solution)/shard_map/all_to_all | solution.py:217
  164.5 17.5 %all-to-all-done.1 = bf16[8,128,640]{2,1,0:T(8,128)(2,1)S(1)} async-done(((bf16[8,128,640]{2,1,0:T(8,128)(2,1)}), bf16[8,128,640]{2,1,0:T(8,128)(2,1)S(1)}, u32[]{:S(2)}, u32[]{:S(2)}) %all-to-all-start.1) | async-done | bytes 1310752 | tf_op jit(solution)/shard_map/all_to_all | solution.py:217
  182.0 0.2 convert_reduce_fusion.1
  182.2 0.8 select_convert_fusion
  (13 shorter events, 0.1 us)
Async XLA Ops:
  6.5 56.1 %copy-start = (bf16[5120,128]{1,0:T(8,128)(2,1)S(1)}, bf16[5120,128]{1,0:T(8,128)(2,1)}, u32[]{:S(2)}) copy-start(bf16[5120,128]{1,0:T(8,128)(2,1)} %param.19) | copy-start | bytes 3932164
  6.5 127.5 %all-gather.2.cloned.1.call-start = ((), (), s32[]{:S(2)}) async-start(), calls=%async_computation.2 | async-start | bytes 17301504 | tf_op jit(solution)/shard_map/all_gather | solution.py:211
  10.3 6.4 %copy-start.2 = (bf16[384]{0:T(512)(128)(2,1)S(1)}, bf16[384]{0:T(512)(128)(2,1)}, u32[]{:S(2)}) copy-start(bf16[384]{0:T(512)(128)(2,1)} %param.16) | copy-start | bytes 2308
  10.3 6.4 %copy-start.3 = (bf16[128]{0:T(256)(128)(2,1)S(1)}, bf16[128]{0:T(256)(128)(2,1)}, u32[]{:S(2)}) copy-start(bf16[128]{0:T(256)(128)(2,1)} %param.18) | copy-start | bytes 772
  10.3 6.4 %copy-start.4 = (bf16[128]{0:T(256)(128)(2,1)S(1)}, bf16[128]{0:T(256)(128)(2,1)}, u32[]{:S(2)}) copy-start(bf16[128]{0:T(256)(128)(2,1)} %param.20) | copy-start | bytes 772
  10.3 7.1 %copy-start.5 = (s32[32]{0:T(128)S(1)}, s32[32]{0:T(128)}, u32[]{:S(2)}) copy-start(s32[32]{0:T(128)} %param.25) | copy-start | bytes 388
  10.3 35.5 %all-to-all-start = ((bf16[8,144,640]{2,1,0:T(8,128)(2,1)}), bf16[8,144,640]{2,1,0:T(8,128)(2,1)S(1)}, u32[]{:S(2)}, u32[]{:S(2)}) async-start(bf16[8,144,640]{2,1,0:T(8,128)(2,1)} %broadcast_in_dim.25), calls=%async_computation | async-start | bytes 2949120 | tf_op jit(solution)/shard_map/all_to_all | solution.py:183
  53.9 2.2 %copy-start.1 = (bf16[5120,384]{1,0:T(8,128)(2,1)S(1)}, bf16[5120,384]{1,0:T(8,128)(2,1)}, u32[]{:S(2)}) copy-start(bf16[5120,384]{1,0:T(8,128)(2,1)} %param.15) | copy-start | bytes 11796484
  153.3 28.7 %all-to-all-start.1 = ((bf16[8,128,640]{2,1,0:T(8,128)(2,1)}), bf16[8,128,640]{2,1,0:T(8,128)(2,1)S(1)}, u32[]{:S(2)}, u32[]{:S(2)}) async-start(bf16[8,128,640]{2,1,0:T(8,128)(2,1)} %shard_map.127), calls=%async_computation.1 | async-start | bytes 2621440 | tf_op jit(solution)/shard_map/all_to_all | solution.py:217
Sparse Core Ops, SparseCore 0:
  9.9 124.0 all-gather.1

commit v9 on v6

--- a/solution.py
+++ b/solution.py
@@ -12,6 +12,7 @@
 THETA = 1000000.0
 EPSILON = 1e-06
 ROWS = 144
+PER_STEP = 4
 
 
 def rotate(heads, positions):
@@ -51,9 +52,9 @@
     return (peak, total, mixed)
 
 
-def prefix_kernel(
-    own_ref, q_ref, k_ref, v_ref, m0_ref, l0_ref, a0_ref, w_hbm, o_ref, m_sc, l_sc, acc_sc, w_sc, sem
-):
+def prefix_kernel(own_ref, q_ref, *refs):
+    kv_refs = refs[:2 * PER_STEP]
+    m0_ref, l0_ref, a0_ref, w_hbm, o_ref, m_sc, l_sc, acc_sc, q_sc, w_sc, sem = refs[2 * PER_STEP:]
     step = pl.program_id(0)
     group = q_ref.shape[1] // HD
     fetch = pltpu.make_async_copy(w_hbm, w_sc, sem.at[0])
@@ -64,23 +65,33 @@
         m_sc[...] = m0_ref[...]
         l_sc[...] = l0_ref[...]
         acc_sc[...] = a0_ref[...]
-
-    q = q_ref[...]
-    stacked = jnp.concatenate([q[:, h * HD:(h + 1) * HD] for h in range(group)], axis=0)
-    keys = k_ref[0]
-    values = v_ref[0]
-    scores = lax.dot_general(
-        stacked, keys, (((1,), (1,)), ((), ())), preferred_element_type=jnp.float32
-    ) * HD ** (-0.5)
+        q = q_ref[...]
+        q_sc[...] = jnp.concatenate([q[:, h * HD:(h + 1) * HD] for h in range(group)], axis=0)
+
+    stacked = q_sc[...]
+    dims = (((1,), (1,)), ((), ()))
+    refs = kv_refs
+    parts = [
+        lax.dot_general(stacked, refs[2 * i][0], dims, preferred_element_type=jnp.float32)
+        * HD ** (-0.5)
+        for i in range(len(refs) // 2)
+    ]
     old = m_sc[...]
-    new = jnp.maximum(old, jnp.max(scores, axis=-1, keepdims=True))
-    alpha = jnp.exp(old - new)
-    weights = jnp.exp(scores - new)
-    l_sc[...] = alpha * l_sc[...] + jnp.sum(weights, axis=-1, keepdims=True)
-    acc_sc[...] = alpha * acc_sc[...] + jnp.dot(
-        weights.astype(jnp.bfloat16), values, preferred_element_type=jnp.float32
-    )
-    m_sc[...] = new
+    top = old
+    for part in parts:
+        top = jnp.maximum(top, jnp.max(part, axis=-1, keepdims=True))
+    alpha = jnp.exp(old - top)
+    weights = [jnp.exp(part - top) for part in parts]
+    summed = weights[0].sum(axis=-1, keepdims=True)
+    mixed = jnp.dot(weights[0].astype(jnp.bfloat16), refs[1][0], preferred_element_type=jnp.float32)
+    for i in range(1, len(weights)):
+        summed = summed + weights[i].sum(axis=-1, keepdims=True)
+        mixed = mixed + jnp.dot(
+            weights[i].astype(jnp.bfloat16), refs[2 * i + 1][0], preferred_element_type=jnp.float32
+        )
+    l_sc[...] = alpha * l_sc[...] + summed
+    acc_sc[...] = alpha * acc_sc[...] + mixed
+    m_sc[...] = top
 
     @pl.when(step == pl.num_programs(0) - 1)
     def _():
@@ -112,11 +123,14 @@
         out_shape=jax.ShapeDtypeStruct((pieces, length, out_width // pieces), jnp.bfloat16),
         grid_spec=pltpu.PrefetchScalarGridSpec(
             num_scalar_prefetch=1,
-            grid=(steps,),
+            grid=(steps // PER_STEP,),
             in_specs=[
                 pl.BlockSpec((length, width), lambda j, own: (0, 0)),
-                pl.BlockSpec((1, block, HD), lambda j, own: (own[j], 0, 0)),
-                pl.BlockSpec((1, block, HD), lambda j, own: (own[j], 0, 1)),
+                *[
+                    pl.BlockSpec((1, block, HD), lambda j, own, i=i, c=c: (own[PER_STEP * j + i], 0, c))
+                    for i in range(PER_STEP)
+                    for c in range(2)
+                ],
                 pl.BlockSpec((rows, 1), lambda j, own: (0, 0)),
                 pl.BlockSpec((rows, 1), lambda j, own: (0, 0)),
                 pl.BlockSpec((rows, HD), lambda j, own: (0, 0)),
@@ -127,13 +141,14 @@
                 pltpu.VMEM((rows, 1), jnp.float32),
                 pltpu.VMEM((rows, 1), jnp.float32),
                 pltpu.VMEM((rows, HD), jnp.float32),
+                pltpu.VMEM((rows, HD), jnp.bfloat16),
                 pltpu.VMEM((width, out_width), jnp.bfloat16),
                 pltpu.SemaphoreType.DMA((1,)),
             ],
         ),
         compiler_params=pltpu.CompilerParams(dimension_semantics=("arbitrary",)),
         cost_estimate=cost,
-    )(owners, flat_q, kv, kv, peak0, total0, mixed0, o_weight)
+    )(owners, flat_q, *([kv] * (2 * PER_STEP)), peak0, total0, mixed0, o_weight)
 
 
 def shards(

time: 184 us -> 182 us (0.989)
  Pallas kernels: 13 us -> 10.9 us
    pallas_call x1, Pallas kernels: 13 us -> 10.9 us  [prefix_attention(): pl.pallas_call(prefix_kernel, out_shape=jax.ShapeDtypeStruct((pieces, len...]
where the time goes in v9:
time: 182 us; the launch traced here: 181 us
  waiting for transfers between devices  115 us (63%)
  starting transfers between devices  17.2 us (9%)
  between operations  14.9 us (8%)
  Pallas kernels  10.9 us (6%)
  local copies, waits for them, and re-layouts  9.79 us (5%)
  other arithmetic  9.26 us (5%)
  matrix products  4.39 us (2%)
    all_gather x1, waiting for transfers between devices, shards(): gathered = lax.all_gather(rowwise, 'req', axis=0, tiled=True)  70.8 us
    all_to_all x1, waiting for transfers between devices, shards(): pieces_in = lax.all_to_all(spread, 'tp', 0, 0, tiled=True)  26.5 us
    all_to_all x1, waiting for transfers between devices, shards(): lax.all_to_all(pieces_out, 'tp', 0, 0, tiled=True).astype(jnp.float32)  17.5 us
    pallas_call x1, Pallas kernels, prefix_attention(): pl.pallas_call(prefix_kernel, out_shape=jax.ShapeDtypeStruct((pieces, len...  10.9 us
    all_to_all x1, starting transfers between devices, shards(): lax.all_to_all(pieces_out, 'tp', 0, 0, tiled=True).astype(jnp.float32)  10.9 us
    all_to_all x1, starting transfers between devices, shards(): pieces_in = lax.all_to_all(spread, 'tp', 0, 0, tiled=True)  6.35 us
    unnamed x23, local copies, waits for them, and re-layouts  4.01 us
  transfers between devices with their start and end apart: 3, of which 3 were waited for; matrix products, arithmetic and copies ran while one was open for 11% of the time, Pallas kernels for 0%

profile of v9, /device:TPU:1, one launch (start us, length us, event | category | flops | bytes accessed | tf_op | source)
XLA Modules:
  0.0 181.3 jit_solution(15621199165034183418)
XLA Ops:
  6.5 0.0 copy-start
  6.5 0.0 copy-start.3
  6.5 0.0 copy-start.2
  6.5 0.0 all-gather.2.cloned.1.call-start
  6.5 2.0 %copy.62 = bf16[128,8,2,128]{3,1,2,0:T(8,128)(2,1)} copy(bf16[128,8,2,128]{3,2,1,0:T(2,128)(2,1)} %bitcast.87) | data formatting | bytes 1048576
  8.6 0.0 all-gather.2.cloned.1.call-update
  8.6 0.0 copy-done.3
  8.6 0.1 pad.6.clone
  8.7 0.0 copy-done.2
  8.7 0.1 maximum_maximum_fusion
  8.8 1.2 broadcast_in_dim.25
  10.1 6.3 %all-to-all-start = ((bf16[8,144,640]{2,1,0:T(8,128)(2,1)}), bf16[8,144,640]{2,1,0:T(8,128)(2,1)S(1)}, u32[]{:S(2)}, u32[]{:S(2)}) async-start(bf16[8,144,640]{2,1,0:T(8,128)(2,1)} %broadcast_in_dim.25), calls=%async_computation | async-start | bytes 2949120 | tf_op jit(solution)/shard_map/all_to_all | solution.py:184
  16.4 0.0 copy-done.4
  16.4 0.0 copy-done.5
  16.5 0.0 copy-done.6
  17.1 0.0 copy-done.7
  17.2 0.6 dynamic_slice.3.own_ref
  17.8 0.3 multiply_cosine_fusion
  18.1 26.5 %all-to-all-done = bf16[8,144,640]{2,1,0:T(8,128)(2,1)S(1)} async-done(((bf16[8,144,640]{2,1,0:T(8,128)(2,1)}), bf16[8,144,640]{2,1,0:T(8,128)(2,1)S(1)}, u32[]{:S(2)}, u32[]{:S(2)}) %all-to-all-start) | async-done | bytes 1474592 | tf_op jit(solution)/shard_map/all_to_all | solution.py:184
  44.6 2.9 %copy.39 = bf16[8,144,640]{1,2,0:T(8,128)(2,1)} copy(bf16[8,144,640]{2,1,0:T(8,128)(2,1)S(1)} %all-to-all-done) | data formatting | bytes 2949120 | tf_op jit(solution)/shard_map/all_to_all | solution.py:184
  47.5 1.7 convert_reduce_fusion
  49.2 2.0 %multiply_reduce_fusion = f32[128]{0:T(128)S(1)} fusion(bf16[144,8,640]{0,2,1:T(8,128)(2,1)} %bitcast.80), kind=kLoop, calls=%fused_computation.5 | loop fusion | flops 1965952 | bytes 1311232 | tf_op jit(solution)/shard_map/reduce_sum | solution.py:188
  51.2 1.5 slice_convert_fusion
  52.8 0.0 copy-start.1
  52.8 2.2 %fusion.1 = bf16[128,5120]{0,1:T(8,128)(2,1)S(1)} fusion(f32[128,8,640]{0,2,1:T(8,128)S(1)} %slice_convert_fusion, f32[5120]{0:T(1024)S(1)} %reshape.227, f32[128]{0:T(128)S(1)} %add_rsqrt_fusion), kind=kLoop, calls=%fused_computation.2 | loop fusion | flops 1966080 | bytes 3953152 | tf_op jit(solution)/shard_map/convert_element_type | solution.py:189
  55.0 0.0 copy-done.1
  55.0 0.9 convolution_add_fusion
  55.9 0.1 copy.40
  56.1 0.1 copy.52
  56.2 0.1 copy.53
  56.3 0.1 multiply_subtract_fusion
  56.4 0.1 maximum_convert_fusion
  56.5 0.1 copy.43
  56.6 1.9 %fusion.4 = f32[128,1,128]{0,2,1:T(8,128)S(1)} fusion(bf16[128,5120]{0,1:T(8,128)(2,1)S(1)} %fusion.1, bf16[5120,128]{1,0:T(8,128)(2,1)} %param.17, f32[128]{0:T(128)S(1)} %convert_element_type.88), kind=kOutput, calls=%fused_computation.13 | convolution fusion | flops 167788544 | bytes 2687488 | tf_op jit(solution)/shard_map/dot_general | solution.py:196
  58.5 0.2 fusion.25
  58.7 0.2 fusion.28
  58.9 0.1 fusion.9
  59.0 0.8 copy.58
  59.8 0.8 copy.56
  60.7 0.8 copy.46.q_ref
  61.4 0.0 copy-done
  61.4 1.4 fusion.7
  62.8 70.8 %all-gather.2.cloned.1.call-done = bf16[32768,256]{1,0:T(8,128)(2,1)} async-done(((bf16[1024,256]{1,0:T(8,128)(2,1)}), bf16[32768,256]{1,0:T(8,128)(2,1)}) %all-gather.2.cloned.1.call-update) | async-done | bytes 16777232 | tf_op jit(solution)/shard_map/all_gather | solution.py:213
  133.6 10.9 %shard_map.127 = bf16[8,128,640]{2,1,0:T(8,128)(2,1)} custom-call(s32[8]{0:T(128)} %dynamic_slice.3.own_ref, bf16[128,384]{1,0:T(8,128)(2,1)} %copy.46.q_ref, bf16[32,1024,256]{2,1,0:T(8,128)(2,1)} %bitcast.71, bf16[32,1024,256]{2,1,0:T(8,128)(2,1)} %bitcast.72, bf16[32,1024,256]{2,1,0:T(8,128)(2,1)} %bitcast.73, bf16[32,1024,256]{2,1,0:T(8,128)(2,1)} %bitcast.74, ...), custom_call_target="tpu_custom_call" | custom-call | flops 1610612736 | bytes 9830400 | tf_op jit(solution)/shard_map/pallas_call | solution.py:121
  144.5 10.9 %all-to-all-start.1 = ((bf16[8,128,640]{2,1,0:T(8,128)(2,1)}), bf16[8,128,640]{2,1,0:T(8,128)(2,1)S(1)}, u32[]{:S(2)}, u32[]{:S(2)}) async-start(bf16[8,128,640]{2,1,0:T(8,128)(2,1)} %shard_map.127), calls=%async_computation.1 | async-start | bytes 2621440 | tf_op jit(solution)/shard_map/all_to_all | solution.py:220
  156.0 17.5 %all-to-all-done.1 = bf16[8,128,640]{2,1,0:T(8,128)(2,1)S(1)} async-done(((bf16[8,128,640]{2,1,0:T(8,128)(2,1)}), bf16[8,128,640]{2,1,0:T(8,128)(2,1)S(1)}, u32[]{:S(2)}, u32[]{:S(2)}) %all-to-all-start.1) | async-done | bytes 1310752 | tf_op jit(solution)/shard_map/all_to_all | solution.py:220
  173.5 0.2 convert_reduce_fusion.1
  173.7 0.8 select_convert_fusion
  (18 shorter events, 0.1 us)
Async XLA Ops:
  6.5 54.9 %copy-start = (bf16[5120,128]{1,0:T(8,128)(2,1)S(1)}, bf16[5120,128]{1,0:T(8,128)(2,1)}, u32[]{:S(2)}) copy-start(bf16[5120,128]{1,0:T(8,128)(2,1)} %param.19) | copy-start | bytes 3932164
  6.5 2.1 %copy-start.3 = (bf16[640]{0:T(1024)(128)(2,1)S(1)}, bf16[640]{0:T(1024)(128)(2,1)}, u32[]{:S(2)}) copy-start(bf16[640]{0:T(1024)(128)(2,1)} %param.14) | copy-start | bytes 3844
  6.5 2.2 %copy-start.2 = (bf16[128,640]{1,0:T(8,128)(2,1)S(1)}, bf16[128,640]{1,0:T(8,128)(2,1)}, u32[]{:S(2)}) copy-start(bf16[128,640]{1,0:T(8,128)(2,1)} %param.13) | copy-start | bytes 491524
  6.5 127.1 %all-gather.2.cloned.1.call-start = ((), (), s32[]{:S(2)}) async-start(), calls=%async_computation.2 | async-start | bytes 17301504 | tf_op jit(solution)/shard_map/all_gather | solution.py:213
  10.1 6.4 %copy-start.4 = (bf16[384]{0:T(512)(128)(2,1)S(1)}, bf16[384]{0:T(512)(128)(2,1)}, u32[]{:S(2)}) copy-start(bf16[384]{0:T(512)(128)(2,1)} %param.16) | copy-start | bytes 2308
  10.1 6.4 %copy-start.5 = (bf16[128]{0:T(256)(128)(2,1)S(1)}, bf16[128]{0:T(256)(128)(2,1)}, u32[]{:S(2)}) copy-start(bf16[128]{0:T(256)(128)(2,1)} %param.18) | copy-start | bytes 772
  10.1 6.4 %copy-start.6 = (bf16[128]{0:T(256)(128)(2,1)S(1)}, bf16[128]{0:T(256)(128)(2,1)}, u32[]{:S(2)}) copy-start(bf16[128]{0:T(256)(128)(2,1)} %param.20) | copy-start | bytes 772
  10.1 7.1 %copy-start.7 = (s32[32]{0:T(128)S(1)}, s32[32]{0:T(128)}, u32[]{:S(2)}) copy-start(s32[32]{0:T(128)} %param.25) | copy-start | bytes 388
  10.1 34.5 %all-to-all-start = ((bf16[8,144,640]{2,1,0:T(8,128)(2,1)}), bf16[8,144,640]{2,1,0:T(8,128)(2,1)S(1)}, u32[]{:S(2)}, u32[]{:S(2)}) async-start(bf16[8,144,640]{2,1,0:T(8,128)(2,1)} %broadcast_in_dim.25), calls=%async_computation | async-start | bytes 2949120 | tf_op jit(solution)/shard_map/all_to_all | solution.py:184
  52.8 2.2 %copy-start.1 = (bf16[5120,384]{1,0:T(8,128)(2,1)S(1)}, bf16[5120,384]{1,0:T(8,128)(2,1)}, u32[]{:S(2)}) copy-start(bf16[5120,384]{1,0:T(8,128)(2,1)} %param.15) | copy-start | bytes 11796484
  144.5 29.0 %all-to-all-start.1 = ((bf16[8,128,640]{2,1,0:T(8,128)(2,1)}), bf16[8,128,640]{2,1,0:T(8,128)(2,1)S(1)}, u32[]{:S(2)}, u32[]{:S(2)}) async-start(bf16[8,128,640]{2,1,0:T(8,128)(2,1)} %shard_map.127), calls=%async_computation.1 | async-start | bytes 2621440 | tf_op jit(solution)/shard_map/all_to_all | solution.py:220
Sparse Core Ops, SparseCore 0:
  9.9 123.6 all-gather.1

commit v10 on v9

--- a/solution.py
+++ b/solution.py
@@ -180,8 +180,15 @@
         [hidden_in, norm_gain[None, :], jnp.zeros((ROWS - length - 1, feat), hidden_in.dtype)],
         axis=0,
     )
-    spread = jnp.broadcast_to(packed[None], (n_tp,) + packed.shape)
-    pieces_in = lax.all_to_all(spread, "tp", 0, 0, tiled=True)
+    me_tp = lax.axis_index("tp")
+    by_shift = jnp.stack(
+        [packed]
+        + [
+            lax.ppermute(packed, "tp", [(i, (i + s) % n_tp) for i in range(n_tp)])
+            for s in range(1, n_tp)
+        ]
+    )
+    pieces_in = jnp.take(by_shift, (me_tp - jnp.arange(n_tp, dtype=jnp.int32)) % n_tp, axis=0)
     full = pieces_in.transpose(1, 0, 2).reshape(ROWS, n_tp * feat)
     tokens = full[:length].astype(jnp.float32)
     gain = full[length]

time: 182 us -> 179 us (0.984)
  waiting for transfers between devices: 115 us -> 102 us
  starting transfers between devices: 17.2 us -> 22.5 us
  local copies, waits for them, and re-layouts: 9.79 us -> 14.7 us
    all_to_all x1 -> x0, waiting for transfers between devices: 26.5 us -> none  [shards(): pieces_in = lax.all_to_all(spread, 'tp', 0, 0, tiled=True)]
    ppermute x0 -> x7, waiting for transfers between devices: none -> 15.2 us  [shards(): lax.ppermute(packed, 'tp', [(i, (i + s) % n_tp) for i in range(n_tp)])]
    ppermute x0 -> x7, starting transfers between devices: none -> 11.3 us  [shards(): lax.ppermute(packed, 'tp', [(i, (i + s) % n_tp) for i in range(n_tp)])]
    all_to_all x1 -> x0, starting transfers between devices: 6.35 us -> none  [shards(): pieces_in = lax.all_to_all(spread, 'tp', 0, 0, tiled=True)]
    unnamed x23 -> x31, local copies, waits for them, and re-layouts: 4.01 us -> 7.84 us
    convert_element_type x1, local copies, waits for them, and re-layouts: 0.01 us -> 3.25 us  [shards(): tokens = full[:length].astype(jnp.float32)]
    all_to_all x1 -> x0, local copies, waits for them, and re-layouts: 2.86 us -> none  [shards(): pieces_in = lax.all_to_all(spread, 'tp', 0, 0, tiled=True)]
    gather x0 -> x1, local copies, waits for them, and re-layouts: none -> 1.85 us  [shards(): jnp.take(by_shift, (me_tp - jnp.arange(n_tp, dtype=jnp.int32)) % n_tp, ax...]
  transfers between devices with their start and end apart: 3 -> 9, of which waited for: 3 -> 5; matrix products, arithmetic and copies ran while one was open for 11% -> 14% of each run, Pallas kernels for 0% -> 0%
where the time goes in v10:
time: 179 us
  waiting for transfers between devices  102 us (57%)
  starting transfers between devices  22.5 us (13%)
  between operations  15 us (8%)
  local copies, waits for them, and re-layouts  14.7 us (8%)
  Pallas kernels  10.9 us (6%)
  other arithmetic  9.72 us (5%)
  matrix products  4.37 us (2%)
    all_gather x1, waiting for transfers between devices, shards(): gathered = lax.all_gather(rowwise, 'req', axis=0, tiled=True)  69.2 us
    all_to_all x1, waiting for transfers between devices, shards(): lax.all_to_all(pieces_out, 'tp', 0, 0, tiled=True).astype(jnp.float32)  17.5 us
    ppermute x7, waiting for transfers between devices, shards(): lax.ppermute(packed, 'tp', [(i, (i + s) % n_tp) for i in range(n_tp)])  15.2 us
    ppermute x7, starting transfers between devices, shards(): lax.ppermute(packed, 'tp', [(i, (i + s) % n_tp) for i in range(n_tp)])  11.3 us
    all_to_all x1, starting transfers between devices, shards(): lax.all_to_all(pieces_out, 'tp', 0, 0, tiled=True).astype(jnp.float32)  11.1 us
    pallas_call x1, Pallas kernels, prefix_attention(): pl.pallas_call(prefix_kernel, out_shape=jax.ShapeDtypeStruct((pieces, len...  10.9 us
    unnamed x31, local copies, waits for them, and re-layouts  7.84 us
    convert_element_type x1, other arithmetic, shards(): (tokens * lax.rsqrt(meansq + EPSILON) * gain.astype(jnp.float32)).astype(...  3.63 us
  transfers between devices with their start and end apart: 9, of which 5 were waited for; matrix products, arithmetic and copies ran while one was open for 14% of the time, Pallas kernels for 0%

profile of v10, /device:TPU:1, one launch (start us, length us, event | category | flops | bytes accessed | tf_op | source)
XLA Modules:
  0.0 179.0 jit_solution(8528491319399881176)
XLA Ops:
  6.6 0.0 all-gather.2.cloned.1.call-start
  6.6 2.1 %copy.51 = bf16[128,8,2,128]{3,1,2,0:T(8,128)(2,1)} copy(bf16[128,8,2,128]{3,2,1,0:T(2,128)(2,1)} %bitcast.104) | data formatting | bytes 1048576
  8.7 0.1 pad.6.clone
  8.8 0.1 maximum_maximum_fusion
  8.9 2.5 %collective-permute-start = (bf16[144,640]{1,0:T(8,128)(2,1)S(1)}, bf16[144,640]{1,0:T(8,128)(2,1)}, u32[]{:S(2)}, u32[]{:S(2)}) collective-permute-start(bf16[144,640]{1,0:T(8,128)(2,1)S(1)} %maximum_maximum_fusion), channel_id=1, source_target_pairs={{0,1},{1,2},{2,3},{3,4},{4,5},{5,6},{6,7},{7,0},{8,9},{9,10},{10,1... | collective-permute-start | bytes 552968 | tf_op jit(solution)/shard_map/ppermute | solution.py:187
  11.5 1.2 collective-permute-start.1
  12.7 1.4 collective-permute-start.2
  14.1 1.7 collective-permute-start.3
  15.8 3.2 %collective-permute-start.4 = (bf16[144,640]{1,0:T(8,128)(2,1)S(1)}, bf16[144,640]{1,0:T(8,128)(2,1)S(1)}, u32[]{:S(2)}, u32[]{:S(2)}) collective-permute-start(bf16[144,640]{1,0:T(8,128)(2,1)S(1)} %maximum_maximum_fusion), channel_id=1, source_target_pairs={{0,5},{1,6},{2,7},{3,0},{4,1},{5,2},{6,3},{7,4},{8,13},{9,14},{10,... | collective-permute-start | bytes 552968 | tf_op jit(solution)/shard_map/ppermute | solution.py:187
  19.0 0.5 convert_element_type.89
  20.2 0.6 dynamic_slice.3.own_ref
  20.9 0.1 bitcast_dynamic-update-slice_fusion.7
  21.0 0.3 multiply_cosine_fusion
  21.3 1.2 collective-permute-start.5
  22.6 0.9 bitcast_dynamic-update-slice_fusion.6
  23.5 3.2 %collective-permute-done.1 = bf16[144,640]{1,0:T(8,128)(2,1)} collective-permute-done((bf16[144,640]{1,0:T(8,128)(2,1)S(1)}, bf16[144,640]{1,0:T(8,128)(2,1)}, u32[]{:S(2)}, u32[]{:S(2)}) %collective-permute-start.1) | collective-permute-done | bytes 184352 | tf_op jit(solution)/shard_map/ppermute | solution.py:187
  26.8 1.0 bitcast_dynamic-update-slice_fusion.5
  27.7 0.9 bitcast_dynamic-update-slice_fusion.4
  28.7 2.8 %collective-permute-done.3 = bf16[144,640]{1,0:T(8,128)(2,1)} collective-permute-done((bf16[144,640]{1,0:T(8,128)(2,1)S(1)}, bf16[144,640]{1,0:T(8,128)(2,1)}, u32[]{:S(2)}, u32[]{:S(2)}) %collective-permute-start.3) | collective-permute-done | bytes 184352 | tf_op jit(solution)/shard_map/ppermute | solution.py:187
  31.4 1.0 bitcast_dynamic-update-slice_fusion.3
  32.5 9.2 %collective-permute-done.6 = bf16[144,640]{1,0:T(8,128)(2,1)S(1)} collective-permute-done((bf16[144,640]{1,0:T(8,128)(2,1)S(1)}, bf16[144,640]{1,0:T(8,128)(2,1)S(1)}, u32[]{:S(2)}, u32[]{:S(2)}) %collective-permute-start.6) | collective-permute-done | bytes 184352 | tf_op jit(solution)/shard_map/ppermute | solution.py:187
  41.7 1.8 %gather_fusion = bf16[8,144,640]{2,1,0:T(8,128)(2,1)} fusion(bf16[8,144,640]{2,1,0:T(8,128)(2,1)S(1)} %bitcast_dynamic-update-slice_fusion, s32[1024]{0:T(1024)S(1)} %pad_clamp_fusion), kind=kCustom, calls=%fused_computation | custom fusion | bytes 2949152 | tf_op jit(solution)/shard_map/jit(_take)/gather | solution.py:191
  43.6 1.6 select_bitcast_fusion
  45.2 1.7 slice_convert_fusion
  46.9 3.3 %copy.28 = f32[128,8,640]{0,2,1:T(8,128)} copy(f32[128,8,640]{2,0,1:T(8,128)} %slice_convert_fusion) | data formatting | bytes 5242880 | tf_op jit(solution)/shard_map/convert_element_type | solution.py:193
  50.1 0.3 multiply_reduce_fusion
  50.5 3.6 %fusion.1 = bf16[128,5120]{0,1:T(8,128)(2,1)S(1)} fusion(f32[128,8,640]{0,2,1:T(8,128)} %copy.28, f32[5120]{0:T(1024)S(1)} %bitcast.106, f32[128]{0:T(128)S(1)} %add_rsqrt_fusion), kind=kLoop, calls=%fused_computation.3 | loop fusion | flops 1966080 | bytes 3953152 | tf_op jit(solution)/shard_map/convert_element_type | solution.py:196
  54.1 0.9 convolution_add_fusion
  55.1 0.1 copy.29
  55.2 0.1 copy.41
  55.3 0.1 copy.42
  55.5 0.1 multiply_subtract_fusion
  55.5 0.1 maximum_convert_fusion
  55.6 0.1 copy.32
  55.8 1.9 %fusion.4 = f32[128,1,128]{0,2,1:T(8,128)S(1)} fusion(bf16[128,5120]{0,1:T(8,128)(2,1)S(1)} %fusion.1, bf16[5120,128]{1,0:T(8,128)(2,1)} %param.17, f32[128]{0:T(128)S(1)} %convert_element_type.88), kind=kOutput, calls=%fused_computation.14 | convolution fusion | flops 167788544 | bytes 2687488 | tf_op jit(solution)/shard_map/dot_general | solution.py:203
  57.7 0.2 fusion.25
  57.9 0.2 fusion.31
  58.1 0.1 fusion.9
  58.2 0.8 copy.47
  59.0 0.8 copy.45
  59.8 0.8 copy.35.q_ref
  60.6 1.4 fusion.7
  61.9 69.2 %all-gather.2.cloned.1.call-done = bf16[32768,256]{1,0:T(8,128)(2,1)} async-done(((bf16[1024,256]{1,0:T(8,128)(2,1)}), bf16[32768,256]{1,0:T(8,128)(2,1)}) %all-gather.2.cloned.1.call-update) | async-done | bytes 16777232 | tf_op jit(solution)/shard_map/all_gather | solution.py:220
  131.1 10.9 %shard_map.127 = bf16[8,128,640]{2,1,0:T(8,128)(2,1)} custom-call(s32[8]{0:T(128)} %dynamic_slice.3.own_ref, bf16[128,384]{1,0:T(8,128)(2,1)} %copy.35.q_ref, bf16[32,1024,256]{2,1,0:T(8,128)(2,1)} %bitcast.91, bf16[32,1024,256]{2,1,0:T(8,128)(2,1)} %bitcast.92, bf16[32,1024,256]{2,1,0:T(8,128)(2,1)} %bitcast.93, bf16[32,1024,256]{2,1,0:T(8,128)(2,1)} %bitcast.94, ...), custom_call_target="tpu_custom_call" | custom-call | flops 1610612736 | bytes 9830400 | tf_op jit(solution)/shard_map/pallas_call | solution.py:121
  142.0 11.1 %all-to-all-start = ((bf16[8,128,640]{2,1,0:T(8,128)(2,1)}), bf16[8,128,640]{2,1,0:T(8,128)(2,1)S(1)}, u32[]{:S(2)}, u32[]{:S(2)}) async-start(bf16[8,128,640]{2,1,0:T(8,128)(2,1)} %shard_map.127), calls=%async_computation | async-start | bytes 2621440 | tf_op jit(solution)/shard_map/all_to_all | solution.py:227
  153.8 17.5 %all-to-all-done = bf16[8,128,640]{2,1,0:T(8,128)(2,1)S(1)} async-done(((bf16[8,128,640]{2,1,0:T(8,128)(2,1)}), bf16[8,128,640]{2,1,0:T(8,128)(2,1)S(1)}, u32[]{:S(2)}, u32[]{:S(2)}) %all-to-all-start) | async-done | bytes 1310752 | tf_op jit(solution)/shard_map/all_to_all | solution.py:227
  171.3 0.2 convert_reduce_fusion
  171.4 0.8 select_convert_fusion
  (43 shorter events, 0.3 us)
Async XLA Ops:
  6.5 54.0 %copy-start = (bf16[5120,128]{1,0:T(8,128)(2,1)S(1)}, bf16[5120,128]{1,0:T(8,128)(2,1)}, u32[]{:S(2)}) copy-start(bf16[5120,128]{1,0:T(8,128)(2,1)} %param.19) | copy-start | bytes 3932164
  6.5 2.2 %copy-start.3 = (bf16[640]{0:T(1024)(128)(2,1)S(1)}, bf16[640]{0:T(1024)(128)(2,1)}, u32[]{:S(2)}) copy-start(bf16[640]{0:T(1024)(128)(2,1)} %param.14) | copy-start | bytes 3844
  6.5 2.3 %copy-start.2 = (bf16[128,640]{1,0:T(8,128)(2,1)S(1)}, bf16[128,640]{1,0:T(8,128)(2,1)}, u32[]{:S(2)}) copy-start(bf16[128,640]{1,0:T(8,128)(2,1)} %param.13) | copy-start | bytes 491524
  6.5 12.4 %copy-start.4 = (bf16[384]{0:T(512)(128)(2,1)S(1)}, bf16[384]{0:T(512)(128)(2,1)}, u32[]{:S(2)}) copy-start(bf16[384]{0:T(512)(128)(2,1)} %param.16) | copy-start | bytes 2308
  6.5 12.4 %copy-start.6 = (bf16[128]{0:T(256)(128)(2,1)S(1)}, bf16[128]{0:T(256)(128)(2,1)}, u32[]{:S(2)}) copy-start(bf16[128]{0:T(256)(128)(2,1)} %param.18) | copy-start | bytes 772
  6.5 12.5 %copy-start.7 = (bf16[128]{0:T(256)(128)(2,1)S(1)}, bf16[128]{0:T(256)(128)(2,1)}, u32[]{:S(2)}) copy-start(bf16[128]{0:T(256)(128)(2,1)} %param.20) | copy-start | bytes 772
  6.6 13.6 %copy-start.8 = (s32[32]{0:T(128)S(1)}, s32[32]{0:T(128)}, u32[]{:S(2)}) copy-start(s32[32]{0:T(128)} %param.25) | copy-start | bytes 388
  6.6 124.6 %all-gather.2.cloned.1.call-start = ((), (), s32[]{:S(2)}) async-start(), calls=%async_computation.1 | async-start | bytes 17301504 | tf_op jit(solution)/shard_map/all_gather | solution.py:220
  8.9 12.4 %collective-permute-start = (bf16[144,640]{1,0:T(8,128)(2,1)S(1)}, bf16[144,640]{1,0:T(8,128)(2,1)}, u32[]{:S(2)}, u32[]{:S(2)}) collective-permute-start(bf16[144,640]{1,0:T(8,128)(2,1)S(1)} %maximum_maximum_fusion), channel_id=1, source_target_pairs={{0,1},{1,2},{2,3},{3,4},{4,5},{5,6},{6,7},{7,0},{8,9},{9,10},{10,1... | collective-permute-start | bytes 552968 | tf_op jit(solution)/shard_map/ppermute | solution.py:187
  11.5 15.3 %collective-permute-start.1 = (bf16[144,640]{1,0:T(8,128)(2,1)S(1)}, bf16[144,640]{1,0:T(8,128)(2,1)}, u32[]{:S(2)}, u32[]{:S(2)}) collective-permute-start(bf16[144,640]{1,0:T(8,128)(2,1)S(1)} %maximum_maximum_fusion), channel_id=1, source_target_pairs={{0,2},{1,3},{2,4},{3,5},{4,6},{5,7},{6,0},{7,1},{8,10},{9,11},{10,... | collective-permute-start | bytes 552968 | tf_op jit(solution)/shard_map/ppermute | solution.py:187
  12.7 15.1 %collective-permute-start.2 = (bf16[144,640]{1,0:T(8,128)(2,1)S(1)}, bf16[144,640]{1,0:T(8,128)(2,1)}, u32[]{:S(2)}, u32[]{:S(2)}) collective-permute-start(bf16[144,640]{1,0:T(8,128)(2,1)S(1)} %maximum_maximum_fusion), channel_id=1, source_target_pairs={{0,3},{1,4},{2,5},{3,6},{4,7},{5,0},{6,1},{7,2},{8,11},{9,12},{10,... | collective-permute-start | bytes 552968 | tf_op jit(solution)/shard_map/ppermute | solution.py:187
  14.1 17.4 %collective-permute-start.3 = (bf16[144,640]{1,0:T(8,128)(2,1)S(1)}, bf16[144,640]{1,0:T(8,128)(2,1)}, u32[]{:S(2)}, u32[]{:S(2)}) collective-permute-start(bf16[144,640]{1,0:T(8,128)(2,1)S(1)} %maximum_maximum_fusion), channel_id=1, source_target_pairs={{0,4},{1,5},{2,6},{3,7},{4,0},{5,1},{6,2},{7,3},{8,12},{9,13},{10,... | collective-permute-start | bytes 552968 | tf_op jit(solution)/shard_map/ppermute | solution.py:187
  15.8 16.6 %collective-permute-start.4 = (bf16[144,640]{1,0:T(8,128)(2,1)S(1)}, bf16[144,640]{1,0:T(8,128)(2,1)S(1)}, u32[]{:S(2)}, u32[]{:S(2)}) collective-permute-start(bf16[144,640]{1,0:T(8,128)(2,1)S(1)} %maximum_maximum_fusion), channel_id=1, source_target_pairs={{0,5},{1,6},{2,7},{3,0},{4,1},{5,2},{6,3},{7,4},{8,13},{9,14},{10,... | collective-permute-start | bytes 552968 | tf_op jit(solution)/shard_map/ppermute | solution.py:187
  21.3 11.1 %collective-permute-start.5 = (bf16[144,640]{1,0:T(8,128)(2,1)S(1)}, bf16[144,640]{1,0:T(8,128)(2,1)S(1)}, u32[]{:S(2)}, u32[]{:S(2)}) collective-permute-start(bf16[144,640]{1,0:T(8,128)(2,1)S(1)} %maximum_maximum_fusion), channel_id=1, source_target_pairs={{0,6},{1,7},{2,0},{3,1},{4,2},{5,3},{6,4},{7,5},{8,14},{9,15},{10,... | collective-permute-start | bytes 552968 | tf_op jit(solution)/shard_map/ppermute | solution.py:187
  26.8 15.0 %collective-permute-start.6 = (bf16[144,640]{1,0:T(8,128)(2,1)S(1)}, bf16[144,640]{1,0:T(8,128)(2,1)S(1)}, u32[]{:S(2)}, u32[]{:S(2)}) collective-permute-start(bf16[144,640]{1,0:T(8,128)(2,1)S(1)} %maximum_maximum_fusion), channel_id=1, source_target_pairs={{0,7},{1,0},{2,1},{3,2},{4,3},{5,4},{6,5},{7,6},{8,15},{9,8},{10,9... | collective-permute-start | bytes 552968 | tf_op jit(solution)/shard_map/ppermute | solution.py:187
  50.5 3.7 %copy-start.1 = (bf16[5120,384]{1,0:T(8,128)(2,1)S(1)}, bf16[5120,384]{1,0:T(8,128)(2,1)}, u32[]{:S(2)}) copy-start(bf16[5120,384]{1,0:T(8,128)(2,1)} %param.15) | copy-start | bytes 11796484
  55.8 4.8 %copy-start.5 = (f32[128]{0:T(128)S(1)}, f32[128]{0:T(128)}, u32[]{:S(2)}) copy-start(f32[128]{0:T(128)} %convert_element_type.89) | copy-start | bytes 1540
  142.0 29.2 %all-to-all-start = ((bf16[8,128,640]{2,1,0:T(8,128)(2,1)}), bf16[8,128,640]{2,1,0:T(8,128)(2,1)S(1)}, u32[]{:S(2)}, u32[]{:S(2)}) async-start(bf16[8,128,640]{2,1,0:T(8,128)(2,1)} %shard_map.127), calls=%async_computation | async-start | bytes 2621440 | tf_op jit(solution)/shard_map/all_to_all | solution.py:227
Sparse Core Ops, SparseCore 0:
  10.0 121.1 all-gather.1

commit v11 on v10

--- a/solution.py
+++ b/solution.py
@@ -224,7 +224,12 @@
         owners, queries.reshape(length, q_heads * HD), stacked, peak0, total0, mixed0,
         o_weight, n_tp,
     )
-    summed = jnp.sum(lax.all_to_all(pieces_out, "tp", 0, 0, tiled=True).astype(jnp.float32), axis=0)
+    rotated = jnp.take(pieces_out, (me_tp + jnp.arange(n_tp, dtype=jnp.int32)) % n_tp, axis=0)
+    summed = rotated[0].astype(jnp.float32)
+    for s in range(1, n_tp):
+        summed = summed + lax.ppermute(
+            rotated[s], "tp", [(i, (i + s) % n_tp) for i in range(n_tp)]
+        ).astype(jnp.float32)
     valid = slot_index < suffix_len[0]
     return jnp.where(valid[:, None], summed, jnp.float32(0.0)).astype(jnp.bfloat16)
 

time: 179 us -> 182 us (1.017); the launches traced: 179 us -> 179 us
  waiting for transfers between devices: 102 us -> 82.6 us
  starting transfers between devices: 22.5 us -> 38.6 us
  local copies, waits for them, and re-layouts: 14.7 us -> 16.9 us
    ppermute x0 -> x7, starting transfers between devices: none -> 27.3 us  [shards(): lax.ppermute(rotated[s], 'tp', [(i, (i + s) % n_tp) for i in range(n_tp)])]
    all_to_all x1 -> x0, waiting for transfers between devices: 17.5 us -> none  [shards(): lax.all_to_all(pieces_out, 'tp', 0, 0, tiled=True).astype(jnp.float32)]
    all_to_all x1 -> x0, starting transfers between devices: 11.1 us -> none  [shards(): lax.all_to_all(pieces_out, 'tp', 0, 0, tiled=True).astype(jnp.float32)]
    all_gather x1, waiting for transfers between devices: 69.2 us -> 61.7 us  [shards(): gathered = lax.all_gather(rowwise, 'req', axis=0, tiled=True)]
    ppermute x0 -> x7, waiting for transfers between devices: none -> 6.89 us  [shards(): lax.ppermute(rotated[s], 'tp', [(i, (i + s) % n_tp) for i in range(n_tp)])]
    gather x0 -> x1, local copies, waits for them, and re-layouts: none -> 2.1 us  [shards(): jnp.take(pieces_out, (me_tp + jnp.arange(n_tp, dtype=jnp.int32)) % n_tp,...]
    unnamed x31 -> x35, local copies, waits for them, and re-layouts: 7.84 us -> 7.81 us
  transfers between devices with their start and end apart: 9 -> 15, of which waited for: 5 -> 8; matrix products, arithmetic and copies ran while one was open for 14% -> 15% of each run, Pallas kernels for 0% -> 0%
where the time goes in v11:
time: 182 us; the launch traced here: 179 us
  waiting for transfers between devices  82.6 us (45%)
  starting transfers between devices  38.6 us (21%)
  local copies, waits for them, and re-layouts  16.9 us (9%)
  between operations  15.1 us (8%)
  other arithmetic  11 us (6%)
  Pallas kernels  10.9 us (6%)
  matrix products  4.39 us (2%)
    all_gather x1, waiting for transfers between devices, shards(): gathered = lax.all_gather(rowwise, 'req', axis=0, tiled=True)  61.7 us
    ppermute x7, starting transfers between devices, shards(): lax.ppermute(rotated[s], 'tp', [(i, (i + s) % n_tp) for i in range(n_tp)])  27.3 us
    ppermute x7, waiting for transfers between devices, shards(): lax.ppermute(packed, 'tp', [(i, (i + s) % n_tp) for i in range(n_tp)])  14 us
    ppermute x7, starting transfers between devices, shards(): lax.ppermute(packed, 'tp', [(i, (i + s) % n_tp) for i in range(n_tp)])  11.3 us
    pallas_call x1, Pallas kernels, prefix_attention(): pl.pallas_call(prefix_kernel, out_shape=jax.ShapeDtypeStruct((pieces, len...  10.9 us
    unnamed x35, local copies, waits for them, and re-layouts  7.81 us
    ppermute x7, waiting for transfers between devices, shards(): lax.ppermute(rotated[s], 'tp', [(i, (i + s) % n_tp) for i in range(n_tp)])  6.89 us
  transfers between devices with their start and end apart: 15, of which 8 were waited for; matrix products, arithmetic and copies ran while one was open for 15% of the time, Pallas kernels for 0%

profile of v11, /device:TPU:1, one launch (start us, length us, event | category | flops | bytes accessed | tf_op | source)
XLA Modules:
  0.0 179.4 jit_solution(11569730223433608335)
XLA Ops:
  6.6 2.0 %copy.51 = bf16[128,8,2,128]{3,1,2,0:T(8,128)(2,1)} copy(bf16[128,8,2,128]{3,2,1,0:T(2,128)(2,1)} %bitcast.125) | data formatting | bytes 1048576
  8.9 2.5 %collective-permute-start = (bf16[144,640]{1,0:T(8,128)(2,1)S(1)}, bf16[144,640]{1,0:T(8,128)(2,1)}, u32[]{:S(2)}, u32[]{:S(2)}) collective-permute-start(bf16[144,640]{1,0:T(8,128)(2,1)S(1)} %maximum_maximum_fusion), channel_id=1, source_target_pairs={{0,1},{1,2},{2,3},{3,4},{4,5},{5,6},{6,7},{7,0},{8,9},{9,10},{10,1... | collective-permute-start | bytes 552968 | tf_op jit(solution)/shard_map/ppermute | solution.py:187
  11.4 1.2 collective-permute-start.1
  12.6 1.4 collective-permute-start.2
  14.0 1.7 collective-permute-start.3
  15.7 3.2 %collective-permute-start.4 = (bf16[144,640]{1,0:T(8,128)(2,1)S(1)}, bf16[144,640]{1,0:T(8,128)(2,1)S(1)}, u32[]{:S(2)}, u32[]{:S(2)}) collective-permute-start(bf16[144,640]{1,0:T(8,128)(2,1)S(1)} %maximum_maximum_fusion), channel_id=1, source_target_pairs={{0,5},{1,6},{2,7},{3,0},{4,1},{5,2},{6,3},{7,4},{8,13},{9,14},{10,... | collective-permute-start | bytes 552968 | tf_op jit(solution)/shard_map/ppermute | solution.py:187
  19.0 0.5 convert_element_type.112
  19.5 0.6 convert_element_type.113
  20.7 0.6 dynamic_slice.3.own_ref
  21.4 0.6 compare_and_fusion.1
  22.1 0.3 multiply_cosine_fusion
  22.4 1.2 collective-permute-start.5
  23.6 0.9 bitcast_dynamic-update-slice_fusion.6
  24.6 2.1 %collective-permute-done.1 = bf16[144,640]{1,0:T(8,128)(2,1)} collective-permute-done((bf16[144,640]{1,0:T(8,128)(2,1)S(1)}, bf16[144,640]{1,0:T(8,128)(2,1)}, u32[]{:S(2)}, u32[]{:S(2)}) %collective-permute-start.1) | collective-permute-done | bytes 184352 | tf_op jit(solution)/shard_map/ppermute | solution.py:187
  26.7 1.0 bitcast_dynamic-update-slice_fusion.5
  27.7 0.9 bitcast_dynamic-update-slice_fusion.4
  28.6 2.7 %collective-permute-done.3 = bf16[144,640]{1,0:T(8,128)(2,1)} collective-permute-done((bf16[144,640]{1,0:T(8,128)(2,1)S(1)}, bf16[144,640]{1,0:T(8,128)(2,1)}, u32[]{:S(2)}, u32[]{:S(2)}) %collective-permute-start.3) | collective-permute-done | bytes 184352 | tf_op jit(solution)/shard_map/ppermute | solution.py:187
  31.4 1.0 bitcast_dynamic-update-slice_fusion.3
  32.4 9.1 %collective-permute-done.6 = bf16[144,640]{1,0:T(8,128)(2,1)S(1)} collective-permute-done((bf16[144,640]{1,0:T(8,128)(2,1)S(1)}, bf16[144,640]{1,0:T(8,128)(2,1)S(1)}, u32[]{:S(2)}, u32[]{:S(2)}) %collective-permute-start.6) | collective-permute-done | bytes 184352 | tf_op jit(solution)/shard_map/ppermute | solution.py:187
  41.6 1.9 %gather_fusion = bf16[8,144,640]{2,1,0:T(8,128)(2,1)} fusion(bf16[8,144,640]{2,1,0:T(8,128)(2,1)S(1)} %bitcast_dynamic-update-slice_fusion, s32[1024]{0:T(1024)S(1)} %pad_clamp_fusion.1), kind=kCustom, calls=%fused_computation | custom fusion | bytes 2949152 | tf_op jit(solution)/shard_map/jit(_take)/gather | solution.py:191
  43.4 1.6 select_bitcast_fusion
  45.0 1.7 slice_convert_fusion
  46.7 3.3 %copy.28 = f32[128,8,640]{0,2,1:T(8,128)} copy(f32[128,8,640]{2,0,1:T(8,128)} %slice_convert_fusion) | data formatting | bytes 5242880 | tf_op jit(solution)/shard_map/convert_element_type | solution.py:193
  50.0 0.3 multiply_reduce_fusion
  50.4 3.6 %fusion.1 = bf16[128,5120]{0,1:T(8,128)(2,1)S(1)} fusion(f32[128,8,640]{0,2,1:T(8,128)} %copy.28, f32[5120]{0:T(1024)S(1)} %bitcast.127, f32[128]{0:T(128)S(1)} %add_rsqrt_fusion), kind=kLoop, calls=%fused_computation.4 | loop fusion | flops 1966080 | bytes 3953152 | tf_op jit(solution)/shard_map/convert_element_type | solution.py:196
  54.0 0.9 convolution_add_fusion
  55.2 0.1 copy.42
  55.7 1.9 %fusion.4 = f32[128,1,128]{0,2,1:T(8,128)S(1)} fusion(bf16[128,5120]{0,1:T(8,128)(2,1)S(1)} %fusion.1, bf16[5120,128]{1,0:T(8,128)(2,1)} %param.17, f32[128]{0:T(128)S(1)} %copy-done.5), kind=kOutput, calls=%fused_computation.15 | convolution fusion | flops 167788544 | bytes 2687488 | tf_op jit(solution)/shard_map/dot_general | solution.py:203
  57.6 0.2 fusion.33
  57.8 0.2 fusion.42
  58.1 0.8 copy.47
  58.9 0.8 copy.45
  59.7 0.8 copy.35.q_ref
  60.5 1.4 fusion.7
  61.9 61.7 %all-gather.2.cloned.1.call-done = bf16[32768,256]{1,0:T(8,128)(2,1)} async-done(((bf16[1024,256]{1,0:T(8,128)(2,1)}), bf16[32768,256]{1,0:T(8,128)(2,1)}) %all-gather.2.cloned.1.call-update) | async-done | bytes 16777232 | tf_op jit(solution)/shard_map/all_gather | solution.py:220
  123.5 10.9 %shard_map.127 = bf16[8,128,640]{2,1,0:T(8,128)(2,1)} custom-call(s32[8]{0:T(128)} %dynamic_slice.3.own_ref, bf16[128,384]{1,0:T(8,128)(2,1)} %copy.35.q_ref, bf16[32,1024,256]{2,1,0:T(8,128)(2,1)} %bitcast.112, bf16[32,1024,256]{2,1,0:T(8,128)(2,1)} %bitcast.113, bf16[32,1024,256]{2,1,0:T(8,128)(2,1)} %bitcast.114, bf16[32,1024,256]{2,1,0:T(8,128)(2,1)} %bitcast.115, ...), custom_call_target="tpu_custom_call" | custom-call | flops 1610612736 | bytes 9830400 | tf_op jit(solution)/shard_map/pallas_call | solution.py:121
  134.4 2.1 %gather_fusion.1 = bf16[8,128,640]{2,1,0:T(8,128)(2,1)S(1)} fusion(bf16[8,128,640]{2,1,0:T(8,128)(2,1)} %shard_map.127, s32[1024]{0:T(1024)S(1)} %pad_clamp_fusion), kind=kCustom, calls=%fused_computation.1 | custom fusion | bytes 2621472 | tf_op jit(solution)/shard_map/jit(_take)/gather | solution.py:227
  136.5 0.2 broadcast_select_fusion
  136.9 2.5 %collective-permute-start.10 = (bf16[128,640]{1,0:T(8,128)(2,1)S(1)}, bf16[128,640]{1,0:T(8,128)(2,1)S(1)}, u32[]{:S(2)}, u32[]{:S(2)}) collective-permute-start(bf16[128,640]{1,0:T(8,128)(2,1)S(1)} %get-tuple-element.9), channel_id=1, source_target_pairs={{0,4},{1,5},{2,6},{3,7},{4,0},{5,1},{6,2},{7,3},{8,12},{9,13},{10,... | collective-permute-start | bytes 491528 | tf_op jit(solution)/shard_map/ppermute | solution.py:230
  139.3 14.9 %collective-permute-start.11 = (bf16[128,640]{1,0:T(8,128)(2,1)S(1)}, bf16[128,640]{1,0:T(8,128)(2,1)S(1)}, u32[]{:S(2)}, u32[]{:S(2)}) collective-permute-start(bf16[128,640]{1,0:T(8,128)(2,1)S(1)} %get-tuple-element.8), channel_id=1, source_target_pairs={{0,5},{1,6},{2,7},{3,0},{4,1},{5,2},{6,3},{7,4},{8,13},{9,14},{10,... | collective-permute-start | bytes 491528 | tf_op jit(solution)/shard_map/ppermute | solution.py:230
  154.2 2.5 %collective-permute-start.12 = (bf16[128,640]{1,0:T(8,128)(2,1)S(1)}, bf16[128,640]{1,0:T(8,128)(2,1)S(1)}, u32[]{:S(2)}, u32[]{:S(2)}) collective-permute-start(bf16[128,640]{1,0:T(8,128)(2,1)S(1)} %get-tuple-element.7), channel_id=1, source_target_pairs={{0,6},{1,7},{2,0},{3,1},{4,2},{5,3},{6,4},{7,5},{8,14},{9,15},{10,... | collective-permute-start | bytes 491528 | tf_op jit(solution)/shard_map/ppermute | solution.py:230
  156.7 1.5 collective-permute-start.7
  158.2 0.2 collective-permute-done.11
  158.4 6.0 %collective-permute-start.9 = (bf16[128,640]{1,0:T(8,128)(2,1)S(1)}, bf16[128,640]{1,0:T(8,128)(2,1)S(1)}, u32[]{:S(2)}, u32[]{:S(2)}) collective-permute-start(bf16[128,640]{1,0:T(8,128)(2,1)S(1)} %get-tuple-element.10), channel_id=1, source_target_pairs={{0,3},{1,4},{2,5},{3,6},{4,7},{5,0},{6,1},{7,2},{8,11},{9,12},{10,... | collective-permute-start | bytes 491528 | tf_op jit(solution)/shard_map/ppermute | solution.py:230
  165.1 0.1 collective-permute-done.7
  165.2 2.6 %collective-permute-done.8 = bf16[128,640]{1,0:T(8,128)(2,1)S(1)} collective-permute-done((bf16[128,640]{1,0:T(8,128)(2,1)S(1)}, bf16[128,640]{1,0:T(8,128)(2,1)S(1)}, u32[]{:S(2)}, u32[]{:S(2)}) %collective-permute-start.8) | collective-permute-done | bytes 163872 | tf_op jit(solution)/shard_map/ppermute | solution.py:230
  167.8 3.9 %collective-permute-done.9 = bf16[128,640]{1,0:T(8,128)(2,1)S(1)} collective-permute-done((bf16[128,640]{1,0:T(8,128)(2,1)S(1)}, bf16[128,640]{1,0:T(8,128)(2,1)S(1)}, u32[]{:S(2)}, u32[]{:S(2)}) %collective-permute-start.9) | collective-permute-done | bytes 163872 | tf_op jit(solution)/shard_map/ppermute | solution.py:230
  171.7 0.9 fusion.15
  (64 shorter events, 1.3 us)
Async XLA Ops:
  6.5 53.9 %copy-start = (bf16[5120,128]{1,0:T(8,128)(2,1)S(1)}, bf16[5120,128]{1,0:T(8,128)(2,1)}, u32[]{:S(2)}) copy-start(bf16[5120,128]{1,0:T(8,128)(2,1)} %param.19) | copy-start | bytes 3932164
  6.5 2.1 %copy-start.3 = (bf16[640]{0:T(1024)(128)(2,1)S(1)}, bf16[640]{0:T(1024)(128)(2,1)}, u32[]{:S(2)}) copy-start(bf16[640]{0:T(1024)(128)(2,1)} %param.14) | copy-start | bytes 3844
  6.5 2.2 %copy-start.2 = (bf16[128,640]{1,0:T(8,128)(2,1)S(1)}, bf16[128,640]{1,0:T(8,128)(2,1)}, u32[]{:S(2)}) copy-start(bf16[128,640]{1,0:T(8,128)(2,1)} %param.13) | copy-start | bytes 491524
  6.5 12.4 %copy-start.4 = (bf16[384]{0:T(512)(128)(2,1)S(1)}, bf16[384]{0:T(512)(128)(2,1)}, u32[]{:S(2)}) copy-start(bf16[384]{0:T(512)(128)(2,1)} %param.16) | copy-start | bytes 2308
  6.5 12.4 %copy-start.8 = (bf16[128]{0:T(256)(128)(2,1)S(1)}, bf16[128]{0:T(256)(128)(2,1)}, u32[]{:S(2)}) copy-start(bf16[128]{0:T(256)(128)(2,1)} %param.18) | copy-start | bytes 772
  6.5 12.9 %copy-start.9 = (bf16[128]{0:T(256)(128)(2,1)S(1)}, bf16[128]{0:T(256)(128)(2,1)}, u32[]{:S(2)}) copy-start(bf16[128]{0:T(256)(128)(2,1)} %param.20) | copy-start | bytes 772
  6.6 14.2 %copy-start.10 = (s32[32]{0:T(128)S(1)}, s32[32]{0:T(128)}, u32[]{:S(2)}) copy-start(s32[32]{0:T(128)} %param.25) | copy-start | bytes 388
  6.6 117.0 %all-gather.2.cloned.1.call-start = ((), (), s32[]{:S(2)}) async-start(), calls=%async_computation | async-start | bytes 17301504 | tf_op jit(solution)/shard_map/all_gather | solution.py:220
  8.9 13.5 %collective-permute-start = (bf16[144,640]{1,0:T(8,128)(2,1)S(1)}, bf16[144,640]{1,0:T(8,128)(2,1)}, u32[]{:S(2)}, u32[]{:S(2)}) collective-permute-start(bf16[144,640]{1,0:T(8,128)(2,1)S(1)} %maximum_maximum_fusion), channel_id=1, source_target_pairs={{0,1},{1,2},{2,3},{3,4},{4,5},{5,6},{6,7},{7,0},{8,9},{9,10},{10,1... | collective-permute-start | bytes 552968 | tf_op jit(solution)/shard_map/ppermute | solution.py:187
  11.4 15.3 %collective-permute-start.1 = (bf16[144,640]{1,0:T(8,128)(2,1)S(1)}, bf16[144,640]{1,0:T(8,128)(2,1)}, u32[]{:S(2)}, u32[]{:S(2)}) collective-permute-start(bf16[144,640]{1,0:T(8,128)(2,1)S(1)} %maximum_maximum_fusion), channel_id=1, source_target_pairs={{0,2},{1,3},{2,4},{3,5},{4,6},{5,7},{6,0},{7,1},{8,10},{9,11},{10,... | collective-permute-start | bytes 552968 | tf_op jit(solution)/shard_map/ppermute | solution.py:187
  12.6 15.1 %collective-permute-start.2 = (bf16[144,640]{1,0:T(8,128)(2,1)S(1)}, bf16[144,640]{1,0:T(8,128)(2,1)}, u32[]{:S(2)}, u32[]{:S(2)}) collective-permute-start(bf16[144,640]{1,0:T(8,128)(2,1)S(1)} %maximum_maximum_fusion), channel_id=1, source_target_pairs={{0,3},{1,4},{2,5},{3,6},{4,7},{5,0},{6,1},{7,2},{8,11},{9,12},{10,... | collective-permute-start | bytes 552968 | tf_op jit(solution)/shard_map/ppermute | solution.py:187
  14.0 17.4 %collective-permute-start.3 = (bf16[144,640]{1,0:T(8,128)(2,1)S(1)}, bf16[144,640]{1,0:T(8,128)(2,1)}, u32[]{:S(2)}, u32[]{:S(2)}) collective-permute-start(bf16[144,640]{1,0:T(8,128)(2,1)S(1)} %maximum_maximum_fusion), channel_id=1, source_target_pairs={{0,4},{1,5},{2,6},{3,7},{4,0},{5,1},{6,2},{7,3},{8,12},{9,13},{10,... | collective-permute-start | bytes 552968 | tf_op jit(solution)/shard_map/ppermute | solution.py:187
  15.7 16.6 %collective-permute-start.4 = (bf16[144,640]{1,0:T(8,128)(2,1)S(1)}, bf16[144,640]{1,0:T(8,128)(2,1)S(1)}, u32[]{:S(2)}, u32[]{:S(2)}) collective-permute-start(bf16[144,640]{1,0:T(8,128)(2,1)S(1)} %maximum_maximum_fusion), channel_id=1, source_target_pairs={{0,5},{1,6},{2,7},{3,0},{4,1},{5,2},{6,3},{7,4},{8,13},{9,14},{10,... | collective-permute-start | bytes 552968 | tf_op jit(solution)/shard_map/ppermute | solution.py:187
  22.4 10.0 %collective-permute-start.5 = (bf16[144,640]{1,0:T(8,128)(2,1)S(1)}, bf16[144,640]{1,0:T(8,128)(2,1)S(1)}, u32[]{:S(2)}, u32[]{:S(2)}) collective-permute-start(bf16[144,640]{1,0:T(8,128)(2,1)S(1)} %maximum_maximum_fusion), channel_id=1, source_target_pairs={{0,6},{1,7},{2,0},{3,1},{4,2},{5,3},{6,4},{7,5},{8,14},{9,15},{10,... | collective-permute-start | bytes 552968 | tf_op jit(solution)/shard_map/ppermute | solution.py:187
  26.7 14.8 %collective-permute-start.6 = (bf16[144,640]{1,0:T(8,128)(2,1)S(1)}, bf16[144,640]{1,0:T(8,128)(2,1)S(1)}, u32[]{:S(2)}, u32[]{:S(2)}) collective-permute-start(bf16[144,640]{1,0:T(8,128)(2,1)S(1)} %maximum_maximum_fusion), channel_id=1, source_target_pairs={{0,7},{1,0},{2,1},{3,2},{4,3},{5,4},{6,5},{7,6},{8,15},{9,8},{10,9... | collective-permute-start | bytes 552968 | tf_op jit(solution)/shard_map/ppermute | solution.py:187
  50.4 3.7 %copy-start.1 = (bf16[5120,384]{1,0:T(8,128)(2,1)S(1)}, bf16[5120,384]{1,0:T(8,128)(2,1)}, u32[]{:S(2)}) copy-start(bf16[5120,384]{1,0:T(8,128)(2,1)} %param.15) | copy-start | bytes 11796484
  55.0 0.7 copy-start.5
  55.7 4.8 %copy-start.6 = (f32[128]{0:T(128)S(1)}, f32[128]{0:T(128)}, u32[]{:S(2)}) copy-start(f32[128]{0:T(128)} %convert_element_type.113) | copy-start | bytes 1540
  134.4 2.1 %copy-start.7 = (pred[8]{0:T(512)(128)(4,1)S(1)}, pred[8]{0:T(512)(128)(4,1)}, u32[]{:S(2)}) copy-start(pred[8]{0:T(512)(128)(4,1)} %compare_and_fusion.1) | copy-start | bytes 28
  136.9 21.3 %collective-permute-start.10 = (bf16[128,640]{1,0:T(8,128)(2,1)S(1)}, bf16[128,640]{1,0:T(8,128)(2,1)S(1)}, u32[]{:S(2)}, u32[]{:S(2)}) collective-permute-start(bf16[128,640]{1,0:T(8,128)(2,1)S(1)} %get-tuple-element.9), channel_id=1, source_target_pairs={{0,4},{1,5},{2,6},{3,7},{4,0},{5,1},{6,2},{7,3},{8,12},{9,13},{10,... | collective-permute-start | bytes 491528 | tf_op jit(solution)/shard_map/ppermute | solution.py:230
  139.3 19.0 %collective-permute-start.11 = (bf16[128,640]{1,0:T(8,128)(2,1)S(1)}, bf16[128,640]{1,0:T(8,128)(2,1)S(1)}, u32[]{:S(2)}, u32[]{:S(2)}) collective-permute-start(bf16[128,640]{1,0:T(8,128)(2,1)S(1)} %get-tuple-element.8), channel_id=1, source_target_pairs={{0,5},{1,6},{2,7},{3,0},{4,1},{5,2},{6,3},{7,4},{8,13},{9,14},{10,... | collective-permute-start | bytes 491528 | tf_op jit(solution)/shard_map/ppermute | solution.py:230
  154.2 10.8 %collective-permute-start.12 = (bf16[128,640]{1,0:T(8,128)(2,1)S(1)}, bf16[128,640]{1,0:T(8,128)(2,1)S(1)}, u32[]{:S(2)}, u32[]{:S(2)}) collective-permute-start(bf16[128,640]{1,0:T(8,128)(2,1)S(1)} %get-tuple-element.7), channel_id=1, source_target_pairs={{0,6},{1,7},{2,0},{3,1},{4,2},{5,3},{6,4},{7,5},{8,14},{9,15},{10,... | collective-permute-start | bytes 491528 | tf_op jit(solution)/shard_map/ppermute | solution.py:230
  156.7 8.4 %collective-permute-start.13 = (bf16[128,640]{1,0:T(8,128)(2,1)S(1)}, bf16[128,640]{1,0:T(8,128)(2,1)S(1)}, u32[]{:S(2)}, u32[]{:S(2)}) collective-permute-start(bf16[128,640]{1,0:T(8,128)(2,1)S(1)} %get-tuple-element.6), channel_id=1, source_target_pairs={{0,7},{1,0},{2,1},{3,2},{4,3},{5,4},{6,5},{7,6},{8,15},{9,8},{10,9... | collective-permute-start | bytes 491528 | tf_op jit(solution)/shard_map/ppermute | solution.py:230
  156.7 8.5 %collective-permute-start.7 = (bf16[128,640]{1,0:T(8,128)(2,1)S(1)}, bf16[128,640]{1,0:T(8,128)(2,1)S(1)}, u32[]{:S(2)}, u32[]{:S(2)}) collective-permute-start(bf16[128,640]{1,0:T(8,128)(2,1)S(1)} %get-tuple-element.5), channel_id=1, source_target_pairs={{0,1},{1,2},{2,3},{3,4},{4,5},{5,6},{6,7},{7,0},{8,9},{9,10},{10,1... | collective-permute-start | bytes 491528 | tf_op jit(solution)/shard_map/ppermute | solution.py:230
  158.2 9.6 %collective-permute-start.8 = (bf16[128,640]{1,0:T(8,128)(2,1)S(1)}, bf16[128,640]{1,0:T(8,128)(2,1)S(1)}, u32[]{:S(2)}, u32[]{:S(2)}) collective-permute-start(bf16[128,640]{1,0:T(8,128)(2,1)S(1)} %get-tuple-element.11), channel_id=1, source_target_pairs={{0,2},{1,3},{2,4},{3,5},{4,6},{5,7},{6,0},{7,1},{8,10},{9,11},{10,... | collective-permute-start | bytes 491528 | tf_op jit(solution)/shard_map/ppermute | solution.py:230
  158.4 13.3 %collective-permute-start.9 = (bf16[128,640]{1,0:T(8,128)(2,1)S(1)}, bf16[128,640]{1,0:T(8,128)(2,1)S(1)}, u32[]{:S(2)}, u32[]{:S(2)}) collective-permute-start(bf16[128,640]{1,0:T(8,128)(2,1)S(1)} %get-tuple-element.10), channel_id=1, source_target_pairs={{0,3},{1,4},{2,5},{3,6},{4,7},{5,0},{6,1},{7,2},{8,11},{9,12},{10,... | collective-permute-start | bytes 491528 | tf_op jit(solution)/shard_map/ppermute | solution.py:230
Sparse Core Ops, SparseCore 0:
  10.0 113.5 all-gather.1

commit v12 on v10

--- a/solution.py
+++ b/solution.py
@@ -181,14 +181,20 @@
         axis=0,
     )
     me_tp = lax.axis_index("tp")
-    by_shift = jnp.stack(
-        [packed]
+    swapped = lax.ppermute(packed, "tp", [(i, i ^ 1) for i in range(n_tp)])
+    low = me_tp % 2 == 0
+    pair = jnp.stack([jnp.where(low, packed, swapped), jnp.where(low, swapped, packed)])
+    n_x = n_tp // 2
+    along = jnp.stack(
+        [pair]
         + [
-            lax.ppermute(packed, "tp", [(i, (i + s) % n_tp) for i in range(n_tp)])
-            for s in range(1, n_tp)
+            lax.ppermute(pair, "tp", [(i, (i + 2 * u) % n_tp) for i in range(n_tp)])
+            for u in range(1, n_x)
         ]
     )
-    pieces_in = jnp.take(by_shift, (me_tp - jnp.arange(n_tp, dtype=jnp.int32)) % n_tp, axis=0)
+    me_x = me_tp // 2
+    ordered = jnp.take(along, (me_x - jnp.arange(n_x, dtype=jnp.int32)) % n_x, axis=0)
+    pieces_in = ordered.reshape((n_tp,) + packed.shape)
     full = pieces_in.transpose(1, 0, 2).reshape(ROWS, n_tp * feat)
     tokens = full[:length].astype(jnp.float32)
     gain = full[length]

time: 179 us -> 175 us (0.978)
  waiting for transfers between devices: 102 us -> 94.5 us
  other arithmetic: 9.72 us -> 13.2 us
    all_gather x1, waiting for transfers between devices: 69.2 us -> 63.5 us  [shards(): gathered = lax.all_gather(rowwise, 'req', axis=0, tiled=True)]
    gather x1 -> x2, local copies, waits for them, and re-layouts: 1.85 us -> 6.05 us  [shards(): jnp.take(along, (me_x - jnp.arange(n_x, dtype=jnp.int32)) % n_x, axis=0)]
    convert_element_type x1, local copies, waits for them, and re-layouts: 3.25 us -> 0.01 us  [shards(): gain.astype(jnp.float32)]
    ppermute x7 -> x4, starting transfers between devices: 11.3 us -> 8.38 us  [the longest x3 5.83 us: shards(): lax.ppermute(pair, 'tp', [(i, (i + 2 * u) % n_tp) for i in range(n_tp)])]
    all_to_all x1, starting transfers between devices: 11.1 us -> 13.5 us  [shards(): lax.all_to_all(pieces_out, 'tp', 0, 0, tiled=True).astype(jnp.float32)]
    ppermute x7 -> x4, waiting for transfers between devices: 15.2 us -> 13.5 us  [the longest x3 10.3 us: shards(): lax.ppermute(pair, 'tp', [(i, (i + 2 * u) % n_tp) for i in range(n_tp)])]
    unnamed x31 -> x39, local copies, waits for them, and re-layouts: 7.84 us -> 6.27 us
  transfers between devices with their start and end apart: 9 -> 6, of which waited for: 5 -> 5; matrix products, arithmetic and copies ran while one was open for 14% -> 15% of each run, Pallas kernels for 0% -> 0%
where the time goes in v12:
time: 175 us
  waiting for transfers between devices  94.5 us (54%)
  starting transfers between devices  21.9 us (13%)
  between operations  15 us (9%)
  local copies, waits for them, and re-layouts  14.7 us (8%)
  other arithmetic  13.2 us (8%)
  Pallas kernels  10.9 us (6%)
  matrix products  4.37 us (2%)
    all_gather x1, waiting for transfers between devices, shards(): gathered = lax.all_gather(rowwise, 'req', axis=0, tiled=True)  63.5 us
    all_to_all x1, waiting for transfers between devices, shards(): lax.all_to_all(pieces_out, 'tp', 0, 0, tiled=True).astype(jnp.float32)  17.5 us
    all_to_all x1, starting transfers between devices, shards(): lax.all_to_all(pieces_out, 'tp', 0, 0, tiled=True).astype(jnp.float32)  13.5 us
    pallas_call x1, Pallas kernels, prefix_attention(): pl.pallas_call(prefix_kernel, out_shape=jax.ShapeDtypeStruct((pieces, len...  10.9 us
    ppermute x3, waiting for transfers between devices, shards(): lax.ppermute(pair, 'tp', [(i, (i + 2 * u) % n_tp) for i in range(n_tp)])  10.3 us
    unnamed x39, local copies, waits for them, and re-layouts  6.27 us
    gather x2, local copies, waits for them, and re-layouts, shards(): jnp.take(along, (me_x - jnp.arange(n_x, dtype=jnp.int32)) % n_x, axis=0)  6.05 us
    ppermute x3, starting transfers between devices, shards(): lax.ppermute(pair, 'tp', [(i, (i + 2 * u) % n_tp) for i in range(n_tp)])  5.83 us
  transfers between devices with their start and end apart: 6, of which 5 were waited for; matrix products, arithmetic and copies ran while one was open for 15% of the time, Pallas kernels for 0%

profile of v12, /device:TPU:1, one launch (start us, length us, event | category | flops | bytes accessed | tf_op | source)
XLA Modules:
  0.0 174.6 jit_solution(7074248750112817794)
XLA Ops:
  6.5 2.0 %copy.52 = bf16[128,8,2,128]{3,1,2,0:T(8,128)(2,1)} copy(bf16[128,8,2,128]{3,2,1,0:T(2,128)(2,1)} %bitcast.100) | data formatting | bytes 1048576
  8.7 0.1 pad.12.clone
  8.7 0.1 maximum_maximum_fusion
  8.8 2.6 %collective-permute-start = (bf16[144,640]{1,0:T(8,128)(2,1)S(1)}, bf16[144,640]{1,0:T(8,128)(2,1)S(1)}, u32[]{:S(2)}, u32[]{:S(2)}) collective-permute-start(bf16[144,640]{1,0:T(8,128)(2,1)S(1)} %maximum_maximum_fusion), channel_id=1, source_target_pairs={{0,1},{1,0},{2,3},{3,2},{4,5},{5,4},{6,7},{7,6},{8,9},{9,8},{10,11... | collective-permute-start | bytes 552968 | tf_op jit(solution)/shard_map/ppermute | solution.py:184
  11.4 3.3 %collective-permute-done = bf16[144,640]{1,0:T(8,128)(2,1)S(1)} collective-permute-done((bf16[144,640]{1,0:T(8,128)(2,1)S(1)}, bf16[144,640]{1,0:T(8,128)(2,1)S(1)}, u32[]{:S(2)}, u32[]{:S(2)}) %collective-permute-start) | collective-permute-done | bytes 184352 | tf_op jit(solution)/shard_map/ppermute | solution.py:184
  14.7 0.2 select_bitcast_fusion.1
  14.9 0.1 fusion.30
  14.9 2.2 %collective-permute-start.1 = (bf16[2,144,640]{2,1,0:T(8,128)(2,1)S(1)}, bf16[2,144,640]{2,1,0:T(8,128)(2,1)S(1)}, u32[]{:S(2)}, u32[]{:S(2)}) collective-permute-start(bf16[2,144,640]{2,1,0:T(8,128)(2,1)S(1)} %get-tuple-element.8), channel_id=1, source_target_pairs={{0,2},{1,3},{2,4},{3,5},{4,6},{5,7},{6,0},{7,1},{8,10},{9,11},{10,... | collective-permute-start | bytes 1105928 | tf_op jit(solution)/shard_map/ppermute | solution.py:191
  17.2 2.5 %collective-permute-start.2 = (bf16[2,144,640]{2,1,0:T(8,128)(2,1)S(1)}, bf16[2,144,640]{2,1,0:T(8,128)(2,1)S(1)}, u32[]{:S(2)}, u32[]{:S(2)}) collective-permute-start(bf16[2,144,640]{2,1,0:T(8,128)(2,1)S(1)} %get-tuple-element.8), channel_id=1, source_target_pairs={{0,4},{1,5},{2,6},{3,7},{4,0},{5,1},{6,2},{7,3},{8,12},{9,13},{10,... | collective-permute-start | bytes 1105928 | tf_op jit(solution)/shard_map/ppermute | solution.py:191
  19.6 1.2 collective-permute-start.3
  20.8 0.1 broadcast_in_dim.63
  20.8 0.6 broadcast_in_dim.64
  21.4 0.5 convert_element_type.88
  22.0 0.5 convert_element_type.89
  23.1 0.6 dynamic_slice.3.own_ref
  23.8 1.0 multiply_cosine_fusion
  24.8 10.1 %collective-permute-done.2 = bf16[2,144,640]{2,1,0:T(8,128)(2,1)S(1)} collective-permute-done((bf16[2,144,640]{2,1,0:T(8,128)(2,1)S(1)}, bf16[2,144,640]{2,1,0:T(8,128)(2,1)S(1)}, u32[]{:S(2)}, u32[]{:S(2)}) %collective-permute-start.2) | collective-permute-done | bytes 368672 | tf_op jit(solution)/shard_map/ppermute | solution.py:191
  34.9 0.1 collective-permute-done.3
  35.0 0.6 copy-done.4
  35.6 0.2 copy-done.5
  35.8 1.3 pad_maximum_fusion
  37.1 1.9 %gather_fusion = bf16[4,2,144,640]{3,2,1,0:T(8,128)(2,1)} fusion(bf16[4,2,144,640]{3,2,1,0:T(8,128)(2,1)S(1)} %pad_maximum_fusion, s32[1024]{0:T(1024)S(1)} %pad_clamp_fusion), kind=kCustom, calls=%fused_computation | custom fusion | bytes 2949136 | tf_op jit(solution)/shard_map/jit(_take)/gather | solution.py:196
  39.0 4.2 %copy.29 = bf16[4,2,144,640]{2,3,1,0:T(8,128)(2,1)} copy(bf16[4,2,144,640]{3,2,1,0:T(8,128)(2,1)} %gather_fusion) | data formatting | bytes 2949120 | tf_op jit(solution)/shard_map/jit(_take)/gather | solution.py:196
  43.2 2.1 %bitcast_select_fusion = bf16[8,144,640]{1,2,0:T(8,128)(2,1)S(1)} fusion(bf16[4,2,144,640]{2,3,1,0:T(8,128)(2,1)} %copy.29, pred[8]{0:T(512)(128)(4,1)S(1)} %copy-done.12), kind=kLoop, calls=%fused_computation.4 | loop fusion | flops 737280 | bytes 2949128 | tf_op jit(solution)/shard_map/jit(_take)/select_n | solution.py:196
  45.3 1.5 copy-done.1
  46.7 0.4 convert_reduce_fusion
  47.2 2.0 %multiply_reduce_fusion = f32[128]{0:T(128)S(1)} fusion(bf16[144,8,640]{0,2,1:T(8,128)(2,1)} %bitcast.93), kind=kLoop, calls=%fused_computation.7 | loop fusion | flops 1965952 | bytes 1311232 | tf_op jit(solution)/shard_map/reduce_sum | solution.py:201
  49.2 1.5 slice_convert_fusion
  50.7 2.2 %fusion.1 = bf16[128,5120]{0,1:T(8,128)(2,1)S(1)} fusion(f32[128,8,640]{0,2,1:T(8,128)S(1)} %slice_convert_fusion, f32[5120]{0:T(1024)S(1)} %reshape.283, f32[128]{0:T(128)S(1)} %add_rsqrt_fusion), kind=kLoop, calls=%fused_computation.3 | loop fusion | flops 1966080 | bytes 3953152 | tf_op jit(solution)/shard_map/convert_element_type | solution.py:202
  52.9 0.9 convolution_add_fusion
  53.9 0.1 copy.30
  54.0 0.1 copy.42
  54.2 0.1 copy.43
  54.4 0.1 maximum_convert_fusion
  54.5 0.1 copy.33
  54.6 1.9 %fusion.4 = f32[128,1,128]{0,2,1:T(8,128)S(1)} fusion(bf16[128,5120]{0,1:T(8,128)(2,1)S(1)} %fusion.1, bf16[5120,128]{1,0:T(8,128)(2,1)} %param.17, f32[128]{0:T(128)S(1)} %copy-done.10), kind=kOutput, calls=%fused_computation.16 | convolution fusion | flops 167788544 | bytes 2687488 | tf_op jit(solution)/shard_map/dot_general | solution.py:209
  56.5 0.2 fusion.25
  56.7 0.2 fusion.32
  57.0 0.8 copy.48
  57.8 0.8 copy.46
  58.7 0.8 copy.36.q_ref
  59.4 1.4 fusion.7
  60.8 63.5 %all-gather.2.cloned.1.call-done = bf16[32768,256]{1,0:T(8,128)(2,1)} async-done(((bf16[1024,256]{1,0:T(8,128)(2,1)}), bf16[32768,256]{1,0:T(8,128)(2,1)}) %all-gather.2.cloned.1.call-update) | async-done | bytes 16777232 | tf_op jit(solution)/shard_map/all_gather | solution.py:226
  124.3 10.9 %shard_map.127 = bf16[8,128,640]{2,1,0:T(8,128)(2,1)} custom-call(s32[8]{0:T(128)} %dynamic_slice.3.own_ref, bf16[128,384]{1,0:T(8,128)(2,1)} %copy.36.q_ref, bf16[32,1024,256]{2,1,0:T(8,128)(2,1)} %bitcast.84, bf16[32,1024,256]{2,1,0:T(8,128)(2,1)} %bitcast.85, bf16[32,1024,256]{2,1,0:T(8,128)(2,1)} %bitcast.86, bf16[32,1024,256]{2,1,0:T(8,128)(2,1)} %bitcast.87, ...), custom_call_target="tpu_custom_call" | custom-call | flops 1610612736 | bytes 9830400 | tf_op jit(solution)/shard_map/pallas_call | solution.py:121
  135.2 13.5 %all-to-all-start = ((bf16[8,128,640]{2,1,0:T(8,128)(2,1)}), bf16[8,128,640]{2,1,0:T(8,128)(2,1)S(1)}, u32[]{:S(2)}, u32[]{:S(2)}) async-start(bf16[8,128,640]{2,1,0:T(8,128)(2,1)} %shard_map.127), calls=%async_computation | async-start | bytes 2621440 | tf_op jit(solution)/shard_map/all_to_all | solution.py:233
  149.3 17.5 %all-to-all-done = bf16[8,128,640]{2,1,0:T(8,128)(2,1)S(1)} async-done(((bf16[8,128,640]{2,1,0:T(8,128)(2,1)}), bf16[8,128,640]{2,1,0:T(8,128)(2,1)S(1)}, u32[]{:S(2)}, u32[]{:S(2)}) %all-to-all-start) | async-done | bytes 1310752 | tf_op jit(solution)/shard_map/all_to_all | solution.py:233
  166.8 0.2 convert_reduce_fusion.1
  167.0 0.8 select_convert_fusion
  (49 shorter events, 0.3 us)
Async XLA Ops:
  6.5 52.9 %copy-start = (bf16[5120,128]{1,0:T(8,128)(2,1)S(1)}, bf16[5120,128]{1,0:T(8,128)(2,1)}, u32[]{:S(2)}) copy-start(bf16[5120,128]{1,0:T(8,128)(2,1)} %param.19) | copy-start | bytes 3932164
  6.5 2.1 %copy-start.8 = (bf16[640]{0:T(1024)(128)(2,1)S(1)}, bf16[640]{0:T(1024)(128)(2,1)}, u32[]{:S(2)}) copy-start(bf16[640]{0:T(1024)(128)(2,1)} %param.14) | copy-start | bytes 3844
  6.5 2.2 %copy-start.3 = (bf16[128,640]{1,0:T(8,128)(2,1)S(1)}, bf16[128,640]{1,0:T(8,128)(2,1)}, u32[]{:S(2)}) copy-start(bf16[128,640]{1,0:T(8,128)(2,1)} %param.13) | copy-start | bytes 491524
  6.5 117.8 %all-gather.2.cloned.1.call-start = ((), (), s32[]{:S(2)}) async-start(), calls=%async_computation.1 | async-start | bytes 17301504 | tf_op jit(solution)/shard_map/all_gather | solution.py:226
  8.6 12.9 %copy-start.9 = (bf16[384]{0:T(512)(128)(2,1)S(1)}, bf16[384]{0:T(512)(128)(2,1)}, u32[]{:S(2)}) copy-start(bf16[384]{0:T(512)(128)(2,1)} %param.16) | copy-start | bytes 2308
  8.6 12.9 %copy-start.13 = (bf16[128]{0:T(256)(128)(2,1)S(1)}, bf16[128]{0:T(256)(128)(2,1)}, u32[]{:S(2)}) copy-start(bf16[128]{0:T(256)(128)(2,1)} %param.18) | copy-start | bytes 772
  8.6 13.4 %copy-start.14 = (bf16[128]{0:T(256)(128)(2,1)S(1)}, bf16[128]{0:T(256)(128)(2,1)}, u32[]{:S(2)}) copy-start(bf16[128]{0:T(256)(128)(2,1)} %param.20) | copy-start | bytes 772
  8.6 14.5 %copy-start.15 = (s32[32]{0:T(128)S(1)}, s32[32]{0:T(128)}, u32[]{:S(2)}) copy-start(s32[32]{0:T(128)} %param.25) | copy-start | bytes 388
  8.8 5.9 %collective-permute-start = (bf16[144,640]{1,0:T(8,128)(2,1)S(1)}, bf16[144,640]{1,0:T(8,128)(2,1)S(1)}, u32[]{:S(2)}, u32[]{:S(2)}) collective-permute-start(bf16[144,640]{1,0:T(8,128)(2,1)S(1)} %maximum_maximum_fusion), channel_id=1, source_target_pairs={{0,1},{1,0},{2,3},{3,2},{4,5},{5,4},{6,7},{7,6},{8,9},{9,8},{10,11... | collective-permute-start | bytes 552968 | tf_op jit(solution)/shard_map/ppermute | solution.py:184
  14.9 9.9 %collective-permute-start.1 = (bf16[2,144,640]{2,1,0:T(8,128)(2,1)S(1)}, bf16[2,144,640]{2,1,0:T(8,128)(2,1)S(1)}, u32[]{:S(2)}, u32[]{:S(2)}) collective-permute-start(bf16[2,144,640]{2,1,0:T(8,128)(2,1)S(1)} %get-tuple-element.8), channel_id=1, source_target_pairs={{0,2},{1,3},{2,4},{3,5},{4,6},{5,7},{6,0},{7,1},{8,10},{9,11},{10,... | collective-permute-start | bytes 1105928 | tf_op jit(solution)/shard_map/ppermute | solution.py:191
  17.2 17.7 %collective-permute-start.2 = (bf16[2,144,640]{2,1,0:T(8,128)(2,1)S(1)}, bf16[2,144,640]{2,1,0:T(8,128)(2,1)S(1)}, u32[]{:S(2)}, u32[]{:S(2)}) collective-permute-start(bf16[2,144,640]{2,1,0:T(8,128)(2,1)S(1)} %get-tuple-element.8), channel_id=1, source_target_pairs={{0,4},{1,5},{2,6},{3,7},{4,0},{5,1},{6,2},{7,3},{8,12},{9,13},{10,... | collective-permute-start | bytes 1105928 | tf_op jit(solution)/shard_map/ppermute | solution.py:191
  19.6 15.4 %collective-permute-start.3 = (bf16[2,144,640]{2,1,0:T(8,128)(2,1)S(1)}, bf16[2,144,640]{2,1,0:T(8,128)(2,1)S(1)}, u32[]{:S(2)}, u32[]{:S(2)}) collective-permute-start(bf16[2,144,640]{2,1,0:T(8,128)(2,1)S(1)} %get-tuple-element.8), channel_id=1, source_target_pairs={{0,6},{1,7},{2,0},{3,1},{4,2},{5,3},{6,4},{7,5},{8,14},{9,15},{10,... | collective-permute-start | bytes 1105928 | tf_op jit(solution)/shard_map/ppermute | solution.py:191
  34.9 0.8 copy-start.4
  35.0 0.8 copy-start.5
  39.0 4.2 %copy-start.12 = (pred[8]{0:T(512)(128)(4,1)S(1)}, pred[8]{0:T(512)(128)(4,1)}, u32[]{:S(2)}) copy-start(pred[8]{0:T(512)(128)(4,1)} %broadcast_in_dim.64) | copy-start | bytes 28
  45.2 1.5 copy-start.1
  50.7 2.2 %copy-start.2 = (bf16[5120,384]{1,0:T(8,128)(2,1)S(1)}, bf16[5120,384]{1,0:T(8,128)(2,1)}, u32[]{:S(2)}) copy-start(bf16[5120,384]{1,0:T(8,128)(2,1)} %param.15) | copy-start | bytes 11796484
  52.9 1.4 copy-start.6
  52.9 1.4 copy-start.7
  53.9 0.8 copy-start.10
  54.6 4.8 %copy-start.11 = (f32[128]{0:T(128)S(1)}, f32[128]{0:T(128)}, u32[]{:S(2)}) copy-start(f32[128]{0:T(128)} %convert_element_type.89) | copy-start | bytes 1540
  135.2 31.6 %all-to-all-start = ((bf16[8,128,640]{2,1,0:T(8,128)(2,1)}), bf16[8,128,640]{2,1,0:T(8,128)(2,1)S(1)}, u32[]{:S(2)}, u32[]{:S(2)}) async-start(bf16[8,128,640]{2,1,0:T(8,128)(2,1)} %shard_map.127), calls=%async_computation | async-start | bytes 2621440 | tf_op jit(solution)/shard_map/all_to_all | solution.py:233
Sparse Core Ops, SparseCore 0:
  9.9 114.3 all-gather.1

commit v13 on v12

--- a/solution.py
+++ b/solution.py
@@ -12,7 +12,7 @@
 THETA = 1000000.0
 EPSILON = 1e-06
 ROWS = 144
-PER_STEP = 4
+PER_STEP = 8
 
 
 def rotate(heads, positions):

time: 175 us -> 174 us (level)
  transfers between devices with their start and end apart: 6 -> 6, of which waited for: 5 -> 5; matrix products, arithmetic and copies ran while one was open for 15% -> 16% of each run, Pallas kernels for 0% -> 0%
where the time goes in v13:
time: 174 us
  waiting for transfers between devices  93.8 us (54%)
  starting transfers between devices  21.7 us (12%)
  between operations  15 us (9%)
  local copies, waits for them, and re-layouts  14.7 us (8%)
  other arithmetic  13.4 us (8%)
  Pallas kernels  10.6 us (6%)
  matrix products  4.35 us (2%)
    all_gather x1, waiting for transfers between devices, shards(): gathered = lax.all_gather(rowwise, 'req', axis=0, tiled=True)  62.8 us
    all_to_all x1, waiting for transfers between devices, shards(): lax.all_to_all(pieces_out, 'tp', 0, 0, tiled=True).astype(jnp.float32)  17.5 us
    all_to_all x1, starting transfers between devices, shards(): lax.all_to_all(pieces_out, 'tp', 0, 0, tiled=True).astype(jnp.float32)  13.3 us
    pallas_call x1, Pallas kernels, prefix_attention(): pl.pallas_call(prefix_kernel, out_shape=jax.ShapeDtypeStruct((pieces, len...  10.6 us
    ppermute x3, waiting for transfers between devices, shards(): lax.ppermute(pair, 'tp', [(i, (i + 2 * u) % n_tp) for i in range(n_tp)])  10.3 us
    unnamed x39, local copies, waits for them, and re-layouts  6.27 us
    gather x2, local copies, waits for them, and re-layouts, shards(): jnp.take(along, (me_x - jnp.arange(n_x, dtype=jnp.int32)) % n_x, axis=0)  6.05 us
    ppermute x3, starting transfers between devices, shards(): lax.ppermute(pair, 'tp', [(i, (i + 2 * u) % n_tp) for i in range(n_tp)])  5.83 us
  transfers between devices with their start and end apart: 6, of which 5 were waited for; matrix products, arithmetic and copies ran while one was open for 16% of the time, Pallas kernels for 0%

profile of v13, /device:TPU:1, one launch (start us, length us, event | category | flops | bytes accessed | tf_op | source)
XLA Modules:
  0.0 173.6 jit_solution(10373271168650425471)
XLA Ops:
  6.5 2.0 %copy.52 = bf16[128,8,2,128]{3,1,2,0:T(8,128)(2,1)} copy(bf16[128,8,2,128]{3,2,1,0:T(2,128)(2,1)} %bitcast.108) | data formatting | bytes 1048576
  8.7 0.1 pad.12.clone
  8.7 0.1 maximum_maximum_fusion
  8.8 2.6 %collective-permute-start = (bf16[144,640]{1,0:T(8,128)(2,1)S(1)}, bf16[144,640]{1,0:T(8,128)(2,1)S(1)}, u32[]{:S(2)}, u32[]{:S(2)}) collective-permute-start(bf16[144,640]{1,0:T(8,128)(2,1)S(1)} %maximum_maximum_fusion), channel_id=1, source_target_pairs={{0,1},{1,0},{2,3},{3,2},{4,5},{5,4},{6,7},{7,6},{8,9},{9,8},{10,11... | collective-permute-start | bytes 552968 | tf_op jit(solution)/shard_map/ppermute | solution.py:184
  11.4 3.3 %collective-permute-done = bf16[144,640]{1,0:T(8,128)(2,1)S(1)} collective-permute-done((bf16[144,640]{1,0:T(8,128)(2,1)S(1)}, bf16[144,640]{1,0:T(8,128)(2,1)S(1)}, u32[]{:S(2)}, u32[]{:S(2)}) %collective-permute-start) | collective-permute-done | bytes 184352 | tf_op jit(solution)/shard_map/ppermute | solution.py:184
  14.7 0.2 select_bitcast_fusion.1
  14.9 0.1 fusion.30
  14.9 2.2 %collective-permute-start.1 = (bf16[2,144,640]{2,1,0:T(8,128)(2,1)S(1)}, bf16[2,144,640]{2,1,0:T(8,128)(2,1)S(1)}, u32[]{:S(2)}, u32[]{:S(2)}) collective-permute-start(bf16[2,144,640]{2,1,0:T(8,128)(2,1)S(1)} %get-tuple-element.8), channel_id=1, source_target_pairs={{0,2},{1,3},{2,4},{3,5},{4,6},{5,7},{6,0},{7,1},{8,10},{9,11},{10,... | collective-permute-start | bytes 1105928 | tf_op jit(solution)/shard_map/ppermute | solution.py:191
  17.2 2.5 %collective-permute-start.2 = (bf16[2,144,640]{2,1,0:T(8,128)(2,1)S(1)}, bf16[2,144,640]{2,1,0:T(8,128)(2,1)S(1)}, u32[]{:S(2)}, u32[]{:S(2)}) collective-permute-start(bf16[2,144,640]{2,1,0:T(8,128)(2,1)S(1)} %get-tuple-element.8), channel_id=1, source_target_pairs={{0,4},{1,5},{2,6},{3,7},{4,0},{5,1},{6,2},{7,3},{8,12},{9,13},{10,... | collective-permute-start | bytes 1105928 | tf_op jit(solution)/shard_map/ppermute | solution.py:191
  19.6 1.2 collective-permute-start.3
  20.8 0.1 broadcast_in_dim.63
  20.8 0.6 broadcast_in_dim.64
  21.4 0.5 convert_element_type.88
  22.0 0.5 convert_element_type.89
  23.1 0.6 dynamic_slice.3.own_ref
  23.8 1.0 multiply_cosine_fusion
  24.8 10.1 %collective-permute-done.2 = bf16[2,144,640]{2,1,0:T(8,128)(2,1)S(1)} collective-permute-done((bf16[2,144,640]{2,1,0:T(8,128)(2,1)S(1)}, bf16[2,144,640]{2,1,0:T(8,128)(2,1)S(1)}, u32[]{:S(2)}, u32[]{:S(2)}) %collective-permute-start.2) | collective-permute-done | bytes 368672 | tf_op jit(solution)/shard_map/ppermute | solution.py:191
  34.9 0.1 collective-permute-done.3
  35.0 0.6 copy-done.4
  35.6 0.2 copy-done.5
  35.8 1.3 pad_maximum_fusion
  37.1 1.9 %gather_fusion = bf16[4,2,144,640]{3,2,1,0:T(8,128)(2,1)} fusion(bf16[4,2,144,640]{3,2,1,0:T(8,128)(2,1)S(1)} %pad_maximum_fusion, s32[1024]{0:T(1024)S(1)} %pad_clamp_fusion), kind=kCustom, calls=%fused_computation | custom fusion | bytes 2949136 | tf_op jit(solution)/shard_map/jit(_take)/gather | solution.py:196
  39.0 4.2 %copy.29 = bf16[4,2,144,640]{2,3,1,0:T(8,128)(2,1)} copy(bf16[4,2,144,640]{3,2,1,0:T(8,128)(2,1)} %gather_fusion) | data formatting | bytes 2949120 | tf_op jit(solution)/shard_map/jit(_take)/gather | solution.py:196
  43.2 2.1 %bitcast_select_fusion = bf16[8,144,640]{1,2,0:T(8,128)(2,1)S(1)} fusion(bf16[4,2,144,640]{2,3,1,0:T(8,128)(2,1)} %copy.29, pred[8]{0:T(512)(128)(4,1)S(1)} %copy-done.12), kind=kLoop, calls=%fused_computation.4 | loop fusion | flops 737280 | bytes 2949128 | tf_op jit(solution)/shard_map/jit(_take)/select_n | solution.py:196
  45.3 1.5 copy-done.1
  46.7 0.4 convert_reduce_fusion
  47.2 2.0 %multiply_reduce_fusion = f32[128]{0:T(128)S(1)} fusion(bf16[144,8,640]{0,2,1:T(8,128)(2,1)} %bitcast.101), kind=kLoop, calls=%fused_computation.7 | loop fusion | flops 1965952 | bytes 1311232 | tf_op jit(solution)/shard_map/reduce_sum | solution.py:201
  49.2 1.5 slice_convert_fusion
  50.7 2.4 %fusion.1 = bf16[128,5120]{0,1:T(8,128)(2,1)S(1)} fusion(f32[128,8,640]{0,2,1:T(8,128)S(1)} %slice_convert_fusion, f32[5120]{0:T(1024)S(1)} %reshape.283, f32[128]{0:T(128)S(1)} %add_rsqrt_fusion), kind=kLoop, calls=%fused_computation.3 | loop fusion | flops 1966080 | bytes 3953152 | tf_op jit(solution)/shard_map/convert_element_type | solution.py:202
  53.1 0.9 convolution_add_fusion
  54.0 0.1 copy.30
  54.2 0.1 copy.42
  54.3 0.1 copy.43
  54.5 0.1 maximum_convert_fusion
  54.7 0.1 copy.33
  54.8 1.9 %fusion.4 = f32[128,1,128]{0,2,1:T(8,128)S(1)} fusion(bf16[128,5120]{0,1:T(8,128)(2,1)S(1)} %fusion.1, bf16[5120,128]{1,0:T(8,128)(2,1)} %param.17, f32[128]{0:T(128)S(1)} %copy-done.10), kind=kOutput, calls=%fused_computation.16 | convolution fusion | flops 167788544 | bytes 2687488 | tf_op jit(solution)/shard_map/dot_general | solution.py:209
  56.7 0.2 fusion.25
  56.9 0.2 fusion.32
  57.2 0.8 copy.48
  58.0 0.8 copy.46
  58.8 0.8 copy.36.q_ref
  59.6 1.4 fusion.7
  61.0 62.8 %all-gather.2.cloned.1.call-done = bf16[32768,256]{1,0:T(8,128)(2,1)} async-done(((bf16[1024,256]{1,0:T(8,128)(2,1)}), bf16[32768,256]{1,0:T(8,128)(2,1)}) %all-gather.2.cloned.1.call-update) | async-done | bytes 16777232 | tf_op jit(solution)/shard_map/all_gather | solution.py:226
  123.8 10.6 %shard_map.127 = bf16[8,128,640]{2,1,0:T(8,128)(2,1)} custom-call(s32[8]{0:T(128)} %dynamic_slice.3.own_ref, bf16[128,384]{1,0:T(8,128)(2,1)} %copy.36.q_ref, bf16[32,1024,256]{2,1,0:T(8,128)(2,1)} %bitcast.84, bf16[32,1024,256]{2,1,0:T(8,128)(2,1)} %bitcast.85, bf16[32,1024,256]{2,1,0:T(8,128)(2,1)} %bitcast.86, bf16[32,1024,256]{2,1,0:T(8,128)(2,1)} %bitcast.87, ...), custom_call_target="tpu_custom_call" | custom-call | flops 1610612736 | bytes 9830400 | tf_op jit(solution)/shard_map/pallas_call | solution.py:121
  134.4 13.3 %all-to-all-start = ((bf16[8,128,640]{2,1,0:T(8,128)(2,1)}), bf16[8,128,640]{2,1,0:T(8,128)(2,1)S(1)}, u32[]{:S(2)}, u32[]{:S(2)}) async-start(bf16[8,128,640]{2,1,0:T(8,128)(2,1)} %shard_map.127), calls=%async_computation | async-start | bytes 2621440 | tf_op jit(solution)/shard_map/all_to_all | solution.py:233
  148.4 17.5 %all-to-all-done = bf16[8,128,640]{2,1,0:T(8,128)(2,1)S(1)} async-done(((bf16[8,128,640]{2,1,0:T(8,128)(2,1)}), bf16[8,128,640]{2,1,0:T(8,128)(2,1)S(1)}, u32[]{:S(2)}, u32[]{:S(2)}) %all-to-all-start) | async-done | bytes 1310752 | tf_op jit(solution)/shard_map/all_to_all | solution.py:233
  165.9 0.2 convert_reduce_fusion.1
  166.0 0.8 select_convert_fusion
  (49 shorter events, 0.3 us)
Async XLA Ops:
  6.5 53.1 %copy-start = (bf16[5120,128]{1,0:T(8,128)(2,1)S(1)}, bf16[5120,128]{1,0:T(8,128)(2,1)}, u32[]{:S(2)}) copy-start(bf16[5120,128]{1,0:T(8,128)(2,1)} %param.19) | copy-start | bytes 3932164
  6.5 2.1 %copy-start.8 = (bf16[640]{0:T(1024)(128)(2,1)S(1)}, bf16[640]{0:T(1024)(128)(2,1)}, u32[]{:S(2)}) copy-start(bf16[640]{0:T(1024)(128)(2,1)} %param.14) | copy-start | bytes 3844
  6.5 2.2 %copy-start.3 = (bf16[128,640]{1,0:T(8,128)(2,1)S(1)}, bf16[128,640]{1,0:T(8,128)(2,1)}, u32[]{:S(2)}) copy-start(bf16[128,640]{1,0:T(8,128)(2,1)} %param.13) | copy-start | bytes 491524
  6.5 117.2 %all-gather.2.cloned.1.call-start = ((), (), s32[]{:S(2)}) async-start(), calls=%async_computation.1 | async-start | bytes 17301504 | tf_op jit(solution)/shard_map/all_gather | solution.py:226
  8.6 12.9 %copy-start.9 = (bf16[384]{0:T(512)(128)(2,1)S(1)}, bf16[384]{0:T(512)(128)(2,1)}, u32[]{:S(2)}) copy-start(bf16[384]{0:T(512)(128)(2,1)} %param.16) | copy-start | bytes 2308
  8.6 12.9 %copy-start.13 = (bf16[128]{0:T(256)(128)(2,1)S(1)}, bf16[128]{0:T(256)(128)(2,1)}, u32[]{:S(2)}) copy-start(bf16[128]{0:T(256)(128)(2,1)} %param.18) | copy-start | bytes 772
  8.6 13.4 %copy-start.14 = (bf16[128]{0:T(256)(128)(2,1)S(1)}, bf16[128]{0:T(256)(128)(2,1)}, u32[]{:S(2)}) copy-start(bf16[128]{0:T(256)(128)(2,1)} %param.20) | copy-start | bytes 772
  8.6 14.5 %copy-start.15 = (s32[32]{0:T(128)S(1)}, s32[32]{0:T(128)}, u32[]{:S(2)}) copy-start(s32[32]{0:T(128)} %param.25) | copy-start | bytes 388
  8.8 5.9 %collective-permute-start = (bf16[144,640]{1,0:T(8,128)(2,1)S(1)}, bf16[144,640]{1,0:T(8,128)(2,1)S(1)}, u32[]{:S(2)}, u32[]{:S(2)}) collective-permute-start(bf16[144,640]{1,0:T(8,128)(2,1)S(1)} %maximum_maximum_fusion), channel_id=1, source_target_pairs={{0,1},{1,0},{2,3},{3,2},{4,5},{5,4},{6,7},{7,6},{8,9},{9,8},{10,11... | collective-permute-start | bytes 552968 | tf_op jit(solution)/shard_map/ppermute | solution.py:184
  14.9 9.9 %collective-permute-start.1 = (bf16[2,144,640]{2,1,0:T(8,128)(2,1)S(1)}, bf16[2,144,640]{2,1,0:T(8,128)(2,1)S(1)}, u32[]{:S(2)}, u32[]{:S(2)}) collective-permute-start(bf16[2,144,640]{2,1,0:T(8,128)(2,1)S(1)} %get-tuple-element.8), channel_id=1, source_target_pairs={{0,2},{1,3},{2,4},{3,5},{4,6},{5,7},{6,0},{7,1},{8,10},{9,11},{10,... | collective-permute-start | bytes 1105928 | tf_op jit(solution)/shard_map/ppermute | solution.py:191
  17.2 17.7 %collective-permute-start.2 = (bf16[2,144,640]{2,1,0:T(8,128)(2,1)S(1)}, bf16[2,144,640]{2,1,0:T(8,128)(2,1)S(1)}, u32[]{:S(2)}, u32[]{:S(2)}) collective-permute-start(bf16[2,144,640]{2,1,0:T(8,128)(2,1)S(1)} %get-tuple-element.8), channel_id=1, source_target_pairs={{0,4},{1,5},{2,6},{3,7},{4,0},{5,1},{6,2},{7,3},{8,12},{9,13},{10,... | collective-permute-start | bytes 1105928 | tf_op jit(solution)/shard_map/ppermute | solution.py:191
  19.6 15.4 %collective-permute-start.3 = (bf16[2,144,640]{2,1,0:T(8,128)(2,1)S(1)}, bf16[2,144,640]{2,1,0:T(8,128)(2,1)S(1)}, u32[]{:S(2)}, u32[]{:S(2)}) collective-permute-start(bf16[2,144,640]{2,1,0:T(8,128)(2,1)S(1)} %get-tuple-element.8), channel_id=1, source_target_pairs={{0,6},{1,7},{2,0},{3,1},{4,2},{5,3},{6,4},{7,5},{8,14},{9,15},{10,... | collective-permute-start | bytes 1105928 | tf_op jit(solution)/shard_map/ppermute | solution.py:191
  34.9 0.8 copy-start.4
  35.0 0.8 copy-start.5
  39.0 4.2 %copy-start.12 = (pred[8]{0:T(512)(128)(4,1)S(1)}, pred[8]{0:T(512)(128)(4,1)}, u32[]{:S(2)}) copy-start(pred[8]{0:T(512)(128)(4,1)} %broadcast_in_dim.64) | copy-start | bytes 28
  45.2 1.5 copy-start.1
  50.7 2.4 %copy-start.2 = (bf16[5120,384]{1,0:T(8,128)(2,1)S(1)}, bf16[5120,384]{1,0:T(8,128)(2,1)}, u32[]{:S(2)}) copy-start(bf16[5120,384]{1,0:T(8,128)(2,1)} %param.15) | copy-start | bytes 11796484
  53.1 1.4 copy-start.6
  53.1 1.4 copy-start.7
  54.0 0.8 copy-start.10
  54.8 4.8 %copy-start.11 = (f32[128]{0:T(128)S(1)}, f32[128]{0:T(128)}, u32[]{:S(2)}) copy-start(f32[128]{0:T(128)} %convert_element_type.89) | copy-start | bytes 1540
  134.4 31.4 %all-to-all-start = ((bf16[8,128,640]{2,1,0:T(8,128)(2,1)}), bf16[8,128,640]{2,1,0:T(8,128)(2,1)S(1)}, u32[]{:S(2)}, u32[]{:S(2)}) async-start(bf16[8,128,640]{2,1,0:T(8,128)(2,1)} %shard_map.127), calls=%async_computation | async-start | bytes 2621440 | tf_op jit(solution)/shard_map/all_to_all | solution.py:233
Sparse Core Ops, SparseCore 0:
  9.9 113.8 all-gather.1

commit v14 on v13

--- a/solution.py
+++ b/solution.py
@@ -52,58 +52,44 @@
     return (peak, total, mixed)
 
 
-def prefix_kernel(own_ref, q_ref, *refs):
-    kv_refs = refs[:2 * PER_STEP]
-    m0_ref, l0_ref, a0_ref, w_hbm, o_ref, m_sc, l_sc, acc_sc, q_sc, w_sc, sem = refs[2 * PER_STEP:]
-    step = pl.program_id(0)
+def prefix_kernel(own_ref, q_ref, kv_hbm, m0_ref, l0_ref, a0_ref, w_hbm, o_ref, buf, w_sc, sem):
     group = q_ref.shape[1] // HD
-    fetch = pltpu.make_async_copy(w_hbm, w_sc, sem.at[0])
-
-    @pl.when(step == 0)
-    def _():
-        fetch.start()
-        m_sc[...] = m0_ref[...]
-        l_sc[...] = l0_ref[...]
-        acc_sc[...] = a0_ref[...]
-        q = q_ref[...]
-        q_sc[...] = jnp.concatenate([q[:, h * HD:(h + 1) * HD] for h in range(group)], axis=0)
-
-    stacked = q_sc[...]
+    steps = buf.shape[0]
+    fetch = pltpu.make_async_copy(w_hbm, w_sc, sem.at[steps])
+    copies = [
+        pltpu.make_async_copy(kv_hbm.at[own_ref[i]], buf.at[i], sem.at[i]) for i in range(steps)
+    ]
+    for copy in copies:
+        copy.start()
+    fetch.start()
+    q = q_ref[...]
+    stacked = jnp.concatenate([q[:, h * HD:(h + 1) * HD] for h in range(group)], axis=0)
     dims = (((1,), (1,)), ((), ()))
-    refs = kv_refs
-    parts = [
-        lax.dot_general(stacked, refs[2 * i][0], dims, preferred_element_type=jnp.float32)
-        * HD ** (-0.5)
-        for i in range(len(refs) // 2)
-    ]
-    old = m_sc[...]
-    top = old
-    for part in parts:
-        top = jnp.maximum(top, jnp.max(part, axis=-1, keepdims=True))
-    alpha = jnp.exp(old - top)
-    weights = [jnp.exp(part - top) for part in parts]
-    summed = weights[0].sum(axis=-1, keepdims=True)
-    mixed = jnp.dot(weights[0].astype(jnp.bfloat16), refs[1][0], preferred_element_type=jnp.float32)
-    for i in range(1, len(weights)):
-        summed = summed + weights[i].sum(axis=-1, keepdims=True)
-        mixed = mixed + jnp.dot(
-            weights[i].astype(jnp.bfloat16), refs[2 * i + 1][0], preferred_element_type=jnp.float32
+    top = m0_ref[...]
+    summed = l0_ref[...]
+    mixed = a0_ref[...]
+    for i in range(steps):
+        copies[i].wait()
+        keys = buf[i, :, :HD]
+        values = buf[i, :, HD:]
+        part = lax.dot_general(stacked, keys, dims, preferred_element_type=jnp.float32) * HD ** (-0.5)
+        new = jnp.maximum(top, jnp.max(part, axis=-1, keepdims=True))
+        alpha = jnp.exp(top - new)
+        weights = jnp.exp(part - new)
+        summed = alpha * summed + weights.sum(axis=-1, keepdims=True)
+        mixed = alpha * mixed + jnp.dot(
+            weights.astype(jnp.bfloat16), values, preferred_element_type=jnp.float32
         )
-    l_sc[...] = alpha * l_sc[...] + summed
-    acc_sc[...] = alpha * acc_sc[...] + mixed
-    m_sc[...] = top
-
-    @pl.when(step == pl.num_programs(0) - 1)
-    def _():
-        context = (acc_sc[...] / l_sc[...]).astype(jnp.bfloat16)
-        rows = q_ref.shape[0]
-        flat = jnp.concatenate([context[h * rows:(h + 1) * rows] for h in range(group)], axis=1)
-        fetch.wait()
-        partial = jnp.dot(flat, w_sc[...], preferred_element_type=jnp.float32).astype(o_ref.dtype)
-        pieces = o_ref.shape[0]
-        span = o_ref.shape[2]
-        for t in range(pieces):
-            o_ref[t] = partial[:, t * span:(t + 1) * span]
+        top = new
+    context = (mixed / summed).astype(jnp.bfloat16)
+    rows = q_ref.shape[0]
+    flat = jnp.concatenate([context[h * rows:(h + 1) * rows] for h in range(group)], axis=1)
+    fetch.wait()
+    partial = jnp.dot(flat, w_sc[...], preferred_element_type=jnp.float32).astype(o_ref.dtype)
+    pieces = o_ref.shape[0]
+    span = o_ref.shape[2]
+    for t in range(pieces):
+        o_ref[t] = partial[:, t * span:(t + 1) * span]
 
 
 def prefix_attention(owners, flat_q, kv, peak0, total0, mixed0, o_weight, pieces):
@@ -123,14 +109,10 @@
         out_shape=jax.ShapeDtypeStruct((pieces, length, out_width // pieces), jnp.bfloat16),
         grid_spec=pltpu.PrefetchScalarGridSpec(
             num_scalar_prefetch=1,
-            grid=(steps // PER_STEP,),
+            grid=(1,),
             in_specs=[
                 pl.BlockSpec((length, width), lambda j, own: (0, 0)),
-                *[
-                    pl.BlockSpec((1, block, HD), lambda j, own, i=i, c=c: (own[PER_STEP * j + i], 0, c))
-                    for i in range(PER_STEP)
-                    for c in range(2)
-                ],
+                pl.BlockSpec(memory_space=pl.ANY),
                 pl.BlockSpec((rows, 1), lambda j, own: (0, 0)),
                 pl.BlockSpec((rows, 1), lambda j, own: (0, 0)),
                 pl.BlockSpec((rows, HD), lambda j, own: (0, 0)),
@@ -138,17 +120,14 @@
             ],
             out_specs=pl.BlockSpec((pieces, length, out_width // pieces), lambda j, own: (0, 0, 0)),
             scratch_shapes=[
-                pltpu.VMEM((rows, 1), jnp.float32),
-                pltpu.VMEM((rows, 1), jnp.float32),
-                pltpu.VMEM((rows, HD), jnp.float32),
-                pltpu.VMEM((rows, HD), jnp.bfloat16),
+                pltpu.VMEM((steps, block, 2 * HD), jnp.bfloat16),
                 pltpu.VMEM((width, out_width), jnp.bfloat16),
-                pltpu.SemaphoreType.DMA((1,)),
+                pltpu.SemaphoreType.DMA((steps + 1,)),
             ],
         ),
         compiler_params=pltpu.CompilerParams(dimension_semantics=("arbitrary",)),
         cost_estimate=cost,
-    )(owners, flat_q, *([kv] * (2 * PER_STEP)), peak0, total0, mixed0, o_weight)
+    )(owners, flat_q, kv, peak0, total0, mixed0, o_weight)
 
 
 def shards(

time: 174 us -> 177 us (1.017)
  Pallas kernels: 10.6 us -> 13.4 us
    pallas_call x1, Pallas kernels: 10.6 us -> 13.4 us  [prefix_attention(): pl.pallas_call(prefix_kernel, out_shape=jax.ShapeDtypeStruct((pieces, len...]
  transfers between devices with their start and end apart: 6 -> 6, of which waited for: 5 -> 5; matrix products, arithmetic and copies ran while one was open for 16% -> 15% of each run, Pallas kernels for 0% -> 0%
where the time goes in v14:
time: 177 us; the launch traced here: 176 us
  waiting for transfers between devices  93.8 us (53%)
  starting transfers between devices  21.7 us (12%)
  between operations  15 us (8%)
  local copies, waits for them, and re-layouts  14.7 us (8%)
  other arithmetic  13.4 us (8%)
  Pallas kernels  13.4 us (8%)
  matrix products  4.35 us (2%)
    all_gather x1, waiting for transfers between devices, shards(): gathered = lax.all_gather(rowwise, 'req', axis=0, tiled=True)  62.8 us
    all_to_all x1, waiting for transfers between devices, shards(): lax.all_to_all(pieces_out, 'tp', 0, 0, tiled=True).astype(jnp.float32)  17.5 us
    pallas_call x1, Pallas kernels, prefix_attention(): pl.pallas_call(prefix_kernel, out_shape=jax.ShapeDtypeStruct((pieces, len...  13.4 us
    all_to_all x1, starting transfers between devices, shards(): lax.all_to_all(pieces_out, 'tp', 0, 0, tiled=True).astype(jnp.float32)  13.3 us
    ppermute x3, waiting for transfers between devices, shards(): lax.ppermute(pair, 'tp', [(i, (i + 2 * u) % n_tp) for i in range(n_tp)])  10.3 us
    unnamed x39, local copies, waits for them, and re-layouts  6.27 us
    gather x2, local copies, waits for them, and re-layouts, shards(): jnp.take(along, (me_x - jnp.arange(n_x, dtype=jnp.int32)) % n_x, axis=0)  6.05 us
    ppermute x3, starting transfers between devices, shards(): lax.ppermute(pair, 'tp', [(i, (i + 2 * u) % n_tp) for i in range(n_tp)])  5.83 us
  transfers between devices with their start and end apart: 6, of which 5 were waited for; matrix products, arithmetic and copies ran while one was open for 15% of the time, Pallas kernels for 0%

profile of v14, /device:TPU:1, one launch (start us, length us, event | category | flops | bytes accessed | tf_op | source)
XLA Modules:
  0.0 176.4 jit_solution(9560345835592358249)
XLA Ops:
  6.5 2.0 %copy.52 = bf16[128,8,2,128]{3,1,2,0:T(8,128)(2,1)} copy(bf16[128,8,2,128]{3,2,1,0:T(2,128)(2,1)} %bitcast.93) | data formatting | bytes 1048576
  8.7 0.1 pad.12.clone
  8.7 0.1 maximum_maximum_fusion
  8.8 2.6 %collective-permute-start = (bf16[144,640]{1,0:T(8,128)(2,1)S(1)}, bf16[144,640]{1,0:T(8,128)(2,1)S(1)}, u32[]{:S(2)}, u32[]{:S(2)}) collective-permute-start(bf16[144,640]{1,0:T(8,128)(2,1)S(1)} %maximum_maximum_fusion), channel_id=1, source_target_pairs={{0,1},{1,0},{2,3},{3,2},{4,5},{5,4},{6,7},{7,6},{8,9},{9,8},{10,11... | collective-permute-start | bytes 552968 | tf_op jit(solution)/shard_map/ppermute | solution.py:163
  11.4 3.3 %collective-permute-done = bf16[144,640]{1,0:T(8,128)(2,1)S(1)} collective-permute-done((bf16[144,640]{1,0:T(8,128)(2,1)S(1)}, bf16[144,640]{1,0:T(8,128)(2,1)S(1)}, u32[]{:S(2)}, u32[]{:S(2)}) %collective-permute-start) | collective-permute-done | bytes 184352 | tf_op jit(solution)/shard_map/ppermute | solution.py:163
  14.7 0.2 select_bitcast_fusion.1
  14.9 0.1 fusion.30
  14.9 2.2 %collective-permute-start.1 = (bf16[2,144,640]{2,1,0:T(8,128)(2,1)S(1)}, bf16[2,144,640]{2,1,0:T(8,128)(2,1)S(1)}, u32[]{:S(2)}, u32[]{:S(2)}) collective-permute-start(bf16[2,144,640]{2,1,0:T(8,128)(2,1)S(1)} %get-tuple-element.8), channel_id=1, source_target_pairs={{0,2},{1,3},{2,4},{3,5},{4,6},{5,7},{6,0},{7,1},{8,10},{9,11},{10,... | collective-permute-start | bytes 1105928 | tf_op jit(solution)/shard_map/ppermute | solution.py:170
  17.2 2.5 %collective-permute-start.2 = (bf16[2,144,640]{2,1,0:T(8,128)(2,1)S(1)}, bf16[2,144,640]{2,1,0:T(8,128)(2,1)S(1)}, u32[]{:S(2)}, u32[]{:S(2)}) collective-permute-start(bf16[2,144,640]{2,1,0:T(8,128)(2,1)S(1)} %get-tuple-element.8), channel_id=1, source_target_pairs={{0,4},{1,5},{2,6},{3,7},{4,0},{5,1},{6,2},{7,3},{8,12},{9,13},{10,... | collective-permute-start | bytes 1105928 | tf_op jit(solution)/shard_map/ppermute | solution.py:170
  19.6 1.2 collective-permute-start.3
  20.8 0.1 broadcast_in_dim.63
  20.8 0.6 broadcast_in_dim.64
  21.4 0.5 convert_element_type.88
  22.0 0.5 convert_element_type.89
  23.1 0.6 dynamic_slice.3.own_ref
  23.8 1.0 multiply_cosine_fusion
  24.8 10.1 %collective-permute-done.2 = bf16[2,144,640]{2,1,0:T(8,128)(2,1)S(1)} collective-permute-done((bf16[2,144,640]{2,1,0:T(8,128)(2,1)S(1)}, bf16[2,144,640]{2,1,0:T(8,128)(2,1)S(1)}, u32[]{:S(2)}, u32[]{:S(2)}) %collective-permute-start.2) | collective-permute-done | bytes 368672 | tf_op jit(solution)/shard_map/ppermute | solution.py:170
  34.9 0.1 collective-permute-done.3
  35.0 0.6 copy-done.4
  35.6 0.2 copy-done.5
  35.8 1.3 pad_maximum_fusion
  37.1 1.9 %gather_fusion = bf16[4,2,144,640]{3,2,1,0:T(8,128)(2,1)} fusion(bf16[4,2,144,640]{3,2,1,0:T(8,128)(2,1)S(1)} %pad_maximum_fusion, s32[1024]{0:T(1024)S(1)} %pad_clamp_fusion), kind=kCustom, calls=%fused_computation | custom fusion | bytes 2949136 | tf_op jit(solution)/shard_map/jit(_take)/gather | solution.py:175
  39.0 4.2 %copy.29 = bf16[4,2,144,640]{2,3,1,0:T(8,128)(2,1)} copy(bf16[4,2,144,640]{3,2,1,0:T(8,128)(2,1)} %gather_fusion) | data formatting | bytes 2949120 | tf_op jit(solution)/shard_map/jit(_take)/gather | solution.py:175
  43.2 2.1 %bitcast_select_fusion = bf16[8,144,640]{1,2,0:T(8,128)(2,1)S(1)} fusion(bf16[4,2,144,640]{2,3,1,0:T(8,128)(2,1)} %copy.29, pred[8]{0:T(512)(128)(4,1)S(1)} %copy-done.12), kind=kLoop, calls=%fused_computation.4 | loop fusion | flops 737280 | bytes 2949128 | tf_op jit(solution)/shard_map/jit(_take)/select_n | solution.py:175
  45.3 1.5 copy-done.1
  46.7 0.4 convert_reduce_fusion
  47.2 2.0 %multiply_reduce_fusion = f32[128]{0:T(128)S(1)} fusion(bf16[144,8,640]{0,2,1:T(8,128)(2,1)} %bitcast.86), kind=kLoop, calls=%fused_computation.7 | loop fusion | flops 1965952 | bytes 1311232 | tf_op jit(solution)/shard_map/reduce_sum | solution.py:180
  49.2 1.5 slice_convert_fusion
  50.7 2.4 %fusion.1 = bf16[128,5120]{0,1:T(8,128)(2,1)S(1)} fusion(f32[128,8,640]{0,2,1:T(8,128)S(1)} %slice_convert_fusion, f32[5120]{0:T(1024)S(1)} %reshape.283, f32[128]{0:T(128)S(1)} %add_rsqrt_fusion), kind=kLoop, calls=%fused_computation.3 | loop fusion | flops 1966080 | bytes 3953152 | tf_op jit(solution)/shard_map/convert_element_type | solution.py:181
  53.1 0.9 convolution_add_fusion
  54.0 0.1 copy.30
  54.2 0.1 copy.42
  54.3 0.1 copy.43
  54.5 0.1 maximum_convert_fusion
  54.7 0.1 copy.33
  54.8 1.9 %fusion.4 = f32[128,1,128]{0,2,1:T(8,128)S(1)} fusion(bf16[128,5120]{0,1:T(8,128)(2,1)S(1)} %fusion.1, bf16[5120,128]{1,0:T(8,128)(2,1)} %param.17, f32[128]{0:T(128)S(1)} %copy-done.10), kind=kOutput, calls=%fused_computation.16 | convolution fusion | flops 167788544 | bytes 2687488 | tf_op jit(solution)/shard_map/dot_general | solution.py:188
  56.7 0.2 fusion.25
  56.9 0.2 fusion.32
  57.2 0.8 copy.48
  58.0 0.8 copy.46
  58.8 0.8 copy.36.q_ref
  59.6 1.4 fusion.7
  61.0 62.8 %all-gather.2.cloned.1.call-done = bf16[32768,256]{1,0:T(8,128)(2,1)} async-done(((bf16[1024,256]{1,0:T(8,128)(2,1)}), bf16[32768,256]{1,0:T(8,128)(2,1)}) %all-gather.2.cloned.1.call-update) | async-done | bytes 16777232 | tf_op jit(solution)/shard_map/all_gather | solution.py:205
  123.8 13.4 %shard_map.127 = bf16[8,128,640]{2,1,0:T(8,128)(2,1)} custom-call(s32[8]{0:T(128)} %dynamic_slice.3.own_ref, bf16[128,384]{1,0:T(8,128)(2,1)} %copy.36.q_ref, bf16[32,1024,256]{2,1,0:T(8,128)(2,1)} %bitcast.84, f32[384,1]{1,0:T(8,128)} %bitcast.91, f32[384,1]{1,0:T(8,128)} %bitcast.90, f32[384,128]{1,0:T(8,128)} %bitcast.89, bf16[384,5120]{1,0:T(8,128)(2,1)} %w_hbm.1), custom_call_target="tpu_custom_call" | custom-call | flops 1610612736 | bytes 9830400 | tf_op jit(solution)/shard_map/pallas_call | solution.py:107
  137.2 13.3 %all-to-all-start = ((bf16[8,128,640]{2,1,0:T(8,128)(2,1)}), bf16[8,128,640]{2,1,0:T(8,128)(2,1)S(1)}, u32[]{:S(2)}, u32[]{:S(2)}) async-start(bf16[8,128,640]{2,1,0:T(8,128)(2,1)} %shard_map.127), calls=%async_computation | async-start | bytes 2621440 | tf_op jit(solution)/shard_map/all_to_all | solution.py:212
  151.1 17.5 %all-to-all-done = bf16[8,128,640]{2,1,0:T(8,128)(2,1)S(1)} async-done(((bf16[8,128,640]{2,1,0:T(8,128)(2,1)}), bf16[8,128,640]{2,1,0:T(8,128)(2,1)S(1)}, u32[]{:S(2)}, u32[]{:S(2)}) %all-to-all-start) | async-done | bytes 1310752 | tf_op jit(solution)/shard_map/all_to_all | solution.py:212
  168.6 0.2 convert_reduce_fusion.1
  168.8 0.8 select_convert_fusion
  (49 shorter events, 0.3 us)
Async XLA Ops:
  6.5 53.1 %copy-start = (bf16[5120,128]{1,0:T(8,128)(2,1)S(1)}, bf16[5120,128]{1,0:T(8,128)(2,1)}, u32[]{:S(2)}) copy-start(bf16[5120,128]{1,0:T(8,128)(2,1)} %param.19) | copy-start | bytes 3932164
  6.5 2.1 %copy-start.8 = (bf16[640]{0:T(1024)(128)(2,1)S(1)}, bf16[640]{0:T(1024)(128)(2,1)}, u32[]{:S(2)}) copy-start(bf16[640]{0:T(1024)(128)(2,1)} %param.14) | copy-start | bytes 3844
  6.5 2.2 %copy-start.3 = (bf16[128,640]{1,0:T(8,128)(2,1)S(1)}, bf16[128,640]{1,0:T(8,128)(2,1)}, u32[]{:S(2)}) copy-start(bf16[128,640]{1,0:T(8,128)(2,1)} %param.13) | copy-start | bytes 491524
  6.5 117.2 %all-gather.2.cloned.1.call-start = ((), (), s32[]{:S(2)}) async-start(), calls=%async_computation.1 | async-start | bytes 17301504 | tf_op jit(solution)/shard_map/all_gather | solution.py:205
  8.6 12.9 %copy-start.9 = (bf16[384]{0:T(512)(128)(2,1)S(1)}, bf16[384]{0:T(512)(128)(2,1)}, u32[]{:S(2)}) copy-start(bf16[384]{0:T(512)(128)(2,1)} %param.16) | copy-start | bytes 2308
  8.6 12.9 %copy-start.13 = (bf16[128]{0:T(256)(128)(2,1)S(1)}, bf16[128]{0:T(256)(128)(2,1)}, u32[]{:S(2)}) copy-start(bf16[128]{0:T(256)(128)(2,1)} %param.18) | copy-start | bytes 772
  8.6 13.4 %copy-start.14 = (bf16[128]{0:T(256)(128)(2,1)S(1)}, bf16[128]{0:T(256)(128)(2,1)}, u32[]{:S(2)}) copy-start(bf16[128]{0:T(256)(128)(2,1)} %param.20) | copy-start | bytes 772
  8.6 14.5 %copy-start.15 = (s32[32]{0:T(128)S(1)}, s32[32]{0:T(128)}, u32[]{:S(2)}) copy-start(s32[32]{0:T(128)} %param.25) | copy-start | bytes 388
  8.8 5.9 %collective-permute-start = (bf16[144,640]{1,0:T(8,128)(2,1)S(1)}, bf16[144,640]{1,0:T(8,128)(2,1)S(1)}, u32[]{:S(2)}, u32[]{:S(2)}) collective-permute-start(bf16[144,640]{1,0:T(8,128)(2,1)S(1)} %maximum_maximum_fusion), channel_id=1, source_target_pairs={{0,1},{1,0},{2,3},{3,2},{4,5},{5,4},{6,7},{7,6},{8,9},{9,8},{10,11... | collective-permute-start | bytes 552968 | tf_op jit(solution)/shard_map/ppermute | solution.py:163
  14.9 9.9 %collective-permute-start.1 = (bf16[2,144,640]{2,1,0:T(8,128)(2,1)S(1)}, bf16[2,144,640]{2,1,0:T(8,128)(2,1)S(1)}, u32[]{:S(2)}, u32[]{:S(2)}) collective-permute-start(bf16[2,144,640]{2,1,0:T(8,128)(2,1)S(1)} %get-tuple-element.8), channel_id=1, source_target_pairs={{0,2},{1,3},{2,4},{3,5},{4,6},{5,7},{6,0},{7,1},{8,10},{9,11},{10,... | collective-permute-start | bytes 1105928 | tf_op jit(solution)/shard_map/ppermute | solution.py:170
  17.2 17.7 %collective-permute-start.2 = (bf16[2,144,640]{2,1,0:T(8,128)(2,1)S(1)}, bf16[2,144,640]{2,1,0:T(8,128)(2,1)S(1)}, u32[]{:S(2)}, u32[]{:S(2)}) collective-permute-start(bf16[2,144,640]{2,1,0:T(8,128)(2,1)S(1)} %get-tuple-element.8), channel_id=1, source_target_pairs={{0,4},{1,5},{2,6},{3,7},{4,0},{5,1},{6,2},{7,3},{8,12},{9,13},{10,... | collective-permute-start | bytes 1105928 | tf_op jit(solution)/shard_map/ppermute | solution.py:170
  19.6 15.4 %collective-permute-start.3 = (bf16[2,144,640]{2,1,0:T(8,128)(2,1)S(1)}, bf16[2,144,640]{2,1,0:T(8,128)(2,1)S(1)}, u32[]{:S(2)}, u32[]{:S(2)}) collective-permute-start(bf16[2,144,640]{2,1,0:T(8,128)(2,1)S(1)} %get-tuple-element.8), channel_id=1, source_target_pairs={{0,6},{1,7},{2,0},{3,1},{4,2},{5,3},{6,4},{7,5},{8,14},{9,15},{10,... | collective-permute-start | bytes 1105928 | tf_op jit(solution)/shard_map/ppermute | solution.py:170
  34.9 0.8 copy-start.4
  35.0 0.8 copy-start.5
  39.0 4.2 %copy-start.12 = (pred[8]{0:T(512)(128)(4,1)S(1)}, pred[8]{0:T(512)(128)(4,1)}, u32[]{:S(2)}) copy-start(pred[8]{0:T(512)(128)(4,1)} %broadcast_in_dim.64) | copy-start | bytes 28
  45.2 1.5 copy-start.1
  50.7 2.4 %copy-start.2 = (bf16[5120,384]{1,0:T(8,128)(2,1)S(1)}, bf16[5120,384]{1,0:T(8,128)(2,1)}, u32[]{:S(2)}) copy-start(bf16[5120,384]{1,0:T(8,128)(2,1)} %param.15) | copy-start | bytes 11796484
  53.1 1.4 copy-start.6
  53.1 1.4 copy-start.7
  54.0 0.8 copy-start.10
  54.8 4.8 %copy-start.11 = (f32[128]{0:T(128)S(1)}, f32[128]{0:T(128)}, u32[]{:S(2)}) copy-start(f32[128]{0:T(128)} %convert_element_type.89) | copy-start | bytes 1540
  137.2 31.4 %all-to-all-start = ((bf16[8,128,640]{2,1,0:T(8,128)(2,1)}), bf16[8,128,640]{2,1,0:T(8,128)(2,1)S(1)}, u32[]{:S(2)}, u32[]{:S(2)}) async-start(bf16[8,128,640]{2,1,0:T(8,128)(2,1)} %shard_map.127), calls=%async_computation | async-start | bytes 2621440 | tf_op jit(solution)/shard_map/all_to_all | solution.py:212
Sparse Core Ops, SparseCore 0:
  9.9 113.8 all-gather.1

commit v15 on v13

--- a/solution.py
+++ b/solution.py
@@ -54,56 +54,42 @@
 
 def prefix_kernel(own_ref, q_ref, *refs):
     kv_refs = refs[:2 * PER_STEP]
-    m0_ref, l0_ref, a0_ref, w_hbm, o_ref, m_sc, l_sc, acc_sc, q_sc, w_sc, sem = refs[2 * PER_STEP:]
-    step = pl.program_id(0)
+    m0_ref, l0_ref, a0_ref, w_hbm, o_ref, w_sc, sem = refs[2 * PER_STEP:]
     group = q_ref.shape[1] // HD
     fetch = pltpu.make_async_copy(w_hbm, w_sc, sem.at[0])
-
-    @pl.when(step == 0)
-    def _():
-        fetch.start()
-        m_sc[...] = m0_ref[...]
-        l_sc[...] = l0_ref[...]
-        acc_sc[...] = a0_ref[...]
-        q = q_ref[...]
-        q_sc[...] = jnp.concatenate([q[:, h * HD:(h + 1) * HD] for h in range(group)], axis=0)
-
-    stacked = q_sc[...]
+    fetch.start()
+    q = q_ref[...]
+    stacked = jnp.concatenate([q[:, h * HD:(h + 1) * HD] for h in range(group)], axis=0)
     dims = (((1,), (1,)), ((), ()))
-    refs = kv_refs
     parts = [
-        lax.dot_general(stacked, refs[2 * i][0], dims, preferred_element_type=jnp.float32)
+        lax.dot_general(stacked, kv_refs[2 * i][0], dims, preferred_element_type=jnp.float32)
         * HD ** (-0.5)
-        for i in range(len(refs) // 2)
+        for i in range(PER_STEP)
     ]
-    old = m_sc[...]
+    old = m0_ref[...]
     top = old
     for part in parts:
         top = jnp.maximum(top, jnp.max(part, axis=-1, keepdims=True))
     alpha = jnp.exp(old - top)
     weights = [jnp.exp(part - top) for part in parts]
     summed = weights[0].sum(axis=-1, keepdims=True)
-    mixed = jnp.dot(weights[0].astype(jnp.bfloat16), refs[1][0], preferred_element_type=jnp.float32)
-    for i in range(1, len(weights)):
+    mixed = jnp.dot(weights[0].astype(jnp.bfloat16), kv_refs[1][0], preferred_element_type=jnp.float32)
+    for i in range(1, PER_STEP):
         summed = summed + weights[i].sum(axis=-1, keepdims=True)
         mixed = mixed + jnp.dot(
-            weights[i].astype(jnp.bfloat16), refs[2 * i + 1][0], preferred_element_type=jnp.float32
+            weights[i].astype(jnp.bfloat16), kv_refs[2 * i + 1][0], preferred_element_type=jnp.float32
         )
-    l_sc[...] = alpha * l_sc[...] + summed
-    acc_sc[...] = alpha * acc_sc[...] + mixed
-    m_sc[...] = top
-
-    @pl.when(step == pl.num_programs(0) - 1)
-    def _():
-        context = (acc_sc[...] / l_sc[...]).astype(jnp.bfloat16)
-        rows = q_ref.shape[0]
-        flat = jnp.concatenate([context[h * rows:(h + 1) * rows] for h in range(group)], axis=1)
-        fetch.wait()
-        partial = jnp.dot(flat, w_sc[...], preferred_element_type=jnp.float32).astype(o_ref.dtype)
-        pieces = o_ref.shape[0]
-        span = o_ref.shape[2]
-        for t in range(pieces):
-            o_ref[t] = partial[:, t * span:(t + 1) * span]
+    total = alpha * l0_ref[...] + summed
+    acc = alpha * a0_ref[...] + mixed
+    context = (acc / total).astype(jnp.bfloat16)
+    rows = q_ref.shape[0]
+    flat = jnp.concatenate([context[h * rows:(h + 1) * rows] for h in range(group)], axis=1)
+    fetch.wait()
+    partial = jnp.dot(flat, w_sc[...], preferred_element_type=jnp.float32).astype(o_ref.dtype)
+    pieces = o_ref.shape[0]
+    span = o_ref.shape[2]
+    for t in range(pieces):
+        o_ref[t] = partial[:, t * span:(t + 1) * span]
 
 
 def prefix_attention(owners, flat_q, kv, peak0, total0, mixed0, o_weight, pieces):
@@ -138,10 +124,6 @@
             ],
             out_specs=pl.BlockSpec((pieces, length, out_width // pieces), lambda j, own: (0, 0, 0)),
             scratch_shapes=[
-                pltpu.VMEM((rows, 1), jnp.float32),
-                pltpu.VMEM((rows, 1), jnp.float32),
-                pltpu.VMEM((rows, HD), jnp.float32),
-                pltpu.VMEM((rows, HD), jnp.bfloat16),
                 pltpu.VMEM((width, out_width), jnp.bfloat16),
                 pltpu.SemaphoreType.DMA((1,)),
             ],

time: 174 us -> 175 us (level)
  no operation moved by 1% of the time
where the time goes in v15:
time: 175 us; the launch traced here: 174 us
  waiting for transfers between devices  93.2 us (53%)
  starting transfers between devices  23.3 us (13%)
  between operations  15 us (9%)
  local copies, waits for them, and re-layouts  14.7 us (8%)
  other arithmetic  13.2 us (8%)
  Pallas kernels  10.5 us (6%)
  matrix products  4.37 us (2%)
    all_gather x1, waiting for transfers between devices, shards(): gathered = lax.all_gather(rowwise, 'req', axis=0, tiled=True)  62.2 us
    all_to_all x1, waiting for transfers between devices, shards(): lax.all_to_all(pieces_out, 'tp', 0, 0, tiled=True).astype(jnp.float32)  17.5 us
    all_to_all x1, starting transfers between devices, shards(): lax.all_to_all(pieces_out, 'tp', 0, 0, tiled=True).astype(jnp.float32)  14.9 us
    pallas_call x1, Pallas kernels, prefix_attention(): pl.pallas_call(prefix_kernel, out_shape=jax.ShapeDtypeStruct((pieces, len...  10.5 us
    ppermute x3, waiting for transfers between devices, shards(): lax.ppermute(pair, 'tp', [(i, (i + 2 * u) % n_tp) for i in range(n_tp)])  10.3 us
    unnamed x39, local copies, waits for them, and re-layouts  6.27 us
    gather x2, local copies, waits for them, and re-layouts, shards(): jnp.take(along, (me_x - jnp.arange(n_x, dtype=jnp.int32)) % n_x, axis=0)  6.05 us
    ppermute x3, starting transfers between devices, shards(): lax.ppermute(pair, 'tp', [(i, (i + 2 * u) % n_tp) for i in range(n_tp)])  5.83 us
  transfers between devices with their start and end apart: 6, of which 5 were waited for; matrix products, arithmetic and copies ran while one was open for 16% of the time, Pallas kernels for 0%

profile of v15, /device:TPU:1, one launch (start us, length us, event | category | flops | bytes accessed | tf_op | source)
XLA Modules:
  0.0 174.4 jit_solution(16656659466878564265)
XLA Ops:
  6.5 2.0 %copy.52 = bf16[128,8,2,128]{3,1,2,0:T(8,128)(2,1)} copy(bf16[128,8,2,128]{3,2,1,0:T(2,128)(2,1)} %bitcast.108) | data formatting | bytes 1048576
  8.7 0.1 pad.12.clone
  8.7 0.1 maximum_maximum_fusion
  8.8 2.6 %collective-permute-start = (bf16[144,640]{1,0:T(8,128)(2,1)S(1)}, bf16[144,640]{1,0:T(8,128)(2,1)S(1)}, u32[]{:S(2)}, u32[]{:S(2)}) collective-permute-start(bf16[144,640]{1,0:T(8,128)(2,1)S(1)} %maximum_maximum_fusion), channel_id=1, source_target_pairs={{0,1},{1,0},{2,3},{3,2},{4,5},{5,4},{6,7},{7,6},{8,9},{9,8},{10,11... | collective-permute-start | bytes 552968 | tf_op jit(solution)/shard_map/ppermute | solution.py:166
  11.4 3.3 %collective-permute-done = bf16[144,640]{1,0:T(8,128)(2,1)S(1)} collective-permute-done((bf16[144,640]{1,0:T(8,128)(2,1)S(1)}, bf16[144,640]{1,0:T(8,128)(2,1)S(1)}, u32[]{:S(2)}, u32[]{:S(2)}) %collective-permute-start) | collective-permute-done | bytes 184352 | tf_op jit(solution)/shard_map/ppermute | solution.py:166
  14.7 0.2 select_bitcast_fusion.1
  14.9 0.1 fusion.30
  14.9 2.2 %collective-permute-start.1 = (bf16[2,144,640]{2,1,0:T(8,128)(2,1)S(1)}, bf16[2,144,640]{2,1,0:T(8,128)(2,1)S(1)}, u32[]{:S(2)}, u32[]{:S(2)}) collective-permute-start(bf16[2,144,640]{2,1,0:T(8,128)(2,1)S(1)} %get-tuple-element.8), channel_id=1, source_target_pairs={{0,2},{1,3},{2,4},{3,5},{4,6},{5,7},{6,0},{7,1},{8,10},{9,11},{10,... | collective-permute-start | bytes 1105928 | tf_op jit(solution)/shard_map/ppermute | solution.py:173
  17.2 2.5 %collective-permute-start.2 = (bf16[2,144,640]{2,1,0:T(8,128)(2,1)S(1)}, bf16[2,144,640]{2,1,0:T(8,128)(2,1)S(1)}, u32[]{:S(2)}, u32[]{:S(2)}) collective-permute-start(bf16[2,144,640]{2,1,0:T(8,128)(2,1)S(1)} %get-tuple-element.8), channel_id=1, source_target_pairs={{0,4},{1,5},{2,6},{3,7},{4,0},{5,1},{6,2},{7,3},{8,12},{9,13},{10,... | collective-permute-start | bytes 1105928 | tf_op jit(solution)/shard_map/ppermute | solution.py:173
  19.6 1.2 collective-permute-start.3
  20.8 0.1 broadcast_in_dim.63
  20.8 0.6 broadcast_in_dim.64
  21.4 0.5 convert_element_type.88
  22.0 0.5 convert_element_type.89
  23.1 0.6 dynamic_slice.3.own_ref
  23.8 1.0 multiply_cosine_fusion
  24.8 10.1 %collective-permute-done.2 = bf16[2,144,640]{2,1,0:T(8,128)(2,1)S(1)} collective-permute-done((bf16[2,144,640]{2,1,0:T(8,128)(2,1)S(1)}, bf16[2,144,640]{2,1,0:T(8,128)(2,1)S(1)}, u32[]{:S(2)}, u32[]{:S(2)}) %collective-permute-start.2) | collective-permute-done | bytes 368672 | tf_op jit(solution)/shard_map/ppermute | solution.py:173
  34.9 0.1 collective-permute-done.3
  35.0 0.6 copy-done.4
  35.6 0.2 copy-done.5
  35.8 1.3 pad_maximum_fusion
  37.1 1.9 %gather_fusion = bf16[4,2,144,640]{3,2,1,0:T(8,128)(2,1)} fusion(bf16[4,2,144,640]{3,2,1,0:T(8,128)(2,1)S(1)} %pad_maximum_fusion, s32[1024]{0:T(1024)S(1)} %pad_clamp_fusion), kind=kCustom, calls=%fused_computation | custom fusion | bytes 2949136 | tf_op jit(solution)/shard_map/jit(_take)/gather | solution.py:178
  39.0 4.2 %copy.29 = bf16[4,2,144,640]{2,3,1,0:T(8,128)(2,1)} copy(bf16[4,2,144,640]{3,2,1,0:T(8,128)(2,1)} %gather_fusion) | data formatting | bytes 2949120 | tf_op jit(solution)/shard_map/jit(_take)/gather | solution.py:178
  43.2 2.1 %bitcast_select_fusion = bf16[8,144,640]{1,2,0:T(8,128)(2,1)S(1)} fusion(bf16[4,2,144,640]{2,3,1,0:T(8,128)(2,1)} %copy.29, pred[8]{0:T(512)(128)(4,1)S(1)} %copy-done.12), kind=kLoop, calls=%fused_computation.4 | loop fusion | flops 737280 | bytes 2949128 | tf_op jit(solution)/shard_map/jit(_take)/select_n | solution.py:178
  45.3 1.5 copy-done.1
  46.7 0.4 convert_reduce_fusion
  47.2 2.0 %multiply_reduce_fusion = f32[128]{0:T(128)S(1)} fusion(bf16[144,8,640]{0,2,1:T(8,128)(2,1)} %bitcast.101), kind=kLoop, calls=%fused_computation.7 | loop fusion | flops 1965952 | bytes 1311232 | tf_op jit(solution)/shard_map/reduce_sum | solution.py:183
  49.2 1.5 slice_convert_fusion
  50.7 2.2 %fusion.1 = bf16[128,5120]{0,1:T(8,128)(2,1)S(1)} fusion(f32[128,8,640]{0,2,1:T(8,128)S(1)} %slice_convert_fusion, f32[5120]{0:T(1024)S(1)} %reshape.283, f32[128]{0:T(128)S(1)} %add_rsqrt_fusion), kind=kLoop, calls=%fused_computation.3 | loop fusion | flops 1966080 | bytes 3953152 | tf_op jit(solution)/shard_map/convert_element_type | solution.py:184
  52.9 0.9 convolution_add_fusion
  53.9 0.1 copy.30
  54.0 0.1 copy.42
  54.2 0.1 copy.43
  54.4 0.1 maximum_convert_fusion
  54.5 0.1 copy.33
  54.6 1.9 %fusion.4 = f32[128,1,128]{0,2,1:T(8,128)S(1)} fusion(bf16[128,5120]{0,1:T(8,128)(2,1)S(1)} %fusion.1, bf16[5120,128]{1,0:T(8,128)(2,1)} %param.17, f32[128]{0:T(128)S(1)} %copy-done.10), kind=kOutput, calls=%fused_computation.16 | convolution fusion | flops 167788544 | bytes 2687488 | tf_op jit(solution)/shard_map/dot_general | solution.py:191
  56.5 0.2 fusion.25
  56.7 0.2 fusion.32
  57.0 0.8 copy.48
  57.8 0.8 copy.46
  58.7 0.8 copy.36.q_ref
  59.4 1.4 fusion.7
  60.8 62.2 %all-gather.2.cloned.1.call-done = bf16[32768,256]{1,0:T(8,128)(2,1)} async-done(((bf16[1024,256]{1,0:T(8,128)(2,1)}), bf16[32768,256]{1,0:T(8,128)(2,1)}) %all-gather.2.cloned.1.call-update) | async-done | bytes 16777232 | tf_op jit(solution)/shard_map/all_gather | solution.py:208
  123.0 10.5 %shard_map.127 = bf16[8,128,640]{2,1,0:T(8,128)(2,1)} custom-call(s32[8]{0:T(128)} %dynamic_slice.3.own_ref, bf16[128,384]{1,0:T(8,128)(2,1)} %copy.36.q_ref, bf16[32,1024,256]{2,1,0:T(8,128)(2,1)} %bitcast.84, bf16[32,1024,256]{2,1,0:T(8,128)(2,1)} %bitcast.85, bf16[32,1024,256]{2,1,0:T(8,128)(2,1)} %bitcast.86, bf16[32,1024,256]{2,1,0:T(8,128)(2,1)} %bitcast.87, ...), custom_call_target="tpu_custom_call" | custom-call | flops 1610612736 | bytes 9830400 | tf_op jit(solution)/shard_map/pallas_call | solution.py:107
  133.5 14.9 %all-to-all-start = ((bf16[8,128,640]{2,1,0:T(8,128)(2,1)}), bf16[8,128,640]{2,1,0:T(8,128)(2,1)S(1)}, u32[]{:S(2)}, u32[]{:S(2)}) async-start(bf16[8,128,640]{2,1,0:T(8,128)(2,1)} %shard_map.127), calls=%async_computation | async-start | bytes 2621440 | tf_op jit(solution)/shard_map/all_to_all | solution.py:215
  149.1 17.5 %all-to-all-done = bf16[8,128,640]{2,1,0:T(8,128)(2,1)S(1)} async-done(((bf16[8,128,640]{2,1,0:T(8,128)(2,1)}), bf16[8,128,640]{2,1,0:T(8,128)(2,1)S(1)}, u32[]{:S(2)}, u32[]{:S(2)}) %all-to-all-start) | async-done | bytes 1310752 | tf_op jit(solution)/shard_map/all_to_all | solution.py:215
  166.6 0.2 convert_reduce_fusion.1
  166.7 0.8 select_convert_fusion
  (49 shorter events, 0.3 us)
Async XLA Ops:
  6.5 52.9 %copy-start = (bf16[5120,128]{1,0:T(8,128)(2,1)S(1)}, bf16[5120,128]{1,0:T(8,128)(2,1)}, u32[]{:S(2)}) copy-start(bf16[5120,128]{1,0:T(8,128)(2,1)} %param.19) | copy-start | bytes 3932164
  6.5 2.1 %copy-start.8 = (bf16[640]{0:T(1024)(128)(2,1)S(1)}, bf16[640]{0:T(1024)(128)(2,1)}, u32[]{:S(2)}) copy-start(bf16[640]{0:T(1024)(128)(2,1)} %param.14) | copy-start | bytes 3844
  6.5 2.2 %copy-start.3 = (bf16[128,640]{1,0:T(8,128)(2,1)S(1)}, bf16[128,640]{1,0:T(8,128)(2,1)}, u32[]{:S(2)}) copy-start(bf16[128,640]{1,0:T(8,128)(2,1)} %param.13) | copy-start | bytes 491524
  6.5 116.4 %all-gather.2.cloned.1.call-start = ((), (), s32[]{:S(2)}) async-start(), calls=%async_computation.1 | async-start | bytes 17301504 | tf_op jit(solution)/shard_map/all_gather | solution.py:208
  8.6 12.9 %copy-start.9 = (bf16[384]{0:T(512)(128)(2,1)S(1)}, bf16[384]{0:T(512)(128)(2,1)}, u32[]{:S(2)}) copy-start(bf16[384]{0:T(512)(128)(2,1)} %param.16) | copy-start | bytes 2308
  8.6 12.9 %copy-start.13 = (bf16[128]{0:T(256)(128)(2,1)S(1)}, bf16[128]{0:T(256)(128)(2,1)}, u32[]{:S(2)}) copy-start(bf16[128]{0:T(256)(128)(2,1)} %param.18) | copy-start | bytes 772
  8.6 13.4 %copy-start.14 = (bf16[128]{0:T(256)(128)(2,1)S(1)}, bf16[128]{0:T(256)(128)(2,1)}, u32[]{:S(2)}) copy-start(bf16[128]{0:T(256)(128)(2,1)} %param.20) | copy-start | bytes 772
  8.6 14.5 %copy-start.15 = (s32[32]{0:T(128)S(1)}, s32[32]{0:T(128)}, u32[]{:S(2)}) copy-start(s32[32]{0:T(128)} %param.25) | copy-start | bytes 388
  8.8 5.9 %collective-permute-start = (bf16[144,640]{1,0:T(8,128)(2,1)S(1)}, bf16[144,640]{1,0:T(8,128)(2,1)S(1)}, u32[]{:S(2)}, u32[]{:S(2)}) collective-permute-start(bf16[144,640]{1,0:T(8,128)(2,1)S(1)} %maximum_maximum_fusion), channel_id=1, source_target_pairs={{0,1},{1,0},{2,3},{3,2},{4,5},{5,4},{6,7},{7,6},{8,9},{9,8},{10,11... | collective-permute-start | bytes 552968 | tf_op jit(solution)/shard_map/ppermute | solution.py:166
  14.9 9.9 %collective-permute-start.1 = (bf16[2,144,640]{2,1,0:T(8,128)(2,1)S(1)}, bf16[2,144,640]{2,1,0:T(8,128)(2,1)S(1)}, u32[]{:S(2)}, u32[]{:S(2)}) collective-permute-start(bf16[2,144,640]{2,1,0:T(8,128)(2,1)S(1)} %get-tuple-element.8), channel_id=1, source_target_pairs={{0,2},{1,3},{2,4},{3,5},{4,6},{5,7},{6,0},{7,1},{8,10},{9,11},{10,... | collective-permute-start | bytes 1105928 | tf_op jit(solution)/shard_map/ppermute | solution.py:173
  17.2 17.7 %collective-permute-start.2 = (bf16[2,144,640]{2,1,0:T(8,128)(2,1)S(1)}, bf16[2,144,640]{2,1,0:T(8,128)(2,1)S(1)}, u32[]{:S(2)}, u32[]{:S(2)}) collective-permute-start(bf16[2,144,640]{2,1,0:T(8,128)(2,1)S(1)} %get-tuple-element.8), channel_id=1, source_target_pairs={{0,4},{1,5},{2,6},{3,7},{4,0},{5,1},{6,2},{7,3},{8,12},{9,13},{10,... | collective-permute-start | bytes 1105928 | tf_op jit(solution)/shard_map/ppermute | solution.py:173
  19.6 15.4 %collective-permute-start.3 = (bf16[2,144,640]{2,1,0:T(8,128)(2,1)S(1)}, bf16[2,144,640]{2,1,0:T(8,128)(2,1)S(1)}, u32[]{:S(2)}, u32[]{:S(2)}) collective-permute-start(bf16[2,144,640]{2,1,0:T(8,128)(2,1)S(1)} %get-tuple-element.8), channel_id=1, source_target_pairs={{0,6},{1,7},{2,0},{3,1},{4,2},{5,3},{6,4},{7,5},{8,14},{9,15},{10,... | collective-permute-start | bytes 1105928 | tf_op jit(solution)/shard_map/ppermute | solution.py:173
  34.9 0.8 copy-start.4
  35.0 0.8 copy-start.5
  39.0 4.2 %copy-start.12 = (pred[8]{0:T(512)(128)(4,1)S(1)}, pred[8]{0:T(512)(128)(4,1)}, u32[]{:S(2)}) copy-start(pred[8]{0:T(512)(128)(4,1)} %broadcast_in_dim.64) | copy-start | bytes 28
  45.2 1.5 copy-start.1
  50.7 2.2 %copy-start.2 = (bf16[5120,384]{1,0:T(8,128)(2,1)S(1)}, bf16[5120,384]{1,0:T(8,128)(2,1)}, u32[]{:S(2)}) copy-start(bf16[5120,384]{1,0:T(8,128)(2,1)} %param.15) | copy-start | bytes 11796484
  52.9 1.4 copy-start.6
  52.9 1.4 copy-start.7
  53.9 0.8 copy-start.10
  54.6 4.8 %copy-start.11 = (f32[128]{0:T(128)S(1)}, f32[128]{0:T(128)}, u32[]{:S(2)}) copy-start(f32[128]{0:T(128)} %convert_element_type.89) | copy-start | bytes 1540
  133.5 33.1 %all-to-all-start = ((bf16[8,128,640]{2,1,0:T(8,128)(2,1)}), bf16[8,128,640]{2,1,0:T(8,128)(2,1)S(1)}, u32[]{:S(2)}, u32[]{:S(2)}) async-start(bf16[8,128,640]{2,1,0:T(8,128)(2,1)} %shard_map.127), calls=%async_computation | async-start | bytes 2621440 | tf_op jit(solution)/shard_map/all_to_all | solution.py:215
Sparse Core Ops, SparseCore 0:
  9.9 113.0 all-gather.1
